TPU v7x, 128 devices: a whole 4x4x4 slice. The times are simulated.
128 devices in a mesh: lat: 4 (over z_hi, core), lon: 32 (over z_lo, y, x).
Axes of the slice: x: 4, y: 4, z: 4 (z_hi: 2, z_lo: 2; z = z_hi * 2 + z_lo), core: 2. Of those that a mesh axis runs over, the one named last changes fastest.
Arguments:
- atm_fluxes: bfloat16 [24, 262144], P(None, ('lat', 'lon')), may hold values from -6 to 6
- remap_weights: bfloat16 [128, 256, 128, 128], P(('lat', 'lon')), may hold values from 0 to 0.015625
- source_block: int32 [128, 256], P(('lat', 'lon')), may hold values from 0 to 15
- target_block: int32 [128, 256], P(('lat', 'lon')), may hold values from 0 to 15
- block_count: int32 [128, 128], P(('lat', 'lon')), may hold values from 1 to 2, as said below
- tracers: float32 [6, 16, 64, 4096], P(None, None, 'lat', 'lon'), may hold values from -6 to 6
- east_velocity: float32 [16, 64, 4096], P(None, 'lat', 'lon'), may hold values from -0.3 to 0.3
- north_velocity: float32 [16, 64, 4096], P(None, 'lat', 'lon'), may hold values from -0.3 to 0.3
- land_mask: int32 [64, 4096], P('lat', 'lon'), may hold values 0 or 1
- coupling: float32 [96, 24], replicated, may hold values from -3 to 3
Outputs:
- tracer_out: float32 [6, 16, 64, 4096], P(None, None, 'lat', 'lon')
Inputs may be any that keep to these rules, and one draw needn't show every extreme that they name: Slots 0 to block_count - 1 of a source and tile carry data; in every draw one tile receives all 2 slots from every source.
All inputs are finite; a program needn't handle non-finite values. No bound on the sum of `land_mask` on one device may be relied on, other than what follows from the above.
Results may differ from a plain program's by a relative error of at most 0.0003.
Values sent between devices are 32-bit elements; how exact they have to be, the bound alone decides.
No kernel may reach another device: no remote copies, remote signals or barrier semaphores. Data moves between devices by JAX's collectives and lax.ppermute only.
A program may use at most 128 MiB of HBM per device.

v0:
```python
import jax
import jax.numpy as jnp
from jax import lax
from jax.sharding import PartitionSpec as P

NSUB = 4


diffusion_number = 0.2


def shifted_pairs(count, step, wrap):
    pairs = []
    for i in range(count):
        j = i + step
        if 0 <= j < count:
            pairs.append((i, j))
        elif wrap:
            pairs.append((i, j % count))
    return pairs


def with_halo(block, width):
    lon_count = lax.axis_size("lon")
    lat_count = lax.axis_size("lat")
    west = lax.ppermute(block[..., -width:], "lon", shifted_pairs(lon_count, 1, True))
    east = lax.ppermute(block[..., :width], "lon", shifted_pairs(lon_count, -1, True))
    block = jnp.concatenate([west, block, east], axis=-1)
    south = lax.ppermute(block[..., -width:, :], "lat", shifted_pairs(lat_count, 1, False))
    north = lax.ppermute(block[..., :width, :], "lat", shifted_pairs(lat_count, -1, False))
    return jnp.concatenate([south, block, north], axis=-2)


def advect(tracer_now, east_speed, north_speed, sea_mask):
    mask_east = sea_mask[:, :-1] * sea_mask[:, 1:]
    east_flow = mask_east * (
        east_speed[:, :, :-1] * (tracer_now[..., :-1] + tracer_now[..., 1:]) * 0.5
        - diffusion_number * (tracer_now[..., 1:] - tracer_now[..., :-1])
    )
    mask_north = sea_mask[:-1, :] * sea_mask[1:, :]
    north_flow = mask_north * (
        north_speed[:, :-1, :] * (tracer_now[..., :-1, :] + tracer_now[..., 1:, :]) * 0.5
        - diffusion_number * (tracer_now[..., 1:, :] - tracer_now[..., :-1, :])
    )
    inner = tracer_now[..., 1:-1, 1:-1]
    return (
        inner
        + east_flow[..., 1:-1, :-1]
        - east_flow[..., 1:-1, 1:]
        + north_flow[..., :-1, 1:-1]
        - north_flow[..., 1:, 1:-1]
    )


def per_device(
    atm_fluxes,
    remap_weights,
    source_block,
    target_block,
    block_count,
    tracers,
    east_velocity,
    north_velocity,
    land_mask,
    coupling,
):
    field_count, cell_count = atm_fluxes.shape
    block_cells = remap_weights.shape[-1]
    tile_count = block_count.shape[1]
    slot_count = source_block.shape[1] // tile_count
    tracer_count, level_count, lat_rows, lon_cols = tracers.shape

    atm_blocks = atm_fluxes.reshape(field_count, cell_count // block_cells, block_cells)
    chosen = jnp.take(atm_blocks, source_block[0], axis=1)
    partials = jnp.einsum(
        "fsb,sbc->sfc", chosen, remap_weights[0], preferred_element_type=jnp.float32
    )
    slot_ids = jnp.arange(tile_count * slot_count, dtype=jnp.int32)
    is_live = slot_ids % slot_count < jnp.repeat(block_count[0], slot_count)
    partials = jnp.where(is_live[:, None, None], partials, jnp.float32(0.0))
    targets = jnp.where(is_live, target_block[0], -1).astype(jnp.float32)
    arrived = lax.all_to_all(
        partials.reshape(tile_count, slot_count * field_count, block_cells),
        ("lat", "lon"),
        split_axis=0,
        concat_axis=0,
        tiled=True,
    )
    landed = lax.all_to_all(
        targets.reshape(tile_count, slot_count),
        ("lat", "lon"),
        split_axis=0,
        concat_axis=0,
        tiled=True,
    )

    sea_here = land_mask.astype(jnp.float32)
    planes = tracer_count * level_count
    stacked = jnp.concatenate(
        [
            tracers.reshape(planes, lat_rows, lon_cols),
            east_velocity,
            north_velocity,
            sea_here[None],
        ],
        axis=0,
    )
    wide = with_halo(stacked, NSUB)
    tracer_now = wide[:planes].reshape(tracer_count, level_count, lat_rows + 2 * NSUB, lon_cols + 2 * NSUB)
    east_wide = wide[planes : planes + level_count]
    north_wide = wide[planes + level_count : planes + 2 * level_count]
    mask_wide = wide[-1]
    for substep in range(NSUB):
        cut = substep
        end_r = lat_rows + 2 * NSUB - cut
        end_c = lon_cols + 2 * NSUB - cut
        tracer_now = advect(
            tracer_now,
            east_wide[:, cut:end_r, cut:end_c],
            north_wide[:, cut:end_r, cut:end_c],
            mask_wide[cut:end_r, cut:end_c],
        )

    arrived = arrived.reshape(tile_count * slot_count, field_count, block_cells)
    landed = landed.reshape(tile_count * slot_count)
    chooser = (landed[None, :] == jnp.arange(lat_rows, dtype=jnp.float32)[:, None]).astype(
        jnp.float32
    )
    ocean_flux = jnp.einsum(
        "rk,kfc->rfc", chooser, arrived, precision=lax.Precision.HIGHEST,
        preferred_element_type=jnp.float32,
    )
    source = jnp.einsum(
        "pf,ifj->pij", coupling, ocean_flux, precision=lax.Precision.HIGHEST
    ).reshape(tracer_count, level_count, lat_rows, lon_cols)
    return tracer_now + sea_here * source


def solution(mesh):
    placed = (
        P(None, ("lat", "lon")),
        P(("lat", "lon"), None, None, None),
        P(("lat", "lon"), None),
        P(("lat", "lon"), None),
        P(("lat", "lon"), None),
        P(None, None, "lat", "lon"),
        P(None, "lat", "lon"),
        P(None, "lat", "lon"),
        P("lat", "lon"),
        P(),
    )
    return jax.shard_map(
        per_device,
        mesh=mesh,
        in_specs=placed,
        out_specs=P(None, None, "lat", "lon"),
        check_vma=False,
    )
```

profile of v0, /device:TPU:0, one launch (start us, length us, event | category | flops | bytes accessed | tf_op | source)
XLA Modules:
  0.0 108.7 jit_solution(13778881531472629417)
XLA Ops:
  0.5 1.3 %reduce.6 = s32[256]{0:T(256)S(1)} reduce(s32[1,256]{1,0:T(1,128)} %param.13, s32[]{:T(128)} %broadcast.164), dimensions={0}, to_apply=%param.13.reduce_sub_computation.3 | reduce | bytes 2052 | tf_op args[3]
  2.8 0.7 copy.80
  3.5 11.7 %all-to-all-start = ((f32[128,1,2]{2,1,0:T(1,128)}), f32[128,1,2]{2,1,0:T(1,128)}, u32[]{:S(2)}, u32[]{:S(2)}) async-start(f32[128,1,2]{2,1,0:T(1,128)} %copy.80), calls=%async_computation | async-start | bytes 131072 | tf_op jit(solution)/shard_map/all_to_all | solution.py:89
  15.2 1.3 %fusion.25 = (f32[16,128]{1,0:T(8,128)}, f32[1,16,128]{2,1,0:T(8,128)S(1)}) fusion(s32[16,128]{1,0:T(8,128)} %param.18), kind=kLoop, calls=%fused_computation.82 | loop fusion | flops 2048 | bytes 24576 | tf_op jit(solution)/shard_map/convert_element_type | solution.py:97
  16.5 1.3 %pad_maximum_fusion.1 = f32[129,16,128]{2,1,0:T(8,128)S(1)} fusion(f32[1,16,128]{2,1,0:T(8,128)S(1)} %get-tuple-element.10, f32[16,16,128]{2,1,0:T(8,128)} %param.17, f32[16,16,128]{2,1,0:T(8,128)} %param.16, f32[96,16,128]{2,1,0:T(8,128)} %bitcast.42), kind=kLoop, calls=%fused_computation.30 | loop fusion | flops 792576 | bytes 2113536 | tf_op jit(solution)/shard_map/concatenate | solution.py:99
  18.9 5.5 %collective-permute-start.1 = (f32[129,16,4]{0,1,2:T(8,128)S(1)}, f32[129,16,4]{0,1,2:T(8,128)S(1)}, u32[]{:S(2)}, u32[]{:S(2)}) collective-permute-start(f32[129,16,4]{0,1,2:T(8,128)S(1)} %copy.71), channel_id=1, source_target_pairs={{0,31},{1,0},{2,1},{3,2},{4,3},{5,4},{6,5},{7,6},{8,7},{9,8},{10,9... | collective-permute-start | bytes 99080 | tf_op jit(solution)/shard_map/ppermute | solution.py:27
  26.1 2.0 %gather_fusion = bf16[256,24,128]{2,1,0:T(8,128)(2,1)} fusion(bf16[24,16,128]{2,0,1:T(8,128)(2,1)S(1)} %copy_bitcast_fusion, s32[1024]{0:T(1024)S(1)} %pad_clamp_fusion), kind=kCustom, calls=%fused_computation | custom fusion | bytes 3146752 | tf_op jit(solution)/shard_map/jit(_take)/gather | solution.py:74
  28.1 5.5 %collective-permute-done = f32[129,16,4]{0,1,2:T(8,128)S(1)} collective-permute-done((f32[129,16,4]{0,1,2:T(8,128)S(1)}, f32[129,16,4]{0,1,2:T(8,128)S(1)}, u32[]{:S(2)}, u32[]{:S(2)}) %collective-permute-start) | collective-permute-done | bytes 33056 | tf_op jit(solution)/shard_map/ppermute | solution.py:26
  33.7 0.8 copy.72
  34.5 0.8 copy.73
  35.3 2.6 %pad_maximum_fusion.7 = (f32[129,4,136]{2,1,0:T(4,128)}, f32[129,4,136]{2,1,0:T(4,128)S(1)}) fusion(f32[129,16,4]{2,1,0:T(8,128)S(1)} %copy.73, f32[129,16,4]{2,1,0:T(8,128)S(1)} %copy.72, f32[1,16,128]{2,1,0:T(8,128)S(1)} %get-tuple-element.10, f32[16,16,128]{2,1,0:T(8,128)} %param.17, f32[16,16,128]{2,1,0:T(8,128)} %param.16, f32[96,16,128]{2,1,0:T(8,128)S(1)} %bitcast.43), kind=kLoop, calls=%fused_computation.43 | loop fusion | flops 701760 | bytes 1684224 | tf_op jit(solution)/shard_map/slice | solution.py:29
  37.9 2.2 %copy.74 = f32[129,4,136]{0,2,1:T(8,128)} copy(f32[129,4,136]{2,1,0:T(4,128)} %get-tuple-element.5) | data formatting | bytes 561408 | tf_op jit(solution)/shard_map/slice | solution.py:29
  40.1 1.1 %copy.75 = f32[129,4,136]{0,2,1:T(8,128)} copy(f32[129,4,136]{2,1,0:T(4,128)S(1)} %get-tuple-element.6) | data formatting | bytes 561408 | tf_op jit(solution)/shard_map/slice | solution.py:30
  41.2 1.3 %collective-permute-start.3 = (f32[129,4,136]{0,2,1:T(8,128)}, f32[129,4,136]{0,2,1:T(8,128)S(1)}, u32[]{:S(2)}, u32[]{:S(2)}) collective-permute-start(f32[129,4,136]{0,2,1:T(8,128)} %copy.75), channel_id=1, source_target_pairs={{32,0},{64,32},{96,64},{33,1},{65,33},{97,65},{34,2},{66,34},{98,6... | collective-permute-start | bytes 842120 | tf_op jit(solution)/shard_map/ppermute | solution.py:30
  42.5 3.8 %collective-permute-start.2 = (f32[129,4,136]{0,2,1:T(8,128)}, f32[129,4,136]{0,2,1:T(8,128)}, u32[]{:S(2)}, u32[]{:S(2)}) collective-permute-start(f32[129,4,136]{0,2,1:T(8,128)} %copy.74), channel_id=1, source_target_pairs={{0,32},{32,64},{64,96},{1,33},{33,65},{65,97},{2,34},{34,66},{66,9... | collective-permute-start | bytes 842120 | tf_op jit(solution)/shard_map/ppermute | solution.py:29
  46.3 7.9 %broadcast_select_fusion = f32[256,24,128]{2,1,0:T(8,128)} fusion(bf16[1,256,128,128]{3,2,1,0:T(8,128)(2,1)} %param.11, bf16[256,24,128]{2,1,0:T(8,128)(2,1)} %gather_fusion, pred[256]{0:T(512)(128)(4,1)} %get-tuple-element.11, pred[256]{0:T(512)(128)(4,1)} %get-tuple-element.12), kind=kOutput, calls=%fused_computation.28 | convolution fusion | flops 202899456 | bytes 13107712 | tf_op jit(solution)/shard_map/fsb,sbc->sfc/dot_general | solution.py:75
  54.3 5.9 %all-to-all-start.1 = ((f32[128,48,128]{2,1,0:T(8,128)}), f32[128,48,128]{2,1,0:T(8,128)}, u32[]{:S(2)}, u32[]{:S(2)}) async-start(f32[128,48,128]{2,1,0:T(8,128)} %bitcast.46), calls=%async_computation.1 | async-start | bytes 6291456 | tf_op jit(solution)/shard_map/all_to_all | solution.py:82
  60.8 2.2 %reduce.7 = f32[128,2]{1,0:T(8,128)} reduce(f32[128,1,2]{2,1,0:T(1,128)} %all-to-all-done, f32[]{:T(128)} %broadcast.165), dimensions={1}, to_apply=%all_to_all.7.reduce_sub_computation.3 | reduce | bytes 2052 | tf_op jit(solution)/shard_map/all_to_all | solution.py:89
  63.0 1.6 %eq.17 = f32[256]{0:T(256)} reshape(f32[128,2]{1,0:T(8,128)} %reduce.7) | data formatting | bytes 2048 | tf_op jit(solution)/shard_map/eq | solution.py:126
  64.6 1.1 %copy.77 = f32[129,4,136]{2,1,0:T(4,128)} copy(f32[129,4,136]{0,2,1:T(8,128)S(1)} %collective-permute-done.3) | data formatting | bytes 561408 | tf_op jit(solution)/shard_map/ppermute | solution.py:30
  65.7 1.4 %copy.76 = f32[129,4,136]{2,1,0:T(4,128)S(1)} copy(f32[129,4,136]{0,2,1:T(8,128)} %collective-permute-done.2) | data formatting | bytes 561408 | tf_op jit(solution)/shard_map/ppermute | solution.py:29
  67.1 5.1 %pad_maximum_fusion = f32[129,24,136]{2,1,0:T(8,128)S(1)} fusion(f32[129,4,136]{2,1,0:T(4,128)} %copy.77, f32[129,16,4]{2,1,0:T(8,128)S(1)} %copy.73, f32[1,16,128]{2,1,0:T(8,128)} %copy-done.5, f32[16,16,128]{2,1,0:T(8,128)} %param.17, f32[16,16,128]{2,1,0:T(8,128)} %param.16, f32[96,16,128]{2,1,0:T(8,128)S(1)} %bitcast.44, f32[129,16,4]{2,1,0:T(8,128)S(1)} %copy.72, ...), kind=kLoop, calls=%fused_computation.3 | loop fusion | flops 2947392 | bytes 3368448 | tf_op jit(solution)/shard_map/concatenate | solution.py:31
  74.4 2.5 %slice_subtract_fusion.4 = f32[6,16,22,134]{3,2,1,0:T(8,128)S(1)} fusion(f32[6,16,23,136]{3,2,1,0:T(8,128)S(1)} %subtract_multiply_fusion.6, f32[6,16,24,135]{3,2,1,0:T(8,128)S(1)} %subtract_multiply_fusion.7, f32[6,16,24,136]{3,2,1,0:T(8,128)S(1)} %bitcast.41), kind=kLoop, calls=%fused_computation.14 | loop fusion | flops 1132032 | bytes 6792192 | tf_op jit(solution)/shard_map/sub | solution.py:47
  78.9 0.7 subtract_multiply_fusion.4
  79.6 2.5 %slice_subtract_fusion.2 = f32[6,16,20,132]{3,2,1,0:T(8,128)S(1)} fusion(f32[6,16,21,134]{3,2,1,0:T(8,128)S(1)} %subtract_multiply_fusion.4, f32[6,16,22,133]{3,2,1,0:T(8,128)S(1)} %subtract_multiply_fusion.5, f32[6,16,22,134]{3,2,1,0:T(8,128)S(1)} %slice_subtract_fusion.4), kind=kLoop, calls=%fused_computation.10 | loop fusion | flops 1013760 | bytes 6082560 | tf_op jit(solution)/shard_map/sub | solution.py:47
  83.5 2.7 %slice_subtract_fusion = f32[6,16,18,130]{3,2,1,0:T(8,128)S(1)} fusion(f32[6,16,19,132]{3,2,1,0:T(8,128)S(1)} %subtract_multiply_fusion.2, f32[6,16,20,131]{3,2,1,0:T(8,128)S(1)} %subtract_multiply_fusion.3, f32[6,16,20,132]{3,2,1,0:T(8,128)S(1)} %slice_subtract_fusion.2), kind=kLoop, calls=%fused_computation.6 | loop fusion | flops 898560 | bytes 5391360 | tf_op jit(solution)/shard_map/sub | solution.py:47
  86.3 2.2 %subtract_multiply_fusion.1 = f32[6,16,18,129]{3,2,1,0:T(8,128)} fusion(f32[6,16,18,130]{3,2,1,0:T(8,128)S(1)} %slice_subtract_fusion, f32[16,18,129]{2,1,0:T(8,128)S(1)} %slice.376, f32[18,129]{1,0:T(8,128)S(1)} %slice_multiply_fusion.1), kind=kLoop, calls=%fused_computation.19 | loop fusion | flops 1560384 | bytes 2832840 | tf_op jit(solution)/shard_map/mul | solution.py:36
  88.4 2.2 %subtract_multiply_fusion = f32[6,16,17,130]{3,2,1,0:T(8,128)} fusion(f32[6,16,18,130]{3,2,1,0:T(8,128)S(1)} %slice_subtract_fusion, f32[16,17,130]{2,1,0:T(8,128)S(1)} %pad_maximum_fusion.8, f32[17,130]{1,0:T(8,128)S(1)} %slice_multiply_fusion), kind=kLoop, calls=%fused_computation.18 | loop fusion | flops 1485120 | bytes 2696200 | tf_op jit(solution)/shard_map/mul | solution.py:41
  90.6 9.5 %all-to-all-done.1 = f32[128,48,128]{2,1,0:T(8,128)} async-done(((f32[128,48,128]{2,1,0:T(8,128)}), f32[128,48,128]{2,1,0:T(8,128)}, u32[]{:S(2)}, u32[]{:S(2)}) %all-to-all-start.1) | async-done | bytes 3145760 | tf_op jit(solution)/shard_map/all_to_all | solution.py:82
  100.1 3.4 %fusion.2 = f32[16,24,128]{2,0,1:T(8,128)S(1)} fusion(f32[256,24,128]{2,1,0:T(8,128)} %bitcast.13, f32[256]{0:T(256)S(1)} %copy-done.9), kind=kOutput, calls=%fused_computation.4 | convolution fusion | flops 150999040 | bytes 3343360 | tf_op jit(solution)/shard_map/rk,kfc->rfc/dot_general | solution.py:129
  103.5 0.8 fusion.13
  104.3 4.4 %fusion.11 = f32[6,16,16,128]{3,2,1,0:T(8,128)} fusion(f32[6,16,17,130]{3,2,1,0:T(8,128)} %subtract_multiply_fusion, f32[6,16,18,129]{3,2,1,0:T(8,128)S(1)} %copy-done.2, f32[6,16,18,130]{3,2,1,0:T(8,128)S(1)} %slice_subtract_fusion, f32[6,16,16,128]{3,1,0,2:T(8,128)S(1)} %bitcast.47, f32[16,128]{1,0:T(8,128)S(1)} %copy-done.7), kind=kLoop, calls=%fused_computation.32 | loop fusion | flops 1179648 | bytes 5513216 | tf_op jit(solution)/shard_map/add | solution.py:136
  (66 shorter events, 10.0 us)
Async XLA Ops:
  0.0 25.5 %copy-start = (bf16[24,2048]{1,0:T(8,128)(2,1)S(1)}, bf16[24,2048]{1,0:T(8,128)(2,1)}, u32[]{:S(2)}) copy-start(bf16[24,2048]{1,0:T(8,128)(2,1)} %param.10) | copy-start | bytes 294916
  3.5 50.8 %all-to-all-start = ((f32[128,1,2]{2,1,0:T(1,128)}), f32[128,1,2]{2,1,0:T(1,128)}, u32[]{:S(2)}, u32[]{:S(2)}) async-start(f32[128,1,2]{2,1,0:T(1,128)} %copy.80), calls=%async_computation | async-start | bytes 131072 | tf_op jit(solution)/shard_map/all_to_all | solution.py:89
  16.5 18.8 %copy-start.5 = (f32[1,16,128]{2,1,0:T(8,128)}, f32[1,16,128]{2,1,0:T(8,128)S(1)}, u32[]{:S(2)}) copy-start(f32[1,16,128]{2,1,0:T(8,128)S(1)} %get-tuple-element.10) | copy-start | bytes 24580
  17.9 7.3 %copy-start.10 = (s32[1,256]{1,0:T(1,128)S(1)}, s32[1,256]{1,0:T(1,128)}, u32[]{:S(2)}) copy-start(s32[1,256]{1,0:T(1,128)} %param.12) | copy-start | bytes 3076
  17.9 7.3 %copy-start.11 = (s32[1,128]{1,0:T(1,128)S(1)}, s32[1,128]{1,0:T(1,128)}, u32[]{:S(2)}) copy-start(s32[1,128]{1,0:T(1,128)} %param.14) | copy-start | bytes 1540
  18.9 15.6 %collective-permute-start.1 = (f32[129,16,4]{0,1,2:T(8,128)S(1)}, f32[129,16,4]{0,1,2:T(8,128)S(1)}, u32[]{:S(2)}, u32[]{:S(2)}) collective-permute-start(f32[129,16,4]{0,1,2:T(8,128)S(1)} %copy.71), channel_id=1, source_target_pairs={{0,31},{1,0},{2,1},{3,2},{4,3},{5,4},{6,5},{7,6},{8,7},{9,8},{10,9... | collective-permute-start | bytes 99080 | tf_op jit(solution)/shard_map/ppermute | solution.py:27
  25.1 8.5 %collective-permute-start = (f32[129,16,4]{0,1,2:T(8,128)S(1)}, f32[129,16,4]{0,1,2:T(8,128)S(1)}, u32[]{:S(2)}, u32[]{:S(2)}) collective-permute-start(f32[129,16,4]{0,1,2:T(8,128)S(1)} %copy.70), channel_id=1, source_target_pairs={{0,1},{1,2},{2,3},{3,4},{4,5},{5,6},{6,7},{7,8},{8,9},{9,10},{10,1... | collective-permute-start | bytes 99080 | tf_op jit(solution)/shard_map/ppermute | solution.py:26
  26.1 9.2 %copy-start.1 = (f32[6,16,16,128]{3,2,1,0:T(8,128)S(1)}, f32[6,16,16,128]{3,2,1,0:T(8,128)}, u32[]{:S(2)}) copy-start(f32[6,16,16,128]{3,2,1,0:T(8,128)} %param.15) | copy-start | bytes 2359300
  41.2 23.4 %collective-permute-start.3 = (f32[129,4,136]{0,2,1:T(8,128)}, f32[129,4,136]{0,2,1:T(8,128)S(1)}, u32[]{:S(2)}, u32[]{:S(2)}) collective-permute-start(f32[129,4,136]{0,2,1:T(8,128)} %copy.75), channel_id=1, source_target_pairs={{32,0},{64,32},{96,64},{33,1},{65,33},{97,65},{34,2},{66,34},{98,6... | collective-permute-start | bytes 842120 | tf_op jit(solution)/shard_map/ppermute | solution.py:30
  42.5 23.2 %collective-permute-start.2 = (f32[129,4,136]{0,2,1:T(8,128)}, f32[129,4,136]{0,2,1:T(8,128)}, u32[]{:S(2)}, u32[]{:S(2)}) collective-permute-start(f32[129,4,136]{0,2,1:T(8,128)} %copy.74), channel_id=1, source_target_pairs={{0,32},{32,64},{64,96},{1,33},{33,65},{65,97},{2,34},{34,66},{66,9... | collective-permute-start | bytes 842120 | tf_op jit(solution)/shard_map/ppermute | solution.py:29
  54.3 45.8 %all-to-all-start.1 = ((f32[128,48,128]{2,1,0:T(8,128)}), f32[128,48,128]{2,1,0:T(8,128)}, u32[]{:S(2)}, u32[]{:S(2)}) async-start(f32[128,48,128]{2,1,0:T(8,128)} %bitcast.46), calls=%async_computation.1 | async-start | bytes 6291456 | tf_op jit(solution)/shard_map/all_to_all | solution.py:82
  74.4 2.6 %copy-start.3 = (f32[16,16,128]{2,1,0:T(8,128)S(1)}, f32[16,16,128]{2,1,0:T(8,128)}, u32[]{:S(2)}) copy-start(f32[16,16,128]{2,1,0:T(8,128)} %param.17) | copy-start | bytes 393220
  74.4 2.6 %copy-start.4 = (f32[16,16,128]{2,1,0:T(8,128)S(1)}, f32[16,16,128]{2,1,0:T(8,128)}, u32[]{:S(2)}) copy-start(f32[16,16,128]{2,1,0:T(8,128)} %param.16) | copy-start | bytes 393220
  74.4 2.6 %copy-start.6 = (f32[1,16,128]{2,1,0:T(8,128)S(1)}, f32[1,16,128]{2,1,0:T(8,128)}, u32[]{:S(2)}) copy-start(f32[1,16,128]{2,1,0:T(8,128)} %copy-done.5) | copy-start | bytes 24580
  88.4 11.7 %copy-start.9 = (f32[256]{0:T(256)S(1)}, f32[256]{0:T(256)}, u32[]{:S(2)}) copy-start(f32[256]{0:T(256)} %eq.17) | copy-start | bytes 3076
  90.6 12.9 %copy-start.8 = (f32[96,24]{0,1:T(8,128)S(1)}, f32[96,24]{0,1:T(8,128)}, u32[]{:S(2)}) copy-start(f32[96,24]{0,1:T(8,128)} %param.19) | copy-start | bytes 27652
  90.6 13.7 %copy-start.7 = (f32[16,128]{1,0:T(8,128)S(1)}, f32[16,128]{1,0:T(8,128)}, u32[]{:S(2)}) copy-start(f32[16,128]{1,0:T(8,128)} %get-tuple-element.9) | copy-start | bytes 24580
  100.1 4.2 %copy-start.2 = (f32[6,16,18,129]{3,2,1,0:T(8,128)S(1)}, f32[6,16,18,129]{3,2,1,0:T(8,128)}, u32[]{:S(2)}) copy-start(f32[6,16,18,129]{3,2,1,0:T(8,128)} %subtract_multiply_fusion.1) | copy-start | bytes 2674948
where the time goes:
time: 110 us; the launch traced here: 109 us
  other arithmetic  36.7 us (33%)
  starting transfers between devices  28.4 us (26%)
  local copies, waits for them, and re-layouts  16.1 us (15%)
  waiting for transfers between devices  15 us (14%)
  matrix products  12.1 us (11%)
    all_to_all x1, starting transfers between devices, per_device(): lax.all_to_all(targets.reshape(tile_count, slot_count), ('lat', 'lon'), s...  11.7 us
    all_to_all x1, waiting for transfers between devices, per_device(): lax.all_to_all(partials.reshape(tile_count, slot_count * field_count, blo...  9.48 us
    dot_general x1, matrix products, per_device(): jnp.einsum('fsb,sbc->sfc', chosen, remap_weights[0], preferred_element_ty...  7.91 us
    sub x3, other arithmetic, advect(): inner + east_flow[..., 1:-1, :-1] - east_flow[..., 1:-1, 1:]  7.79 us
    all_to_all x1, starting transfers between devices, per_device(): lax.all_to_all(partials.reshape(tile_count, slot_count * field_count, blo...  5.93 us
    ppermute x1, starting transfers between devices, with_halo(): lax.ppermute(block[..., :width], 'lon', shifted_pairs(lon_count, -1, True))  5.54 us
    ppermute x1, waiting for transfers between devices, with_halo(): lax.ppermute(block[..., -width:], 'lon', shifted_pairs(lon_count, 1, True))  5.53 us
    concatenate x2, other arithmetic, with_halo(): return jnp.concatenate([south, block, north], axis=-2)  5.37 us
  transfers between devices with their start and end apart: 6, of which 2 were waited for; matrix products, arithmetic and copies ran while one was open for 49% of the time, Pallas kernels for 0%

commit v1 on v0

--- a/solution.py
+++ b/solution.py
@@ -79,20 +79,14 @@
     is_live = slot_ids % slot_count < jnp.repeat(block_count[0], slot_count)
     partials = jnp.where(is_live[:, None, None], partials, jnp.float32(0.0))
     targets = jnp.where(is_live, target_block[0], -1).astype(jnp.float32)
-    arrived = lax.all_to_all(
-        partials.reshape(tile_count, slot_count * field_count, block_cells),
-        ("lat", "lon"),
-        split_axis=0,
-        concat_axis=0,
-        tiled=True,
+    sent = partials.reshape(tile_count, slot_count * field_count, block_cells)
+    sent, tracers, east_velocity, north_velocity, land_mask = lax.optimization_barrier(
+        (sent, tracers, east_velocity, north_velocity, land_mask)
     )
-    landed = lax.all_to_all(
-        targets.reshape(tile_count, slot_count),
-        ("lat", "lon"),
-        split_axis=0,
-        concat_axis=0,
-        tiled=True,
-    )
+    arrived = lax.all_to_all(sent, ("lat", "lon"), split_axis=0, concat_axis=0, tiled=True)
+    every_target = lax.all_gather(targets, ("lat", "lon"))
+    me = lax.axis_index("lat") * lax.axis_size("lon") + lax.axis_index("lon")
+    landed = lax.dynamic_slice_in_dim(every_target, me * slot_count, slot_count, axis=1)
 
     sea_here = land_mask.astype(jnp.float32)
     planes = tracer_count * level_count

time: 110 us -> 406 us (3.69)
  blocking collectives: 0 us -> 328 us
  waiting for transfers between devices: 15 us -> 0.01 us
  starting transfers between devices: 28.4 us -> 18.9 us
  other arithmetic: 36.7 us -> 32 us
    all_gather x0 -> x1, blocking collectives: none -> 328 us  [per_device(): every_target = lax.all_gather(targets, ('lat', 'lon'))]
    all_to_all x2 -> x1, starting transfers between devices: 17.6 us -> 6.98 us  [per_device(): lax.all_to_all(sent, ('lat', 'lon'), split_axis=0, concat_axis=0, tiled=T...]
    all_to_all x2 -> x1, waiting for transfers between devices: 9.49 us -> 0.01 us  [per_device(): lax.all_to_all(sent, ('lat', 'lon'), split_axis=0, concat_axis=0, tiled=T...]
    ppermute x1, waiting for transfers between devices: 5.53 us -> 0.01 us  [with_halo(): lax.ppermute(block[..., -width:], 'lon', shifted_pairs(lon_count, 1, True))]
  transfers between devices with their start and end apart: 6 -> 5, of which waited for: 2 -> 0; matrix products, arithmetic and copies ran while one was open for 49% -> 9% of each run, Pallas kernels for 0% -> 0%
where the time goes in v1:
time: 406 us
  blocking collectives  328 us (81%)
  other arithmetic  32 us (8%)
  starting transfers between devices  18.9 us (5%)
  local copies, waits for them, and re-layouts  15.3 us (4%)
  matrix products  10.7 us (3%)
    all_gather x1, blocking collectives, per_device(): every_target = lax.all_gather(targets, ('lat', 'lon'))  328 us
  transfers between devices with their start and end apart: 5, of which 0 were waited for; matrix products, arithmetic and copies ran while one was open for 9% of the time, Pallas kernels for 0%

profile of v1, /device:TPU:0, one launch (start us, length us, event | category | flops | bytes accessed | tf_op | source)
XLA Modules:
  0.0 405.7 jit_solution(17114372879626331558)
XLA Ops:
  0.0 0.7 compare_select_fusion
  1.4 0.7 broadcast_in_dim.30
  2.3 1.0 gather_fusion
  3.4 6.5 %broadcast_select_fusion = f32[256,24,128]{2,1,0:T(8,128)} fusion(bf16[1,256,128,128]{3,2,1,0:T(8,128)(2,1)} %param.11, bf16[256,24,128]{2,1,0:T(8,128)(2,1)S(1)} %gather_fusion, pred[256]{0:T(512)(128)(4,1)S(1)} %compare_and_fusion, pred[256]{0:T(512)(128)(4,1)S(1)} %fusion.20), kind=kOutput, calls=%fused_computation.28 | convolution fusion | flops 202899456 | bytes 13107712 | tf_op jit(solution)/shard_map/fsb,sbc->sfc/dot_general | solution.py:75
  11.6 1.7 collective-permute-start
  14.0 5.1 %collective-permute-start.1 = (f32[129,16,4]{0,1,2:T(8,128)S(1)}, f32[129,16,4]{0,1,2:T(8,128)S(1)}, u32[]{:S(2)}, u32[]{:S(2)}) collective-permute-start(f32[129,16,4]{0,1,2:T(8,128)S(1)} %copy.57), channel_id=1, source_target_pairs={{0,31},{1,0},{2,1},{3,2},{4,3},{5,4},{6,5},{7,6},{8,7},{9,8},{10,9... | collective-permute-start | bytes 99080 | tf_op jit(solution)/shard_map/ppermute | solution.py:27
  19.1 7.0 %all-to-all-start = ((f32[128,48,128]{2,1,0:T(8,128)}), f32[128,48,128]{2,1,0:T(8,128)}, u32[]{:S(2)}, u32[]{:S(2)}) async-start(f32[128,48,128]{2,1,0:T(8,128)} %bitcast.48), calls=%async_computation | async-start | bytes 6291456 | tf_op jit(solution)/shard_map/all_to_all | solution.py:86
  26.1 0.7 reshape.137
  26.8 0.8 copy.58
  27.6 0.8 copy.59
  28.5 2.6 pad_maximum_fusion.7
  31.1 2.2 copy.60
  33.2 1.1 copy.61
  34.4 1.3 collective-permute-start.3
  35.7 3.8 collective-permute-start.2
  39.5 0.7 convert_bitcast_fusion
  40.2 328.4 %all-gather = f32[128,1,256]{2,1,0:T(1,128)S(1)} all-gather(f32[1,1,256]{2,1,0:T(1,128)S(1)} %convert_bitcast_fusion), channel_id=1, replica_groups=mesh['lat'=4,'lon'=32] {'lat','lon'}, dimensions={0}, use_global_device_ids=true | all-gather | bytes 132096 | tf_op jit(solution)/shard_map/all_gather | solution.py:87
  368.6 0.9 dynamic-slice_reduce_fusion
  369.4 1.6 eq.17
  371.0 1.1 copy.63
  372.1 1.4 copy.62
  373.5 5.2 %pad_maximum_fusion = f32[129,24,136]{2,1,0:T(8,128)S(1)} fusion(f32[129,4,136]{2,1,0:T(4,128)} %copy.63, f32[129,16,4]{2,1,0:T(8,128)S(1)} %copy.59, f32[1,16,128]{2,1,0:T(8,128)} %copy-done.7, f32[16,16,128]{2,1,0:T(8,128)} %param.17, f32[16,16,128]{2,1,0:T(8,128)} %param.16, f32[96,16,128]{2,1,0:T(8,128)S(1)} %bitcast.46, f32[129,16,4]{2,1,0:T(8,128)S(1)} %copy.58, ...), kind=kLoop, calls=%fused_computation.3 | loop fusion | flops 2947392 | bytes 3368448 | tf_op jit(solution)/shard_map/concatenate | solution.py:31
  381.0 2.5 slice_subtract_fusion.4
  385.5 0.7 subtract_multiply_fusion.4
  386.2 2.5 slice_subtract_fusion.2
  389.4 0.7 subtract_multiply_fusion.2
  390.1 2.7 slice_subtract_fusion
  392.8 2.1 subtract_multiply_fusion.1
  395.0 2.2 subtract_multiply_fusion
  397.2 3.4 fusion.2
  400.6 0.8 fusion.13
  401.4 4.3 %fusion.11 = f32[6,16,16,128]{3,2,1,0:T(8,128)} fusion(f32[6,16,17,130]{3,2,1,0:T(8,128)} %subtract_multiply_fusion, f32[6,16,18,129]{3,2,1,0:T(8,128)S(1)} %copy-done.2, f32[6,16,18,130]{3,2,1,0:T(8,128)S(1)} %slice_subtract_fusion, f32[6,16,16,128]{3,1,0,2:T(8,128)S(1)} %bitcast.49, f32[16,128]{1,0:T(8,128)S(1)} %copy-done.9), kind=kLoop, calls=%fused_computation.32 | loop fusion | flops 1179648 | bytes 5513216 | tf_op jit(solution)/shard_map/add | solution.py:130
  (63 shorter events, 7.9 us)
Async XLA Ops:
  0.0 2.3 copy-start
  3.3 6.6 %copy-start.11 = (s32[16,128]{1,0:T(8,128)S(1)}, s32[16,128]{1,0:T(8,128)}, u32[]{:S(2)}) copy-start(s32[16,128]{1,0:T(8,128)} %param.18) | copy-start | bytes 24580
  3.3 7.2 %copy-start.1 = (f32[6,16,16,128]{3,2,1,0:T(8,128)S(1)}, f32[6,16,16,128]{3,2,1,0:T(8,128)}, u32[]{:S(2)}) copy-start(f32[6,16,16,128]{3,2,1,0:T(8,128)} %param.15) | copy-start | bytes 2359300
  3.4 7.2 %copy-start.3 = (f32[16,16,128]{2,1,0:T(8,128)S(1)}, f32[16,16,128]{2,1,0:T(8,128)}, u32[]{:S(2)}) copy-start(f32[16,16,128]{2,1,0:T(8,128)} %param.17) | copy-start | bytes 393220
  3.4 7.2 %copy-start.5 = (f32[16,16,128]{2,1,0:T(8,128)S(1)}, f32[16,16,128]{2,1,0:T(8,128)}, u32[]{:S(2)}) copy-start(f32[16,16,128]{2,1,0:T(8,128)} %param.16) | copy-start | bytes 393220
  10.5 17.9 %copy-start.7 = (f32[1,16,128]{2,1,0:T(8,128)}, f32[1,16,128]{2,1,0:T(8,128)S(1)}, u32[]{:S(2)}) copy-start(f32[1,16,128]{2,1,0:T(8,128)S(1)} %get-tuple-element.20) | copy-start | bytes 24580
  11.6 15.2 %collective-permute-start = (f32[129,16,4]{0,1,2:T(8,128)S(1)}, f32[129,16,4]{0,1,2:T(8,128)S(1)}, u32[]{:S(2)}, u32[]{:S(2)}) collective-permute-start(f32[129,16,4]{0,1,2:T(8,128)S(1)} %copy.56), channel_id=1, source_target_pairs={{0,1},{1,2},{2,3},{3,4},{4,5},{5,6},{6,7},{7,8},{8,9},{9,10},{10,1... | collective-permute-start | bytes 99080 | tf_op jit(solution)/shard_map/ppermute | solution.py:26
  14.0 13.7 %collective-permute-start.1 = (f32[129,16,4]{0,1,2:T(8,128)S(1)}, f32[129,16,4]{0,1,2:T(8,128)S(1)}, u32[]{:S(2)}, u32[]{:S(2)}) collective-permute-start(f32[129,16,4]{0,1,2:T(8,128)S(1)} %copy.57), channel_id=1, source_target_pairs={{0,31},{1,0},{2,1},{3,2},{4,3},{5,4},{6,5},{7,6},{8,7},{9,8},{10,9... | collective-permute-start | bytes 99080 | tf_op jit(solution)/shard_map/ppermute | solution.py:27
  19.1 378.0 %all-to-all-start = ((f32[128,48,128]{2,1,0:T(8,128)}), f32[128,48,128]{2,1,0:T(8,128)}, u32[]{:S(2)}, u32[]{:S(2)}) async-start(f32[128,48,128]{2,1,0:T(8,128)} %bitcast.48), calls=%async_computation | async-start | bytes 6291456 | tf_op jit(solution)/shard_map/all_to_all | solution.py:86
  34.4 336.6 %collective-permute-start.3 = (f32[129,4,136]{0,2,1:T(8,128)}, f32[129,4,136]{0,2,1:T(8,128)S(1)}, u32[]{:S(2)}, u32[]{:S(2)}) collective-permute-start(f32[129,4,136]{0,2,1:T(8,128)} %copy.61), channel_id=1, source_target_pairs={{32,0},{64,32},{96,64},{33,1},{65,33},{97,65},{34,2},{66,34},{98,6... | collective-permute-start | bytes 842120 | tf_op jit(solution)/shard_map/ppermute | solution.py:30
  35.7 336.5 %collective-permute-start.2 = (f32[129,4,136]{0,2,1:T(8,128)}, f32[129,4,136]{0,2,1:T(8,128)}, u32[]{:S(2)}, u32[]{:S(2)}) collective-permute-start(f32[129,4,136]{0,2,1:T(8,128)} %copy.60), channel_id=1, source_target_pairs={{0,32},{32,64},{64,96},{1,33},{33,65},{65,97},{2,34},{34,66},{66,9... | collective-permute-start | bytes 842120 | tf_op jit(solution)/shard_map/ppermute | solution.py:29
  381.0 2.6 copy-start.4
  381.0 2.6 copy-start.6
  381.0 2.6 copy-start.8
  395.0 2.2 copy-start.12
  397.1 3.4 copy-start.10
  397.1 4.2 %copy-start.9 = (f32[16,128]{1,0:T(8,128)S(1)}, f32[16,128]{1,0:T(8,128)}, u32[]{:S(2)}) copy-start(f32[16,128]{1,0:T(8,128)} %get-tuple-element.19) | copy-start | bytes 24580
  397.2 4.2 %copy-start.2 = (f32[6,16,18,129]{3,2,1,0:T(8,128)S(1)}, f32[6,16,18,129]{3,2,1,0:T(8,128)}, u32[]{:S(2)}) copy-start(f32[6,16,18,129]{3,2,1,0:T(8,128)} %subtract_multiply_fusion.1) | copy-start | bytes 2674948

commit v2 on v1

--- a/solution.py
+++ b/solution.py
@@ -2,6 +2,7 @@
 import jax.numpy as jnp
 from jax import lax
 from jax.sharding import PartitionSpec as P
+
 
 NSUB = 4
 
@@ -52,7 +53,7 @@
     )
 
 
-def per_device(
+def coupled_step(
     atm_fluxes,
     remap_weights,
     source_block,
@@ -84,9 +85,13 @@
         (sent, tracers, east_velocity, north_velocity, land_mask)
     )
     arrived = lax.all_to_all(sent, ("lat", "lon"), split_axis=0, concat_axis=0, tiled=True)
-    every_target = lax.all_gather(targets, ("lat", "lon"))
     me = lax.axis_index("lat") * lax.axis_size("lon") + lax.axis_index("lon")
-    landed = lax.dynamic_slice_in_dim(every_target, me * slot_count, slot_count, axis=1)
+    spread = jnp.where(
+        jnp.arange(tile_count)[None, :, None] == me,
+        targets.reshape(tile_count, 1, slot_count),
+        jnp.float32(0.0),
+    )
+    landed = lax.psum_scatter(spread, ("lat", "lon"), scatter_dimension=0, tiled=True)
 
     sea_here = land_mask.astype(jnp.float32)
     planes = tracer_count * level_count
@@ -144,7 +149,7 @@
         P(),
     )
     return jax.shard_map(
-        per_device,
+        coupled_step,
         mesh=mesh,
         in_specs=placed,
         out_specs=P(None, None, "lat", "lon"),

time: 406 us -> 757 us (1.86)
  waiting for transfers between devices: 0.01 us -> 664 us
  blocking collectives: 328 us -> 0 us
  between operations: 0.42 us -> 13.8 us
    reduce_scatter x0 -> x1, waiting for transfers between devices: none -> 657 us  [coupled_step(): lax.psum_scatter(spread, ('lat', 'lon'), scatter_dimension=0, tiled=True)]
    all_gather x1 -> x0, blocking collectives: 328 us -> none  [per_device(): every_target = lax.all_gather(targets, ('lat', 'lon'))]
  transfers between devices with their start and end apart: 5 -> 6, of which waited for: 0 -> 2; matrix products, arithmetic and copies ran while one was open for 9% -> 4% of each run, Pallas kernels for 0% -> 0%
where the time goes in v2:
time: 757 us; the launch traced here: 756 us
  waiting for transfers between devices  664 us (88%)
  other arithmetic  36.4 us (5%)
  starting transfers between devices  17.9 us (2%)
  between operations  13.8 us (2%)
  local copies, waits for them, and re-layouts  13.7 us (2%)
  matrix products  10.7 us (1%)
    reduce_scatter x1, waiting for transfers between devices, coupled_step(): lax.psum_scatter(spread, ('lat', 'lon'), scatter_dimension=0, tiled=True)  657 us
  transfers between devices with their start and end apart: 6, of which 2 were waited for; matrix products, arithmetic and copies ran while one was open for 4% of the time, Pallas kernels for 0%

profile of v2, /device:TPU:0, one launch (start us, length us, event | category | flops | bytes accessed | tf_op | source)
XLA Modules:
  0.0 756.2 jit_solution(10211775214536684573)
XLA Ops:
  6.5 0.7 compare_select_fusion
  7.3 0.7 broadcast_in_dim.50
  8.2 0.7 compare_and_fusion
  8.9 1.0 gather_fusion
  9.9 6.5 broadcast_select_fusion.1
  18.2 6.7 collective-permute-start.1
  27.1 7.0 collective-permute-done
  34.1 0.8 copy.58
  34.9 0.8 copy.59
  35.7 2.6 pad_maximum_fusion.7
  38.3 2.2 copy.60
  40.5 1.1 copy.61
  41.6 1.3 collective-permute-start.3
  42.9 3.9 collective-permute-start.2
  46.8 4.5 broadcast_select_fusion
  51.3 5.9 all-to-all-start
  57.3 656.5 %reduce-scatter.2.cloned.1.call-done = f32[1,128,2]{2,1,0:T(8,128)} async-done(((f32[128,128,2]{2,1,0:T(8,128)}), f32[1,128,2]{2,1,0:T(8,128)}) %reduce-scatter.2.cloned.1.call-update) | async-done | bytes 1040 | tf_op jit(solution)/shard_map/reduce_scatter | solution.py:94
  713.8 1.0 eq.30
  714.8 1.1 copy.63
  715.9 1.4 copy.62
  717.3 5.1 pad_maximum_fusion
  723.9 0.7 subtract_multiply_fusion.6
  724.6 2.5 slice_subtract_fusion.4
  729.1 0.7 subtract_multiply_fusion.4
  729.8 2.5 slice_subtract_fusion.2
  733.0 0.7 subtract_multiply_fusion.2
  733.7 2.7 slice_subtract_fusion
  736.5 2.1 subtract_multiply_fusion.1
  738.6 2.1 subtract_multiply_fusion
  740.7 3.4 fusion.2
  744.1 0.8 fusion.13
  744.9 4.4 fusion.11
  (67 shorter events, 8.1 us)
Async XLA Ops:
  6.5 1.6 copy-start
  6.5 707.2 %reduce-scatter.2.cloned.1.call-start = ((), (), s32[]{:S(2)}) async-start(), calls=%async_computation.2 | async-start | bytes 8454144 | tf_op jit(solution)/shard_map/reduce_scatter | solution.py:94
  9.9 6.6 copy-start.10
  9.9 7.2 copy-start.2
  9.9 7.2 copy-start.4
  9.9 7.2 copy-start.6
  17.1 9.0 %copy-start.12 = (s32[1,256]{1,0:T(1,128)S(1)}, s32[1,256]{1,0:T(1,128)}, u32[]{:S(2)}) copy-start(s32[1,256]{1,0:T(1,128)} %param.13) | copy-start | bytes 3076
  17.1 9.8 %copy-start.11 = (s32[1,128]{1,0:T(1,128)S(1)}, s32[1,128]{1,0:T(1,128)}, u32[]{:S(2)}) copy-start(s32[1,128]{1,0:T(1,128)} %param.14) | copy-start | bytes 1540
  18.2 16.8 %collective-permute-start.1 = (f32[129,16,4]{0,1,2:T(8,128)S(1)}, f32[129,16,4]{0,1,2:T(8,128)S(1)}, u32[]{:S(2)}, u32[]{:S(2)}) collective-permute-start(f32[129,16,4]{0,1,2:T(8,128)S(1)} %copy.57), channel_id=1, source_target_pairs={{0,31},{1,0},{2,1},{3,2},{4,3},{5,4},{6,5},{7,6},{8,7},{9,8},{10,9... | collective-permute-start | bytes 99080 | tf_op jit(solution)/shard_map/ppermute | solution.py:28
  25.6 8.5 %collective-permute-start = (f32[129,16,4]{0,1,2:T(8,128)S(1)}, f32[129,16,4]{0,1,2:T(8,128)S(1)}, u32[]{:S(2)}, u32[]{:S(2)}) collective-permute-start(f32[129,16,4]{0,1,2:T(8,128)S(1)} %copy.56), channel_id=1, source_target_pairs={{0,1},{1,2},{2,3},{3,4},{4,5},{5,6},{6,7},{7,8},{8,9},{9,10},{10,1... | collective-permute-start | bytes 99080 | tf_op jit(solution)/shard_map/ppermute | solution.py:27
  41.6 673.1 %collective-permute-start.3 = (f32[129,4,136]{0,2,1:T(8,128)}, f32[129,4,136]{0,2,1:T(8,128)S(1)}, u32[]{:S(2)}, u32[]{:S(2)}) collective-permute-start(f32[129,4,136]{0,2,1:T(8,128)} %copy.61), channel_id=1, source_target_pairs={{32,0},{64,32},{96,64},{33,1},{65,33},{97,65},{34,2},{66,34},{98,6... | collective-permute-start | bytes 842120 | tf_op jit(solution)/shard_map/ppermute | solution.py:31
  42.9 673.0 %collective-permute-start.2 = (f32[129,4,136]{0,2,1:T(8,128)}, f32[129,4,136]{0,2,1:T(8,128)}, u32[]{:S(2)}, u32[]{:S(2)}) collective-permute-start(f32[129,4,136]{0,2,1:T(8,128)} %copy.60), channel_id=1, source_target_pairs={{0,32},{32,64},{64,96},{1,33},{33,65},{65,97},{2,34},{34,66},{66,9... | collective-permute-start | bytes 842120 | tf_op jit(solution)/shard_map/ppermute | solution.py:30
  51.3 689.4 %all-to-all-start = ((f32[128,48,128]{2,1,0:T(8,128)}), f32[128,48,128]{2,1,0:T(8,128)}, u32[]{:S(2)}, u32[]{:S(2)}) async-start(f32[128,48,128]{2,1,0:T(8,128)} %bitcast.46), calls=%async_computation.1 | async-start | bytes 6291456 | tf_op jit(solution)/shard_map/all_to_all | solution.py:87
  724.6 2.6 copy-start.5
  724.6 2.5 copy-start.7
  740.7 3.4 copy-start.9
  740.7 4.2 copy-start.8
  740.7 4.2 copy-start.3
  744.9 4.4 copy-start.1
Sparse Core Ops, SparseCore 0:
  51.4 662.2 reduce-scatter.1

commit v3 on v0

--- a/solution.py
+++ b/solution.py
@@ -2,6 +2,7 @@
 import jax.numpy as jnp
 from jax import lax
 from jax.sharding import PartitionSpec as P
+
 
 NSUB = 4
 
@@ -9,26 +10,36 @@
 diffusion_number = 0.2
 
 
-def shifted_pairs(count, step, wrap):
+def neighbour_pairs(lat_count, lon_count, dlat, dlon):
     pairs = []
-    for i in range(count):
-        j = i + step
-        if 0 <= j < count:
-            pairs.append((i, j))
-        elif wrap:
-            pairs.append((i, j % count))
+    for a in range(lat_count):
+        for o in range(lon_count):
+            b = a + dlat
+            if 0 <= b < lat_count:
+                pairs.append((a * lon_count + o, b * lon_count + (o + dlon) % lon_count))
     return pairs
 
 
 def with_halo(block, width):
+    lat_count = lax.axis_size("lat")
     lon_count = lax.axis_size("lon")
-    lat_count = lax.axis_size("lat")
-    west = lax.ppermute(block[..., -width:], "lon", shifted_pairs(lon_count, 1, True))
-    east = lax.ppermute(block[..., :width], "lon", shifted_pairs(lon_count, -1, True))
-    block = jnp.concatenate([west, block, east], axis=-1)
-    south = lax.ppermute(block[..., -width:, :], "lat", shifted_pairs(lat_count, 1, False))
-    north = lax.ppermute(block[..., :width, :], "lat", shifted_pairs(lat_count, -1, False))
-    return jnp.concatenate([south, block, north], axis=-2)
+    rows, cols = block.shape[-2:]
+    row_part = {-1: slice(0, width), 0: slice(None), 1: slice(rows - width, rows)}
+    col_part = {-1: slice(0, width), 0: slice(None), 1: slice(cols - width, cols)}
+    got = {}
+    for dlat in (-1, 0, 1):
+        for dlon in (-1, 0, 1):
+            if dlat == 0 and dlon == 0:
+                continue
+            got[dlat, dlon] = lax.ppermute(
+                block[..., row_part[dlat], col_part[dlon]],
+                ("lat", "lon"),
+                neighbour_pairs(lat_count, lon_count, dlat, dlon),
+            )
+    south = jnp.concatenate([got[1, 1], got[1, 0], got[1, -1]], axis=-1)
+    middle = jnp.concatenate([got[0, 1], block, got[0, -1]], axis=-1)
+    north = jnp.concatenate([got[-1, 1], got[-1, 0], got[-1, -1]], axis=-1)
+    return jnp.concatenate([south, middle, north], axis=-2)
 
 
 def advect(tracer_now, east_speed, north_speed, sea_mask):
@@ -52,7 +63,7 @@
     )
 
 
-def per_device(
+def coupled_step(
     atm_fluxes,
     remap_weights,
     source_block,
@@ -79,13 +90,8 @@
     is_live = slot_ids % slot_count < jnp.repeat(block_count[0], slot_count)
     partials = jnp.where(is_live[:, None, None], partials, jnp.float32(0.0))
     targets = jnp.where(is_live, target_block[0], -1).astype(jnp.float32)
-    arrived = lax.all_to_all(
-        partials.reshape(tile_count, slot_count * field_count, block_cells),
-        ("lat", "lon"),
-        split_axis=0,
-        concat_axis=0,
-        tiled=True,
-    )
+    sent = partials.reshape(tile_count, slot_count * field_count, block_cells)
+    arrived = lax.all_to_all(sent, ("lat", "lon"), split_axis=0, concat_axis=0, tiled=True)
     landed = lax.all_to_all(
         targets.reshape(tile_count, slot_count),
         ("lat", "lon"),
@@ -150,7 +156,7 @@
         P(),
     )
     return jax.shard_map(
-        per_device,
+        coupled_step,
         mesh=mesh,
         in_specs=placed,
         out_specs=P(None, None, "lat", "lon"),

time: 110 us -> 123 us (1.12)
  starting transfers between devices: 28.4 us -> 51.8 us
  waiting for transfers between devices: 15 us -> 3.69 us
  local copies, waits for them, and re-layouts: 16.1 us -> 20.8 us
  other arithmetic: 36.7 us -> 34.3 us
  matrix products: 12.1 us -> 10.7 us
    ppermute x4 -> x8, starting transfers between devices: 10.7 us -> 25.9 us  [with_halo(): lax.ppermute(block[..., row_part[dlat], col_part[dlon]], ('lat', 'lon'),...]
    all_to_all x2, starting transfers between devices: 17.6 us -> 25.9 us  [the longest x1 14.2 us: coupled_step(): lax.all_to_all(sent, ('lat', 'lon'), split_axis=0, concat_axis=0, tiled=T...]
    all_to_all x2, waiting for transfers between devices: 9.49 us -> 3.67 us  [the longest x1 3.67 us: coupled_step(): lax.all_to_all(sent, ('lat', 'lon'), split_axis=0, concat_axis=0, tiled=T...]
    ppermute x4 -> x8, waiting for transfers between devices: 5.54 us -> 0.02 us  [with_halo(): lax.ppermute(block[..., row_part[dlat], col_part[dlon]], ('lat', 'lon'),...]
    ppermute x4 -> x8, local copies, waits for them, and re-layouts: 4.13 us -> 8.93 us  [with_halo(): lax.ppermute(block[..., row_part[dlat], col_part[dlon]], ('lat', 'lon'),...]
    slice x1 -> x0, other arithmetic: 2.6 us -> none  [with_halo(): block[..., -width:, :]]
    slice x6 -> x12, local copies, waits for them, and re-layouts: 5.14 us -> 6.96 us  [the longest x11 6.8 us: with_halo(): block[..., row_part[dlat], col_part[dlon]]]
    concatenate x3, other arithmetic: 6.72 us -> 8.24 us  [the longest x2 6.9 us: with_halo(): return jnp.concatenate([south, middle, north], axis=-2)]
  transfers between devices with their start and end apart: 6 -> 10, of which waited for: 2 -> 1; matrix products, arithmetic and copies ran while one was open for 49% -> 44% of each run, Pallas kernels for 0% -> 0%
where the time goes in v3:
time: 123 us; the launch traced here: 122 us
  starting transfers between devices  51.8 us (42%)
  other arithmetic  34.3 us (28%)
  local copies, waits for them, and re-layouts  20.8 us (17%)
  matrix products  10.7 us (9%)
  waiting for transfers between devices  3.69 us (3%)
    ppermute x8, starting transfers between devices, with_halo(): lax.ppermute(block[..., row_part[dlat], col_part[dlon]], ('lat', 'lon'),...  25.9 us
    all_to_all x1, starting transfers between devices, coupled_step(): lax.all_to_all(sent, ('lat', 'lon'), split_axis=0, concat_axis=0, tiled=T...  14.2 us
    all_to_all x1, starting transfers between devices, coupled_step(): lax.all_to_all(targets.reshape(tile_count, slot_count), ('lat', 'lon'), s...  11.7 us
    ppermute x8, local copies, waits for them, and re-layouts, with_halo(): lax.ppermute(block[..., row_part[dlat], col_part[dlon]], ('lat', 'lon'),...  8.93 us
    sub x3, other arithmetic, advect(): inner + east_flow[..., 1:-1, :-1] - east_flow[..., 1:-1, 1:]  7.82 us
    concatenate x2, other arithmetic, with_halo(): return jnp.concatenate([south, middle, north], axis=-2)  6.9 us
    slice x11, local copies, waits for them, and re-layouts, with_halo(): block[..., row_part[dlat], col_part[dlon]]  6.8 us
    dot_general x1, matrix products, coupled_step(): jnp.einsum('fsb,sbc->sfc', chosen, remap_weights[0], preferred_element_ty...  6.46 us
  transfers between devices with their start and end apart: 10, of which 1 were waited for; matrix products, arithmetic and copies ran while one was open for 44% of the time, Pallas kernels for 0%

profile of v3, /device:TPU:0, one launch (start us, length us, event | category | flops | bytes accessed | tf_op | source)
XLA Modules:
  0.0 121.7 jit_solution(3975276642583939792)
XLA Ops:
  0.5 1.3 %reduce.6 = s32[256]{0:T(256)S(1)} reduce(s32[1,256]{1,0:T(1,128)} %param.13, s32[]{:T(128)} %broadcast.164), dimensions={0}, to_apply=%param.13.reduce_sub_computation.3 | reduce | bytes 2052 | tf_op args[3]
  3.5 11.7 %all-to-all-start = ((f32[128,1,2]{2,1,0:T(1,128)}), f32[128,1,2]{2,1,0:T(1,128)}, u32[]{:S(2)}, u32[]{:S(2)}) async-start(f32[128,1,2]{2,1,0:T(1,128)} %copy.87), calls=%async_computation | async-start | bytes 131072 | tf_op jit(solution)/shard_map/all_to_all | solution.py:95
  15.9 1.3 %pad_maximum_fusion = f32[129,16,128]{2,1,0:T(8,128)S(1)} fusion(f32[1,16,128]{2,1,0:T(8,128)S(1)} %get-tuple-element.14, f32[16,16,128]{2,1,0:T(8,128)} %param.17, f32[16,16,128]{2,1,0:T(8,128)} %param.16, f32[96,16,128]{2,1,0:T(8,128)} %bitcast.42), kind=kLoop, calls=%fused_computation.30 | loop fusion | flops 792576 | bytes 2113536 | tf_op jit(solution)/shard_map/concatenate | solution.py:105
  18.1 1.3 %collective-permute-start.6 = (f32[129,4,128]{2,0,1:T(8,128)}, f32[129,4,128]{2,0,1:T(8,128)}, u32[]{:S(2)}, u32[]{:S(2)}) collective-permute-start(f32[129,4,128]{2,0,1:T(8,128)} %copy.81), channel_id=1, source_target_pairs={{32,0},{33,1},{34,2},{35,3},{36,4},{37,5},{38,6},{39,7},{40,8},{41... | collective-permute-start | bytes 792584 | tf_op jit(solution)/shard_map/ppermute | solution.py:34
  20.1 3.8 %collective-permute-start.1 = (f32[129,4,128]{2,0,1:T(8,128)}, f32[129,4,128]{2,0,1:T(8,128)}, u32[]{:S(2)}, u32[]{:S(2)}) collective-permute-start(f32[129,4,128]{2,0,1:T(8,128)} %copy.71), channel_id=1, source_target_pairs={{0,32},{1,33},{2,34},{3,35},{4,36},{5,37},{6,38},{7,39},{8,40},{9,... | collective-permute-start | bytes 792584 | tf_op jit(solution)/shard_map/ppermute | solution.py:34
  25.0 9.7 %collective-permute-start.2 = (f32[129,4,4]{0,2,1:T(4,128)}, f32[129,4,4]{0,2,1:T(4,128)}, u32[]{:S(2)}, u32[]{:S(2)}) collective-permute-start(f32[129,4,4]{0,2,1:T(4,128)} %copy.72), channel_id=1, source_target_pairs={{0,63},{1,32},{2,33},{3,34},{4,35},{5,36},{6,37},{7,38},{8,39},{9,... | collective-permute-start | bytes 24776 | tf_op jit(solution)/shard_map/ppermute | solution.py:34
  34.7 0.8 copy.80
  35.5 1.3 %collective-permute-start.5 = (f32[129,4,4]{0,2,1:T(4,128)}, f32[129,4,4]{0,2,1:T(4,128)}, u32[]{:S(2)}, u32[]{:S(2)}) collective-permute-start(f32[129,4,4]{0,2,1:T(4,128)} %copy.80), channel_id=1, source_target_pairs={{32,1},{33,2},{34,3},{35,4},{36,5},{37,6},{38,7},{39,8},{40,9},{41... | collective-permute-start | bytes 24776 | tf_op jit(solution)/shard_map/ppermute | solution.py:34
  37.6 1.9 %collective-permute-start = (f32[129,4,4]{0,2,1:T(4,128)}, f32[129,4,4]{0,2,1:T(4,128)}, u32[]{:S(2)}, u32[]{:S(2)}) collective-permute-start(f32[129,4,4]{0,2,1:T(4,128)} %copy.70), channel_id=1, source_target_pairs={{0,33},{1,34},{2,35},{3,36},{4,37},{5,38},{6,39},{7,40},{8,41},{9,... | collective-permute-start | bytes 24776 | tf_op jit(solution)/shard_map/ppermute | solution.py:34
  43.5 1.0 gather_fusion
  44.6 1.3 %collective-permute-start.7 = (f32[129,4,4]{0,2,1:T(4,128)S(1)}, f32[129,4,4]{0,2,1:T(4,128)S(1)}, u32[]{:S(2)}, u32[]{:S(2)}) collective-permute-start(f32[129,4,4]{0,2,1:T(4,128)S(1)} %copy-done.5), channel_id=1, source_target_pairs={{32,31},{33,0},{34,1},{35,2},{36,3},{37,4},{38,5},{39,6},{40,7},{4... | collective-permute-start | bytes 24776 | tf_op jit(solution)/shard_map/ppermute | solution.py:34
  45.9 6.7 %collective-permute-start.4 = (f32[129,16,4]{0,1,2:T(8,128)S(1)}, f32[129,16,4]{0,1,2:T(8,128)}, u32[]{:S(2)}, u32[]{:S(2)}) collective-permute-start(f32[129,16,4]{0,1,2:T(8,128)S(1)} %copy.77), channel_id=1, source_target_pairs={{0,31},{1,0},{2,1},{3,2},{4,3},{5,4},{6,5},{7,6},{8,7},{9,8},{10,9... | collective-permute-start | bytes 99080 | tf_op jit(solution)/shard_map/ppermute | solution.py:34
  52.6 6.5 %broadcast_select_fusion = f32[256,24,128]{2,1,0:T(8,128)} fusion(bf16[1,256,128,128]{3,2,1,0:T(8,128)(2,1)} %param.11, bf16[256,24,128]{2,1,0:T(8,128)(2,1)S(1)} %gather_fusion, pred[256]{0:T(512)(128)(4,1)S(1)} %copy-done.8, pred[256]{0:T(512)(128)(4,1)S(1)} %copy-done.9), kind=kOutput, calls=%fused_computation.28 | convolution fusion | flops 202899456 | bytes 13107712 | tf_op jit(solution)/shard_map/fsb,sbc->sfc/dot_general | solution.py:86
  59.1 14.2 %all-to-all-start.1 = ((f32[128,48,128]{2,1,0:T(8,128)}), f32[128,48,128]{2,1,0:T(8,128)}, u32[]{:S(2)}, u32[]{:S(2)}) async-start(f32[128,48,128]{2,1,0:T(8,128)} %bitcast.12), calls=%async_computation.1 | async-start | bytes 6291456 | tf_op jit(solution)/shard_map/all_to_all | solution.py:94
  73.7 1.6 %reduce.7 = f32[128,2]{1,0:T(8,128)S(1)} reduce(f32[128,1,2]{2,1,0:T(1,128)} %all-to-all-done, f32[]{:T(128)} %broadcast.165), dimensions={1}, to_apply=%all_to_all.7.reduce_sub_computation.3 | reduce | bytes 2052 | tf_op jit(solution)/shard_map/all_to_all | solution.py:95
  75.4 1.0 copy.73
  76.4 1.0 copy.75
  77.4 1.6 %copy.83 = f32[129,4,4]{2,1,0:T(4,128)} copy(f32[129,4,4]{0,2,1:T(4,128)} %collective-permute-done.5) | data formatting | bytes 16512 | tf_op jit(solution)/shard_map/ppermute | solution.py:34
  79.0 0.9 copy.85
  80.8 1.6 %copy.79 = f32[129,16,4]{2,1,0:T(8,128)S(1)} copy(f32[129,16,4]{0,1,2:T(8,128)} %collective-permute-done.4) | data formatting | bytes 66048 | tf_op jit(solution)/shard_map/ppermute | solution.py:34
  82.4 1.0 copy.84
  83.4 1.0 copy.74
  84.5 6.6 %maximum_maximum_fusion = f32[129,24,136]{2,1,0:T(8,128)S(1)} fusion(f32[129,4,4]{2,1,0:T(4,128)} %copy.85, f32[129,4,128]{2,1,0:T(4,128)S(1)} %copy.84, f32[129,4,4]{2,1,0:T(4,128)} %copy.83, f32[129,16,4]{2,1,0:T(8,128)S(1)} %copy.79, f32[1,16,128]{2,1,0:T(8,128)S(1)} %get-tuple-element.14, f32[16,16,128]{2,1,0:T(8,128)} %param.17, ...), kind=kLoop, calls=%fused_computation.3 | loop fusion | flops 4631616 | bytes 3368448 | tf_op jit(solution)/shard_map/concatenate | solution.py:42
  93.3 2.5 %slice_subtract_fusion.4 = f32[6,16,22,134]{3,2,1,0:T(8,128)S(1)} fusion(f32[6,16,23,136]{3,2,1,0:T(8,128)S(1)} %subtract_multiply_fusion.6, f32[6,16,24,135]{3,2,1,0:T(8,128)S(1)} %subtract_multiply_fusion.7, f32[6,16,24,136]{3,2,1,0:T(8,128)S(1)} %bitcast.41), kind=kLoop, calls=%fused_computation.14 | loop fusion | flops 1132032 | bytes 6792192 | tf_op jit(solution)/shard_map/sub | solution.py:58
  98.4 2.5 %slice_subtract_fusion.2 = f32[6,16,20,132]{3,2,1,0:T(8,128)S(1)} fusion(f32[6,16,21,134]{3,2,1,0:T(8,128)S(1)} %subtract_multiply_fusion.4, f32[6,16,22,133]{3,2,1,0:T(8,128)S(1)} %subtract_multiply_fusion.5, f32[6,16,22,134]{3,2,1,0:T(8,128)S(1)} %slice_subtract_fusion.4), kind=kLoop, calls=%fused_computation.10 | loop fusion | flops 1013760 | bytes 6082560 | tf_op jit(solution)/shard_map/sub | solution.py:58
  102.3 2.8 %slice_subtract_fusion = f32[6,16,18,130]{3,2,1,0:T(8,128)S(1)} fusion(f32[6,16,19,132]{3,2,1,0:T(8,128)S(1)} %subtract_multiply_fusion.2, f32[6,16,20,131]{3,2,1,0:T(8,128)S(1)} %subtract_multiply_fusion.3, f32[6,16,20,132]{3,2,1,0:T(8,128)S(1)} %slice_subtract_fusion.2), kind=kLoop, calls=%fused_computation.6 | loop fusion | flops 898560 | bytes 5391360 | tf_op jit(solution)/shard_map/sub | solution.py:58
  105.1 2.2 %subtract_multiply_fusion.1 = f32[6,16,18,129]{3,2,1,0:T(8,128)} fusion(f32[6,16,18,130]{3,2,1,0:T(8,128)S(1)} %slice_subtract_fusion, f32[16,18,129]{2,1,0:T(8,128)S(1)} %slice.398, f32[18,129]{1,0:T(8,128)S(1)} %slice_multiply_fusion.1), kind=kLoop, calls=%fused_computation.19 | loop fusion | flops 1560384 | bytes 2832840 | tf_op jit(solution)/shard_map/mul | solution.py:47
  107.3 2.2 %subtract_multiply_fusion = f32[6,16,17,130]{3,2,1,0:T(8,128)} fusion(f32[6,16,18,130]{3,2,1,0:T(8,128)S(1)} %slice_subtract_fusion, f32[16,17,130]{2,1,0:T(8,128)S(1)} %fusion.13, f32[17,130]{1,0:T(8,128)S(1)} %slice_multiply_fusion), kind=kLoop, calls=%fused_computation.18 | loop fusion | flops 1485120 | bytes 2696200 | tf_op jit(solution)/shard_map/mul | solution.py:52
  109.5 3.7 %all-to-all-done.1 = f32[128,48,128]{2,1,0:T(8,128)} async-done(((f32[128,48,128]{2,1,0:T(8,128)}), f32[128,48,128]{2,1,0:T(8,128)}, u32[]{:S(2)}, u32[]{:S(2)}) %all-to-all-start.1) | async-done | bytes 3145760 | tf_op jit(solution)/shard_map/all_to_all | solution.py:94
  113.1 3.4 %fusion.2 = f32[16,24,128]{2,0,1:T(8,128)S(1)} fusion(f32[256,24,128]{2,1,0:T(8,128)} %bitcast.13, f32[256]{0:T(256)S(1)} %eq.17), kind=kOutput, calls=%fused_computation.4 | convolution fusion | flops 150999040 | bytes 3343360 | tf_op jit(solution)/shard_map/rk,kfc->rfc/dot_general | solution.py:135
  116.5 0.8 fusion.14
  117.3 4.4 %fusion.11 = f32[6,16,16,128]{3,2,1,0:T(8,128)} fusion(f32[6,16,17,130]{3,2,1,0:T(8,128)} %subtract_multiply_fusion, f32[6,16,18,129]{3,2,1,0:T(8,128)S(1)} %copy-done.2, f32[6,16,18,130]{3,2,1,0:T(8,128)S(1)} %slice_subtract_fusion, f32[6,16,16,128]{3,1,0,2:T(8,128)S(1)} %bitcast.45, f32[16,128]{1,0:T(8,128)S(1)} %get-tuple-element.13), kind=kLoop, calls=%fused_computation.32 | loop fusion | flops 1179648 | bytes 5513216 | tf_op jit(solution)/shard_map/add | solution.py:142
  (79 shorter events, 17.9 us)
Async XLA Ops:
  0.0 40.8 %copy-start = (bf16[24,2048]{1,0:T(8,128)(2,1)S(1)}, bf16[24,2048]{1,0:T(8,128)(2,1)}, u32[]{:S(2)}) copy-start(bf16[24,2048]{1,0:T(8,128)(2,1)} %param.10) | copy-start | bytes 294916
  3.5 55.6 %all-to-all-start = ((f32[128,1,2]{2,1,0:T(1,128)}), f32[128,1,2]{2,1,0:T(1,128)}, u32[]{:S(2)}, u32[]{:S(2)}) async-start(f32[128,1,2]{2,1,0:T(1,128)} %copy.87), calls=%async_computation | async-start | bytes 131072 | tf_op jit(solution)/shard_map/all_to_all | solution.py:95
  18.1 64.3 %collective-permute-start.6 = (f32[129,4,128]{2,0,1:T(8,128)}, f32[129,4,128]{2,0,1:T(8,128)}, u32[]{:S(2)}, u32[]{:S(2)}) collective-permute-start(f32[129,4,128]{2,0,1:T(8,128)} %copy.81), channel_id=1, source_target_pairs={{32,0},{33,1},{34,2},{35,3},{36,4},{37,5},{38,6},{39,7},{40,8},{41... | collective-permute-start | bytes 792584 | tf_op jit(solution)/shard_map/ppermute | solution.py:34
  20.1 63.3 %collective-permute-start.1 = (f32[129,4,128]{2,0,1:T(8,128)}, f32[129,4,128]{2,0,1:T(8,128)}, u32[]{:S(2)}, u32[]{:S(2)}) collective-permute-start(f32[129,4,128]{2,0,1:T(8,128)} %copy.71), channel_id=1, source_target_pairs={{0,32},{1,33},{2,34},{3,35},{4,36},{5,37},{6,38},{7,39},{8,40},{9,... | collective-permute-start | bytes 792584 | tf_op jit(solution)/shard_map/ppermute | solution.py:34
  25.0 19.5 %collective-permute-start.2 = (f32[129,4,4]{0,2,1:T(4,128)}, f32[129,4,4]{0,2,1:T(4,128)}, u32[]{:S(2)}, u32[]{:S(2)}) collective-permute-start(f32[129,4,4]{0,2,1:T(4,128)} %copy.72), channel_id=1, source_target_pairs={{0,63},{1,32},{2,33},{3,34},{4,35},{5,36},{6,37},{7,38},{8,39},{9,... | collective-permute-start | bytes 24776 | tf_op jit(solution)/shard_map/ppermute | solution.py:34
  34.7 5.1 %copy-start.7 = (s32[1,256]{1,0:T(1,128)S(1)}, s32[1,256]{1,0:T(1,128)}, u32[]{:S(2)}) copy-start(s32[1,256]{1,0:T(1,128)} %param.12) | copy-start | bytes 3076
  35.5 10.3 %collective-permute-start.5 = (f32[129,4,4]{0,2,1:T(4,128)}, f32[129,4,4]{0,2,1:T(4,128)}, u32[]{:S(2)}, u32[]{:S(2)}) collective-permute-start(f32[129,4,4]{0,2,1:T(4,128)} %copy.80), channel_id=1, source_target_pairs={{32,1},{33,2},{34,3},{35,4},{36,5},{37,6},{38,7},{39,8},{40,9},{41... | collective-permute-start | bytes 24776 | tf_op jit(solution)/shard_map/ppermute | solution.py:34
  37.6 14.9 %collective-permute-start = (f32[129,4,4]{0,2,1:T(4,128)}, f32[129,4,4]{0,2,1:T(4,128)}, u32[]{:S(2)}, u32[]{:S(2)}) collective-permute-start(f32[129,4,4]{0,2,1:T(4,128)} %copy.70), channel_id=1, source_target_pairs={{0,33},{1,34},{2,35},{3,36},{4,37},{5,38},{6,39},{7,40},{8,41},{9,... | collective-permute-start | bytes 24776 | tf_op jit(solution)/shard_map/ppermute | solution.py:34
  42.8 1.7 %copy-start.5 = (f32[129,4,4]{0,2,1:T(4,128)S(1)}, f32[129,4,4]{0,2,1:T(4,128)}, u32[]{:S(2)}) copy-start(f32[129,4,4]{0,2,1:T(4,128)} %copy.82) | copy-start | bytes 24772
  42.9 9.7 %copy-start.8 = (pred[256]{0:T(512)(128)(4,1)S(1)}, pred[256]{0:T(512)(128)(4,1)}, u32[]{:S(2)}) copy-start(pred[256]{0:T(512)(128)(4,1)} %get-tuple-element.15) | copy-start | bytes 772
  42.9 9.7 %copy-start.9 = (pred[256]{0:T(512)(128)(4,1)S(1)}, pred[256]{0:T(512)(128)(4,1)}, u32[]{:S(2)}) copy-start(pred[256]{0:T(512)(128)(4,1)} %get-tuple-element.16) | copy-start | bytes 772
  44.6 34.4 %collective-permute-start.7 = (f32[129,4,4]{0,2,1:T(4,128)S(1)}, f32[129,4,4]{0,2,1:T(4,128)S(1)}, u32[]{:S(2)}, u32[]{:S(2)}) collective-permute-start(f32[129,4,4]{0,2,1:T(4,128)S(1)} %copy-done.5), channel_id=1, source_target_pairs={{32,31},{33,0},{34,1},{35,2},{36,3},{37,4},{38,5},{39,6},{40,7},{4... | collective-permute-start | bytes 24776 | tf_op jit(solution)/shard_map/ppermute | solution.py:34
  45.9 34.9 %collective-permute-start.4 = (f32[129,16,4]{0,1,2:T(8,128)S(1)}, f32[129,16,4]{0,1,2:T(8,128)}, u32[]{:S(2)}, u32[]{:S(2)}) collective-permute-start(f32[129,16,4]{0,1,2:T(8,128)S(1)} %copy.77), channel_id=1, source_target_pairs={{0,31},{1,0},{2,1},{3,2},{4,3},{5,4},{6,5},{7,6},{8,7},{9,8},{10,9... | collective-permute-start | bytes 99080 | tf_op jit(solution)/shard_map/ppermute | solution.py:34
  52.6 27.4 %collective-permute-start.3 = (f32[129,16,4]{0,1,2:T(8,128)S(1)}, f32[129,16,4]{0,1,2:T(8,128)S(1)}, u32[]{:S(2)}, u32[]{:S(2)}) collective-permute-start(f32[129,16,4]{0,1,2:T(8,128)S(1)} %copy.76), channel_id=1, source_target_pairs={{0,1},{1,2},{2,3},{3,4},{4,5},{5,6},{6,7},{7,8},{8,9},{9,10},{10,1... | collective-permute-start | bytes 99080 | tf_op jit(solution)/shard_map/ppermute | solution.py:34
  59.1 54.1 %all-to-all-start.1 = ((f32[128,48,128]{2,1,0:T(8,128)}), f32[128,48,128]{2,1,0:T(8,128)}, u32[]{:S(2)}, u32[]{:S(2)}) async-start(f32[128,48,128]{2,1,0:T(8,128)} %bitcast.12), calls=%async_computation.1 | async-start | bytes 6291456 | tf_op jit(solution)/shard_map/all_to_all | solution.py:94
  73.2 11.2 %copy-start.1 = (f32[6,16,16,128]{3,2,1,0:T(8,128)S(1)}, f32[6,16,16,128]{3,2,1,0:T(8,128)}, u32[]{:S(2)}) copy-start(f32[6,16,16,128]{3,2,1,0:T(8,128)} %param.15) | copy-start | bytes 2359300
  93.2 2.5 %copy-start.3 = (f32[16,16,128]{2,1,0:T(8,128)S(1)}, f32[16,16,128]{2,1,0:T(8,128)}, u32[]{:S(2)}) copy-start(f32[16,16,128]{2,1,0:T(8,128)} %param.17) | copy-start | bytes 393220
  93.3 2.5 %copy-start.4 = (f32[16,16,128]{2,1,0:T(8,128)S(1)}, f32[16,16,128]{2,1,0:T(8,128)}, u32[]{:S(2)}) copy-start(f32[16,16,128]{2,1,0:T(8,128)} %param.16) | copy-start | bytes 393220
  109.4 7.1 %copy-start.6 = (f32[96,24]{0,1:T(8,128)S(1)}, f32[96,24]{0,1:T(8,128)}, u32[]{:S(2)}) copy-start(f32[96,24]{0,1:T(8,128)} %param.19) | copy-start | bytes 27652
  113.1 4.2 %copy-start.2 = (f32[6,16,18,129]{3,2,1,0:T(8,128)S(1)}, f32[6,16,18,129]{3,2,1,0:T(8,128)}, u32[]{:S(2)}) copy-start(f32[6,16,18,129]{3,2,1,0:T(8,128)} %subtract_multiply_fusion.1) | copy-start | bytes 2674948

commit v4 on v0

--- a/solution.py
+++ b/solution.py
@@ -2,6 +2,7 @@
 import jax.numpy as jnp
 from jax import lax
 from jax.sharding import PartitionSpec as P
+
 
 NSUB = 4
 
@@ -52,7 +53,7 @@
     )
 
 
-def per_device(
+def coupled_step(
     atm_fluxes,
     remap_weights,
     source_block,
@@ -79,13 +80,8 @@
     is_live = slot_ids % slot_count < jnp.repeat(block_count[0], slot_count)
     partials = jnp.where(is_live[:, None, None], partials, jnp.float32(0.0))
     targets = jnp.where(is_live, target_block[0], -1).astype(jnp.float32)
-    arrived = lax.all_to_all(
-        partials.reshape(tile_count, slot_count * field_count, block_cells),
-        ("lat", "lon"),
-        split_axis=0,
-        concat_axis=0,
-        tiled=True,
-    )
+    sent = partials.reshape(tile_count, slot_count * field_count, block_cells)
+    arrived = lax.all_to_all(sent, ("lat", "lon"), split_axis=0, concat_axis=0, tiled=True)
     landed = lax.all_to_all(
         targets.reshape(tile_count, slot_count),
         ("lat", "lon"),
@@ -150,7 +146,7 @@
         P(),
     )
     return jax.shard_map(
-        per_device,
+        coupled_step,
         mesh=mesh,
         in_specs=placed,
         out_specs=P(None, None, "lat", "lon"),

time: 110 us -> 110 us (level)
  no operation moved by 1% of the time
where the time goes in v4:
time: 110 us; the launch traced here: 109 us
  other arithmetic  36.7 us (33%)
  starting transfers between devices  28.4 us (26%)
  local copies, waits for them, and re-layouts  16.1 us (15%)
  waiting for transfers between devices  15 us (14%)
  matrix products  12.1 us (11%)
    all_to_all x1, starting transfers between devices, coupled_step(): lax.all_to_all(targets.reshape(tile_count, slot_count), ('lat', 'lon'), s...  11.7 us
    all_to_all x1, waiting for transfers between devices, coupled_step(): lax.all_to_all(sent, ('lat', 'lon'), split_axis=0, concat_axis=0, tiled=T...  9.48 us
    dot_general x1, matrix products, coupled_step(): jnp.einsum('fsb,sbc->sfc', chosen, remap_weights[0], preferred_element_ty...  7.91 us
    sub x3, other arithmetic, advect(): inner + east_flow[..., 1:-1, :-1] - east_flow[..., 1:-1, 1:]  7.79 us
    all_to_all x1, starting transfers between devices, coupled_step(): lax.all_to_all(sent, ('lat', 'lon'), split_axis=0, concat_axis=0, tiled=T...  5.93 us
    ppermute x1, starting transfers between devices, with_halo(): lax.ppermute(block[..., :width], 'lon', shifted_pairs(lon_count, -1, True))  5.54 us
    ppermute x1, waiting for transfers between devices, with_halo(): lax.ppermute(block[..., -width:], 'lon', shifted_pairs(lon_count, 1, True))  5.53 us
    concatenate x2, other arithmetic, with_halo(): return jnp.concatenate([south, block, north], axis=-2)  5.37 us
  transfers between devices with their start and end apart: 6, of which 2 were waited for; matrix products, arithmetic and copies ran while one was open for 49% of the time, Pallas kernels for 0%

profile of v4, /device:TPU:0, one launch (start us, length us, event | category | flops | bytes accessed | tf_op | source)
XLA Modules:
  0.0 108.7 jit_solution(13778881531472629417)
XLA Ops:
  0.5 1.3 %reduce.6 = s32[256]{0:T(256)S(1)} reduce(s32[1,256]{1,0:T(1,128)} %param.13, s32[]{:T(128)} %broadcast.164), dimensions={0}, to_apply=%param.13.reduce_sub_computation.3 | reduce | bytes 2052 | tf_op args[3]
  2.8 0.7 copy.80
  3.5 11.7 %all-to-all-start = ((f32[128,1,2]{2,1,0:T(1,128)}), f32[128,1,2]{2,1,0:T(1,128)}, u32[]{:S(2)}, u32[]{:S(2)}) async-start(f32[128,1,2]{2,1,0:T(1,128)} %copy.80), calls=%async_computation | async-start | bytes 131072 | tf_op jit(solution)/shard_map/all_to_all | solution.py:85
  15.2 1.3 %fusion.25 = (f32[16,128]{1,0:T(8,128)}, f32[1,16,128]{2,1,0:T(8,128)S(1)}) fusion(s32[16,128]{1,0:T(8,128)} %param.18), kind=kLoop, calls=%fused_computation.82 | loop fusion | flops 2048 | bytes 24576 | tf_op jit(solution)/shard_map/convert_element_type | solution.py:93
  16.5 1.3 %pad_maximum_fusion.1 = f32[129,16,128]{2,1,0:T(8,128)S(1)} fusion(f32[1,16,128]{2,1,0:T(8,128)S(1)} %get-tuple-element.10, f32[16,16,128]{2,1,0:T(8,128)} %param.17, f32[16,16,128]{2,1,0:T(8,128)} %param.16, f32[96,16,128]{2,1,0:T(8,128)} %bitcast.42), kind=kLoop, calls=%fused_computation.30 | loop fusion | flops 792576 | bytes 2113536 | tf_op jit(solution)/shard_map/concatenate | solution.py:95
  18.9 5.5 %collective-permute-start.1 = (f32[129,16,4]{0,1,2:T(8,128)S(1)}, f32[129,16,4]{0,1,2:T(8,128)S(1)}, u32[]{:S(2)}, u32[]{:S(2)}) collective-permute-start(f32[129,16,4]{0,1,2:T(8,128)S(1)} %copy.71), channel_id=1, source_target_pairs={{0,31},{1,0},{2,1},{3,2},{4,3},{5,4},{6,5},{7,6},{8,7},{9,8},{10,9... | collective-permute-start | bytes 99080 | tf_op jit(solution)/shard_map/ppermute | solution.py:28
  26.1 2.0 %gather_fusion = bf16[256,24,128]{2,1,0:T(8,128)(2,1)} fusion(bf16[24,16,128]{2,0,1:T(8,128)(2,1)S(1)} %copy_bitcast_fusion, s32[1024]{0:T(1024)S(1)} %pad_clamp_fusion), kind=kCustom, calls=%fused_computation | custom fusion | bytes 3146752 | tf_op jit(solution)/shard_map/jit(_take)/gather | solution.py:75
  28.1 5.5 %collective-permute-done = f32[129,16,4]{0,1,2:T(8,128)S(1)} collective-permute-done((f32[129,16,4]{0,1,2:T(8,128)S(1)}, f32[129,16,4]{0,1,2:T(8,128)S(1)}, u32[]{:S(2)}, u32[]{:S(2)}) %collective-permute-start) | collective-permute-done | bytes 33056 | tf_op jit(solution)/shard_map/ppermute | solution.py:27
  33.7 0.8 copy.72
  34.5 0.8 copy.73
  35.3 2.6 %pad_maximum_fusion.7 = (f32[129,4,136]{2,1,0:T(4,128)}, f32[129,4,136]{2,1,0:T(4,128)S(1)}) fusion(f32[129,16,4]{2,1,0:T(8,128)S(1)} %copy.73, f32[129,16,4]{2,1,0:T(8,128)S(1)} %copy.72, f32[1,16,128]{2,1,0:T(8,128)S(1)} %get-tuple-element.10, f32[16,16,128]{2,1,0:T(8,128)} %param.17, f32[16,16,128]{2,1,0:T(8,128)} %param.16, f32[96,16,128]{2,1,0:T(8,128)S(1)} %bitcast.43), kind=kLoop, calls=%fused_computation.43 | loop fusion | flops 701760 | bytes 1684224 | tf_op jit(solution)/shard_map/slice | solution.py:30
  37.9 2.2 %copy.74 = f32[129,4,136]{0,2,1:T(8,128)} copy(f32[129,4,136]{2,1,0:T(4,128)} %get-tuple-element.5) | data formatting | bytes 561408 | tf_op jit(solution)/shard_map/slice | solution.py:30
  40.1 1.1 %copy.75 = f32[129,4,136]{0,2,1:T(8,128)} copy(f32[129,4,136]{2,1,0:T(4,128)S(1)} %get-tuple-element.6) | data formatting | bytes 561408 | tf_op jit(solution)/shard_map/slice | solution.py:31
  41.2 1.3 %collective-permute-start.3 = (f32[129,4,136]{0,2,1:T(8,128)}, f32[129,4,136]{0,2,1:T(8,128)S(1)}, u32[]{:S(2)}, u32[]{:S(2)}) collective-permute-start(f32[129,4,136]{0,2,1:T(8,128)} %copy.75), channel_id=1, source_target_pairs={{32,0},{64,32},{96,64},{33,1},{65,33},{97,65},{34,2},{66,34},{98,6... | collective-permute-start | bytes 842120 | tf_op jit(solution)/shard_map/ppermute | solution.py:31
  42.5 3.8 %collective-permute-start.2 = (f32[129,4,136]{0,2,1:T(8,128)}, f32[129,4,136]{0,2,1:T(8,128)}, u32[]{:S(2)}, u32[]{:S(2)}) collective-permute-start(f32[129,4,136]{0,2,1:T(8,128)} %copy.74), channel_id=1, source_target_pairs={{0,32},{32,64},{64,96},{1,33},{33,65},{65,97},{2,34},{34,66},{66,9... | collective-permute-start | bytes 842120 | tf_op jit(solution)/shard_map/ppermute | solution.py:30
  46.3 7.9 %broadcast_select_fusion = f32[256,24,128]{2,1,0:T(8,128)} fusion(bf16[1,256,128,128]{3,2,1,0:T(8,128)(2,1)} %param.11, bf16[256,24,128]{2,1,0:T(8,128)(2,1)} %gather_fusion, pred[256]{0:T(512)(128)(4,1)} %get-tuple-element.11, pred[256]{0:T(512)(128)(4,1)} %get-tuple-element.12), kind=kOutput, calls=%fused_computation.28 | convolution fusion | flops 202899456 | bytes 13107712 | tf_op jit(solution)/shard_map/fsb,sbc->sfc/dot_general | solution.py:76
  54.3 5.9 %all-to-all-start.1 = ((f32[128,48,128]{2,1,0:T(8,128)}), f32[128,48,128]{2,1,0:T(8,128)}, u32[]{:S(2)}, u32[]{:S(2)}) async-start(f32[128,48,128]{2,1,0:T(8,128)} %bitcast.46), calls=%async_computation.1 | async-start | bytes 6291456 | tf_op jit(solution)/shard_map/all_to_all | solution.py:84
  60.8 2.2 %reduce.7 = f32[128,2]{1,0:T(8,128)} reduce(f32[128,1,2]{2,1,0:T(1,128)} %all-to-all-done, f32[]{:T(128)} %broadcast.165), dimensions={1}, to_apply=%all_to_all.7.reduce_sub_computation.3 | reduce | bytes 2052 | tf_op jit(solution)/shard_map/all_to_all | solution.py:85
  63.0 1.6 %eq.17 = f32[256]{0:T(256)} reshape(f32[128,2]{1,0:T(8,128)} %reduce.7) | data formatting | bytes 2048 | tf_op jit(solution)/shard_map/eq | solution.py:122
  64.6 1.1 %copy.77 = f32[129,4,136]{2,1,0:T(4,128)} copy(f32[129,4,136]{0,2,1:T(8,128)S(1)} %collective-permute-done.3) | data formatting | bytes 561408 | tf_op jit(solution)/shard_map/ppermute | solution.py:31
  65.7 1.4 %copy.76 = f32[129,4,136]{2,1,0:T(4,128)S(1)} copy(f32[129,4,136]{0,2,1:T(8,128)} %collective-permute-done.2) | data formatting | bytes 561408 | tf_op jit(solution)/shard_map/ppermute | solution.py:30
  67.1 5.1 %pad_maximum_fusion = f32[129,24,136]{2,1,0:T(8,128)S(1)} fusion(f32[129,4,136]{2,1,0:T(4,128)} %copy.77, f32[129,16,4]{2,1,0:T(8,128)S(1)} %copy.73, f32[1,16,128]{2,1,0:T(8,128)} %copy-done.5, f32[16,16,128]{2,1,0:T(8,128)} %param.17, f32[16,16,128]{2,1,0:T(8,128)} %param.16, f32[96,16,128]{2,1,0:T(8,128)S(1)} %bitcast.44, f32[129,16,4]{2,1,0:T(8,128)S(1)} %copy.72, ...), kind=kLoop, calls=%fused_computation.3 | loop fusion | flops 2947392 | bytes 3368448 | tf_op jit(solution)/shard_map/concatenate | solution.py:32
  74.4 2.5 %slice_subtract_fusion.4 = f32[6,16,22,134]{3,2,1,0:T(8,128)S(1)} fusion(f32[6,16,23,136]{3,2,1,0:T(8,128)S(1)} %subtract_multiply_fusion.6, f32[6,16,24,135]{3,2,1,0:T(8,128)S(1)} %subtract_multiply_fusion.7, f32[6,16,24,136]{3,2,1,0:T(8,128)S(1)} %bitcast.41), kind=kLoop, calls=%fused_computation.14 | loop fusion | flops 1132032 | bytes 6792192 | tf_op jit(solution)/shard_map/sub | solution.py:48
  78.9 0.7 subtract_multiply_fusion.4
  79.6 2.5 %slice_subtract_fusion.2 = f32[6,16,20,132]{3,2,1,0:T(8,128)S(1)} fusion(f32[6,16,21,134]{3,2,1,0:T(8,128)S(1)} %subtract_multiply_fusion.4, f32[6,16,22,133]{3,2,1,0:T(8,128)S(1)} %subtract_multiply_fusion.5, f32[6,16,22,134]{3,2,1,0:T(8,128)S(1)} %slice_subtract_fusion.4), kind=kLoop, calls=%fused_computation.10 | loop fusion | flops 1013760 | bytes 6082560 | tf_op jit(solution)/shard_map/sub | solution.py:48
  83.5 2.7 %slice_subtract_fusion = f32[6,16,18,130]{3,2,1,0:T(8,128)S(1)} fusion(f32[6,16,19,132]{3,2,1,0:T(8,128)S(1)} %subtract_multiply_fusion.2, f32[6,16,20,131]{3,2,1,0:T(8,128)S(1)} %subtract_multiply_fusion.3, f32[6,16,20,132]{3,2,1,0:T(8,128)S(1)} %slice_subtract_fusion.2), kind=kLoop, calls=%fused_computation.6 | loop fusion | flops 898560 | bytes 5391360 | tf_op jit(solution)/shard_map/sub | solution.py:48
  86.3 2.2 %subtract_multiply_fusion.1 = f32[6,16,18,129]{3,2,1,0:T(8,128)} fusion(f32[6,16,18,130]{3,2,1,0:T(8,128)S(1)} %slice_subtract_fusion, f32[16,18,129]{2,1,0:T(8,128)S(1)} %slice.376, f32[18,129]{1,0:T(8,128)S(1)} %slice_multiply_fusion.1), kind=kLoop, calls=%fused_computation.19 | loop fusion | flops 1560384 | bytes 2832840 | tf_op jit(solution)/shard_map/mul | solution.py:37
  88.4 2.2 %subtract_multiply_fusion = f32[6,16,17,130]{3,2,1,0:T(8,128)} fusion(f32[6,16,18,130]{3,2,1,0:T(8,128)S(1)} %slice_subtract_fusion, f32[16,17,130]{2,1,0:T(8,128)S(1)} %pad_maximum_fusion.8, f32[17,130]{1,0:T(8,128)S(1)} %slice_multiply_fusion), kind=kLoop, calls=%fused_computation.18 | loop fusion | flops 1485120 | bytes 2696200 | tf_op jit(solution)/shard_map/mul | solution.py:42
  90.6 9.5 %all-to-all-done.1 = f32[128,48,128]{2,1,0:T(8,128)} async-done(((f32[128,48,128]{2,1,0:T(8,128)}), f32[128,48,128]{2,1,0:T(8,128)}, u32[]{:S(2)}, u32[]{:S(2)}) %all-to-all-start.1) | async-done | bytes 3145760 | tf_op jit(solution)/shard_map/all_to_all | solution.py:84
  100.1 3.4 %fusion.2 = f32[16,24,128]{2,0,1:T(8,128)S(1)} fusion(f32[256,24,128]{2,1,0:T(8,128)} %bitcast.13, f32[256]{0:T(256)S(1)} %copy-done.9), kind=kOutput, calls=%fused_computation.4 | convolution fusion | flops 150999040 | bytes 3343360 | tf_op jit(solution)/shard_map/rk,kfc->rfc/dot_general | solution.py:125
  103.5 0.8 fusion.13
  104.3 4.4 %fusion.11 = f32[6,16,16,128]{3,2,1,0:T(8,128)} fusion(f32[6,16,17,130]{3,2,1,0:T(8,128)} %subtract_multiply_fusion, f32[6,16,18,129]{3,2,1,0:T(8,128)S(1)} %copy-done.2, f32[6,16,18,130]{3,2,1,0:T(8,128)S(1)} %slice_subtract_fusion, f32[6,16,16,128]{3,1,0,2:T(8,128)S(1)} %bitcast.47, f32[16,128]{1,0:T(8,128)S(1)} %copy-done.7), kind=kLoop, calls=%fused_computation.32 | loop fusion | flops 1179648 | bytes 5513216 | tf_op jit(solution)/shard_map/add | solution.py:132
  (66 shorter events, 10.0 us)
Async XLA Ops:
  0.0 25.5 %copy-start = (bf16[24,2048]{1,0:T(8,128)(2,1)S(1)}, bf16[24,2048]{1,0:T(8,128)(2,1)}, u32[]{:S(2)}) copy-start(bf16[24,2048]{1,0:T(8,128)(2,1)} %param.10) | copy-start | bytes 294916
  3.5 50.8 %all-to-all-start = ((f32[128,1,2]{2,1,0:T(1,128)}), f32[128,1,2]{2,1,0:T(1,128)}, u32[]{:S(2)}, u32[]{:S(2)}) async-start(f32[128,1,2]{2,1,0:T(1,128)} %copy.80), calls=%async_computation | async-start | bytes 131072 | tf_op jit(solution)/shard_map/all_to_all | solution.py:85
  16.5 18.8 %copy-start.5 = (f32[1,16,128]{2,1,0:T(8,128)}, f32[1,16,128]{2,1,0:T(8,128)S(1)}, u32[]{:S(2)}) copy-start(f32[1,16,128]{2,1,0:T(8,128)S(1)} %get-tuple-element.10) | copy-start | bytes 24580
  17.9 7.3 %copy-start.10 = (s32[1,256]{1,0:T(1,128)S(1)}, s32[1,256]{1,0:T(1,128)}, u32[]{:S(2)}) copy-start(s32[1,256]{1,0:T(1,128)} %param.12) | copy-start | bytes 3076
  17.9 7.3 %copy-start.11 = (s32[1,128]{1,0:T(1,128)S(1)}, s32[1,128]{1,0:T(1,128)}, u32[]{:S(2)}) copy-start(s32[1,128]{1,0:T(1,128)} %param.14) | copy-start | bytes 1540
  18.9 15.6 %collective-permute-start.1 = (f32[129,16,4]{0,1,2:T(8,128)S(1)}, f32[129,16,4]{0,1,2:T(8,128)S(1)}, u32[]{:S(2)}, u32[]{:S(2)}) collective-permute-start(f32[129,16,4]{0,1,2:T(8,128)S(1)} %copy.71), channel_id=1, source_target_pairs={{0,31},{1,0},{2,1},{3,2},{4,3},{5,4},{6,5},{7,6},{8,7},{9,8},{10,9... | collective-permute-start | bytes 99080 | tf_op jit(solution)/shard_map/ppermute | solution.py:28
  25.1 8.5 %collective-permute-start = (f32[129,16,4]{0,1,2:T(8,128)S(1)}, f32[129,16,4]{0,1,2:T(8,128)S(1)}, u32[]{:S(2)}, u32[]{:S(2)}) collective-permute-start(f32[129,16,4]{0,1,2:T(8,128)S(1)} %copy.70), channel_id=1, source_target_pairs={{0,1},{1,2},{2,3},{3,4},{4,5},{5,6},{6,7},{7,8},{8,9},{9,10},{10,1... | collective-permute-start | bytes 99080 | tf_op jit(solution)/shard_map/ppermute | solution.py:27
  26.1 9.2 %copy-start.1 = (f32[6,16,16,128]{3,2,1,0:T(8,128)S(1)}, f32[6,16,16,128]{3,2,1,0:T(8,128)}, u32[]{:S(2)}) copy-start(f32[6,16,16,128]{3,2,1,0:T(8,128)} %param.15) | copy-start | bytes 2359300
  41.2 23.4 %collective-permute-start.3 = (f32[129,4,136]{0,2,1:T(8,128)}, f32[129,4,136]{0,2,1:T(8,128)S(1)}, u32[]{:S(2)}, u32[]{:S(2)}) collective-permute-start(f32[129,4,136]{0,2,1:T(8,128)} %copy.75), channel_id=1, source_target_pairs={{32,0},{64,32},{96,64},{33,1},{65,33},{97,65},{34,2},{66,34},{98,6... | collective-permute-start | bytes 842120 | tf_op jit(solution)/shard_map/ppermute | solution.py:31
  42.5 23.2 %collective-permute-start.2 = (f32[129,4,136]{0,2,1:T(8,128)}, f32[129,4,136]{0,2,1:T(8,128)}, u32[]{:S(2)}, u32[]{:S(2)}) collective-permute-start(f32[129,4,136]{0,2,1:T(8,128)} %copy.74), channel_id=1, source_target_pairs={{0,32},{32,64},{64,96},{1,33},{33,65},{65,97},{2,34},{34,66},{66,9... | collective-permute-start | bytes 842120 | tf_op jit(solution)/shard_map/ppermute | solution.py:30
  54.3 45.8 %all-to-all-start.1 = ((f32[128,48,128]{2,1,0:T(8,128)}), f32[128,48,128]{2,1,0:T(8,128)}, u32[]{:S(2)}, u32[]{:S(2)}) async-start(f32[128,48,128]{2,1,0:T(8,128)} %bitcast.46), calls=%async_computation.1 | async-start | bytes 6291456 | tf_op jit(solution)/shard_map/all_to_all | solution.py:84
  74.4 2.6 %copy-start.3 = (f32[16,16,128]{2,1,0:T(8,128)S(1)}, f32[16,16,128]{2,1,0:T(8,128)}, u32[]{:S(2)}) copy-start(f32[16,16,128]{2,1,0:T(8,128)} %param.17) | copy-start | bytes 393220
  74.4 2.6 %copy-start.4 = (f32[16,16,128]{2,1,0:T(8,128)S(1)}, f32[16,16,128]{2,1,0:T(8,128)}, u32[]{:S(2)}) copy-start(f32[16,16,128]{2,1,0:T(8,128)} %param.16) | copy-start | bytes 393220
  74.4 2.6 %copy-start.6 = (f32[1,16,128]{2,1,0:T(8,128)S(1)}, f32[1,16,128]{2,1,0:T(8,128)}, u32[]{:S(2)}) copy-start(f32[1,16,128]{2,1,0:T(8,128)} %copy-done.5) | copy-start | bytes 24580
  88.4 11.7 %copy-start.9 = (f32[256]{0:T(256)S(1)}, f32[256]{0:T(256)}, u32[]{:S(2)}) copy-start(f32[256]{0:T(256)} %eq.17) | copy-start | bytes 3076
  90.6 12.9 %copy-start.8 = (f32[96,24]{0,1:T(8,128)S(1)}, f32[96,24]{0,1:T(8,128)}, u32[]{:S(2)}) copy-start(f32[96,24]{0,1:T(8,128)} %param.19) | copy-start | bytes 27652
  90.6 13.7 %copy-start.7 = (f32[16,128]{1,0:T(8,128)S(1)}, f32[16,128]{1,0:T(8,128)}, u32[]{:S(2)}) copy-start(f32[16,128]{1,0:T(8,128)} %get-tuple-element.9) | copy-start | bytes 24580
  100.1 4.2 %copy-start.2 = (f32[6,16,18,129]{3,2,1,0:T(8,128)S(1)}, f32[6,16,18,129]{3,2,1,0:T(8,128)}, u32[]{:S(2)}) copy-start(f32[6,16,18,129]{3,2,1,0:T(8,128)} %subtract_multiply_fusion.1) | copy-start | bytes 2674948

commit v5 on v4

--- a/solution.py
+++ b/solution.py
@@ -80,15 +80,21 @@
     is_live = slot_ids % slot_count < jnp.repeat(block_count[0], slot_count)
     partials = jnp.where(is_live[:, None, None], partials, jnp.float32(0.0))
     targets = jnp.where(is_live, target_block[0], -1).astype(jnp.float32)
-    sent = partials.reshape(tile_count, slot_count * field_count, block_cells)
+    rows_part = jnp.broadcast_to(
+        targets.reshape(tile_count, slot_count, 1), (tile_count, slot_count, block_cells)
+    )
+    pad_rows = jnp.zeros((tile_count, 8 - slot_count, block_cells), jnp.float32)
+    sent = jnp.concatenate(
+        [
+            partials.reshape(tile_count, slot_count * field_count, block_cells),
+            rows_part,
+            pad_rows,
+        ],
+        axis=1,
+    )
     arrived = lax.all_to_all(sent, ("lat", "lon"), split_axis=0, concat_axis=0, tiled=True)
-    landed = lax.all_to_all(
-        targets.reshape(tile_count, slot_count),
-        ("lat", "lon"),
-        split_axis=0,
-        concat_axis=0,
-        tiled=True,
-    )
+    landed = arrived[:, slot_count * field_count : slot_count * (field_count + 1), 0]
+    arrived = arrived[:, : slot_count * field_count]
 
     sea_here = land_mask.astype(jnp.float32)
     planes = tracer_count * level_count

time: 110 us -> 102 us (0.927)
  starting transfers between devices: 28.4 us -> 21.9 us
  waiting for transfers between devices: 15 us -> 19.3 us
  matrix products: 12.1 us -> 8.65 us
  other arithmetic: 36.7 us -> 34.3 us
    all_to_all x1 -> x0, starting transfers between devices: 11.7 us -> none  [coupled_step(): lax.all_to_all(targets.reshape(tile_count, slot_count), ('lat', 'lon'), s...]
    all_to_all x1, waiting for transfers between devices: 9.48 us -> 19.3 us  [coupled_step(): lax.all_to_all(sent, ('lat', 'lon'), split_axis=0, concat_axis=0, tiled=T...]
    ppermute x1, waiting for transfers between devices: 5.53 us -> 0.01 us  [with_halo(): lax.ppermute(block[..., -width:], 'lon', shifted_pairs(lon_count, 1, True))]
    all_to_all x1, starting transfers between devices: 5.93 us -> 9.97 us  [coupled_step(): lax.all_to_all(sent, ('lat', 'lon'), split_axis=0, concat_axis=0, tiled=T...]
    concatenate x0 -> x1, other arithmetic: none -> 3.99 us  [coupled_step(): jnp.concatenate([partials.reshape(tile_count, slot_count * field_count, b...]
    slice x0 -> x2, local copies, waits for them, and re-layouts: none -> 3.52 us  [the longest x1 2.26 us: coupled_step(): arrived = arrived[:, :slot_count * field_count]]
    add x1, other arithmetic: 4.38 us -> 1.99 us  [coupled_step(): return tracer_now + sea_here * source]
    all_to_all x1 -> x0, other arithmetic: 2.24 us -> none  [coupled_step(): lax.all_to_all(targets.reshape(tile_count, slot_count), ('lat', 'lon'), s...]
  transfers between devices with their start and end apart: 6 -> 5, of which waited for: 2 -> 1; matrix products, arithmetic and copies ran while one was open for 49% -> 40% of each run, Pallas kernels for 0% -> 0%
where the time goes in v5:
time: 102 us; the launch traced here: 101 us
  other arithmetic  34.3 us (34%)
  starting transfers between devices  21.9 us (21%)
  waiting for transfers between devices  19.3 us (19%)
  local copies, waits for them, and re-layouts  16.3 us (16%)
  matrix products  8.65 us (8%)
    all_to_all x1, waiting for transfers between devices, coupled_step(): lax.all_to_all(sent, ('lat', 'lon'), split_axis=0, concat_axis=0, tiled=T...  19.3 us
    all_to_all x1, starting transfers between devices, coupled_step(): lax.all_to_all(sent, ('lat', 'lon'), split_axis=0, concat_axis=0, tiled=T...  9.97 us
    sub x3, other arithmetic, advect(): inner + east_flow[..., 1:-1, :-1] - east_flow[..., 1:-1, 1:]  7.8 us
    ppermute x1, starting transfers between devices, with_halo(): lax.ppermute(block[..., :width], 'lon', shifted_pairs(lon_count, -1, True))  6.74 us
    dot_general x1, matrix products, coupled_step(): jnp.einsum('fsb,sbc->sfc', chosen, remap_weights[0], preferred_element_ty...  6.49 us
    concatenate x2, other arithmetic, with_halo(): return jnp.concatenate([south, block, north], axis=-2)  5.57 us
    mul x4, other arithmetic, advect(): mask_east * (east_speed[:, :, :-1] * (tracer_now[..., :-1] + tracer_now[....  4.24 us
    mul x4, other arithmetic, advect(): mask_north * (north_speed[:, :-1, :] * (tracer_now[..., :-1, :] + tracer_...  4.14 us
  transfers between devices with their start and end apart: 5, of which 1 were waited for; matrix products, arithmetic and copies ran while one was open for 40% of the time, Pallas kernels for 0%

profile of v5, /device:TPU:0, one launch (start us, length us, event | category | flops | bytes accessed | tf_op | source)
XLA Modules:
  0.0 101.0 jit_solution(4682605220688913763)
XLA Ops:
  0.0 1.3 %fusion.25 = (f32[16,128]{1,0:T(8,128)}, f32[1,16,128]{2,1,0:T(8,128)S(1)}) fusion(s32[16,128]{1,0:T(8,128)} %param.18), kind=kLoop, calls=%fused_computation.84 | loop fusion | flops 2048 | bytes 24576 | tf_op jit(solution)/shard_map/convert_element_type | solution.py:99
  1.3 1.3 %pad_maximum_fusion.1 = f32[129,16,128]{2,1,0:T(8,128)S(1)} fusion(f32[1,16,128]{2,1,0:T(8,128)S(1)} %get-tuple-element.10, f32[16,16,128]{2,1,0:T(8,128)} %param.17, f32[16,16,128]{2,1,0:T(8,128)} %param.16, f32[96,16,128]{2,1,0:T(8,128)} %bitcast.43), kind=kLoop, calls=%fused_computation.31 | loop fusion | flops 792576 | bytes 2113536 | tf_op jit(solution)/shard_map/concatenate | solution.py:101
  3.7 6.7 %collective-permute-start.1 = (f32[129,16,4]{0,1,2:T(8,128)S(1)}, f32[129,16,4]{0,1,2:T(8,128)S(1)}, u32[]{:S(2)}, u32[]{:S(2)}) collective-permute-start(f32[129,16,4]{0,1,2:T(8,128)S(1)} %copy.54), channel_id=1, source_target_pairs={{0,31},{1,0},{2,1},{3,2},{4,3},{5,4},{6,5},{7,6},{8,7},{9,8},{10,9... | collective-permute-start | bytes 99080 | tf_op jit(solution)/shard_map/ppermute | solution.py:28
  12.9 1.0 gather_fusion
  13.9 6.5 %broadcast_select_fusion = f32[256,24,128]{2,1,0:T(8,128)} fusion(bf16[1,256,128,128]{3,2,1,0:T(8,128)(2,1)} %param.11, bf16[256,24,128]{2,1,0:T(8,128)(2,1)S(1)} %gather_fusion, pred[256]{0:T(512)(128)(4,1)S(1)} %get-tuple-element.11, pred[256]{0:T(512)(128)(4,1)S(1)} %get-tuple-element.12), kind=kOutput, calls=%fused_computation.29 | convolution fusion | flops 202899456 | bytes 13107712 | tf_op jit(solution)/shard_map/fsb,sbc->sfc/dot_general | solution.py:76
  20.5 0.8 copy.55
  21.4 0.8 copy.56
  22.2 2.6 %pad_maximum_fusion.7 = (f32[129,4,136]{2,1,0:T(4,128)}, f32[129,4,136]{2,1,0:T(4,128)S(1)}) fusion(f32[129,16,4]{2,1,0:T(8,128)S(1)} %copy.56, f32[129,16,4]{2,1,0:T(8,128)S(1)} %copy.55, f32[1,16,128]{2,1,0:T(8,128)S(1)} %get-tuple-element.10, f32[16,16,128]{2,1,0:T(8,128)} %param.17, f32[16,16,128]{2,1,0:T(8,128)} %param.16, f32[96,16,128]{2,1,0:T(8,128)S(1)} %bitcast.44), kind=kLoop, calls=%fused_computation.44 | loop fusion | flops 701760 | bytes 1684224 | tf_op jit(solution)/shard_map/slice | solution.py:30
  24.8 2.2 %copy.57 = f32[129,4,136]{0,2,1:T(8,128)} copy(f32[129,4,136]{2,1,0:T(4,128)} %get-tuple-element.5) | data formatting | bytes 561408 | tf_op jit(solution)/shard_map/slice | solution.py:30
  27.0 1.1 %copy.58 = f32[129,4,136]{0,2,1:T(8,128)} copy(f32[129,4,136]{2,1,0:T(4,128)S(1)} %get-tuple-element.6) | data formatting | bytes 561408 | tf_op jit(solution)/shard_map/slice | solution.py:31
  28.1 1.3 %collective-permute-start.3 = (f32[129,4,136]{0,2,1:T(8,128)}, f32[129,4,136]{0,2,1:T(8,128)S(1)}, u32[]{:S(2)}, u32[]{:S(2)}) collective-permute-start(f32[129,4,136]{0,2,1:T(8,128)} %copy.58), channel_id=1, source_target_pairs={{32,0},{64,32},{96,64},{33,1},{65,33},{97,65},{34,2},{66,34},{98,6... | collective-permute-start | bytes 842120 | tf_op jit(solution)/shard_map/ppermute | solution.py:31
  29.4 3.9 %collective-permute-start.2 = (f32[129,4,136]{0,2,1:T(8,128)}, f32[129,4,136]{0,2,1:T(8,128)}, u32[]{:S(2)}, u32[]{:S(2)}) collective-permute-start(f32[129,4,136]{0,2,1:T(8,128)} %copy.57), channel_id=1, source_target_pairs={{0,32},{32,64},{64,96},{1,33},{33,65},{65,97},{2,34},{34,66},{66,9... | collective-permute-start | bytes 842120 | tf_op jit(solution)/shard_map/ppermute | solution.py:30
  33.5 4.0 %maximum_maximum_fusion = f32[128,56,128]{2,1,0:T(8,128)} fusion(f32[128,2,128]{2,1,0:T(2,128)S(1)} %broadcast_in_dim.66, f32[128,48,128]{2,1,0:T(8,128)} %bitcast.47, f32[56]{0:T(128)S(1)} %pad.2.clone), kind=kLoop, calls=%fused_computation.3 | loop fusion | flops 1835008 | bytes 6947040 | tf_op jit(solution)/shard_map/concatenate | solution.py:87
  37.5 10.0 %all-to-all-start = ((f32[128,56,128]{2,1,0:T(8,128)}), f32[128,56,128]{2,1,0:T(8,128)}, u32[]{:S(2)}, u32[]{:S(2)}) async-start(f32[128,56,128]{2,1,0:T(8,128)} %maximum_maximum_fusion), calls=%async_computation | async-start | bytes 7340032 | tf_op jit(solution)/shard_map/all_to_all | solution.py:95
  47.5 1.1 %copy.60 = f32[129,4,136]{2,1,0:T(4,128)} copy(f32[129,4,136]{0,2,1:T(8,128)S(1)} %collective-permute-done.3) | data formatting | bytes 561408 | tf_op jit(solution)/shard_map/ppermute | solution.py:31
  48.6 1.4 %copy.59 = f32[129,4,136]{2,1,0:T(4,128)S(1)} copy(f32[129,4,136]{0,2,1:T(8,128)} %collective-permute-done.2) | data formatting | bytes 561408 | tf_op jit(solution)/shard_map/ppermute | solution.py:30
  50.0 5.3 %pad_maximum_fusion = f32[129,24,136]{2,1,0:T(8,128)S(1)} fusion(f32[129,4,136]{2,1,0:T(4,128)} %copy.60, f32[129,16,4]{2,1,0:T(8,128)S(1)} %copy.56, f32[1,16,128]{2,1,0:T(8,128)S(1)} %copy-done.8, f32[16,16,128]{2,1,0:T(8,128)} %param.17, f32[16,16,128]{2,1,0:T(8,128)} %param.16, f32[96,16,128]{2,1,0:T(8,128)S(1)} %bitcast.45, f32[129,16,4]{2,1,0:T(8,128)S(1)} %copy.55, ...), kind=kLoop, calls=%fused_computation.4 | loop fusion | flops 2947392 | bytes 3368448 | tf_op jit(solution)/shard_map/concatenate | solution.py:32
  57.7 0.7 subtract_multiply_fusion.6
  58.9 2.5 %slice_subtract_fusion.4 = f32[6,16,22,134]{3,2,1,0:T(8,128)S(1)} fusion(f32[6,16,23,136]{3,2,1,0:T(8,128)S(1)} %subtract_multiply_fusion.6, f32[6,16,24,135]{3,2,1,0:T(8,128)S(1)} %subtract_multiply_fusion.7, f32[6,16,24,136]{3,2,1,0:T(8,128)S(1)} %bitcast.41), kind=kLoop, calls=%fused_computation.15 | loop fusion | flops 1132032 | bytes 6792192 | tf_op jit(solution)/shard_map/sub | solution.py:48
  61.5 0.7 subtract_multiply_fusion.5
  62.2 0.7 subtract_multiply_fusion.4
  62.9 2.5 %slice_subtract_fusion.2 = f32[6,16,20,132]{3,2,1,0:T(8,128)S(1)} fusion(f32[6,16,21,134]{3,2,1,0:T(8,128)S(1)} %subtract_multiply_fusion.4, f32[6,16,22,133]{3,2,1,0:T(8,128)S(1)} %subtract_multiply_fusion.5, f32[6,16,22,134]{3,2,1,0:T(8,128)S(1)} %slice_subtract_fusion.4), kind=kLoop, calls=%fused_computation.11 | loop fusion | flops 1013760 | bytes 6082560 | tf_op jit(solution)/shard_map/sub | solution.py:48
  66.1 0.7 subtract_multiply_fusion.2
  66.8 2.7 %slice_subtract_fusion = f32[6,16,18,130]{3,2,1,0:T(8,128)S(1)} fusion(f32[6,16,19,132]{3,2,1,0:T(8,128)S(1)} %subtract_multiply_fusion.2, f32[6,16,20,131]{3,2,1,0:T(8,128)S(1)} %subtract_multiply_fusion.3, f32[6,16,20,132]{3,2,1,0:T(8,128)S(1)} %slice_subtract_fusion.2), kind=kLoop, calls=%fused_computation.7 | loop fusion | flops 898560 | bytes 5391360 | tf_op jit(solution)/shard_map/sub | solution.py:48
  69.5 2.2 %subtract_multiply_fusion.1 = f32[6,16,18,129]{3,2,1,0:T(8,128)} fusion(f32[6,16,18,130]{3,2,1,0:T(8,128)S(1)} %slice_subtract_fusion, f32[16,18,129]{2,1,0:T(8,128)S(1)} %slice.384, f32[18,129]{1,0:T(8,128)S(1)} %slice_multiply_fusion.1), kind=kLoop, calls=%fused_computation.20 | loop fusion | flops 1560384 | bytes 2832840 | tf_op jit(solution)/shard_map/mul | solution.py:37
  71.7 2.1 %subtract_multiply_fusion = f32[6,16,17,130]{3,2,1,0:T(8,128)} fusion(f32[6,16,18,130]{3,2,1,0:T(8,128)S(1)} %slice_subtract_fusion, f32[16,17,130]{2,1,0:T(8,128)S(1)} %pad_maximum_fusion.8, f32[17,130]{1,0:T(8,128)S(1)} %slice_multiply_fusion), kind=kLoop, calls=%fused_computation.19 | loop fusion | flops 1485120 | bytes 2696200 | tf_op jit(solution)/shard_map/mul | solution.py:42
  73.8 19.3 %all-to-all-done = f32[128,56,128]{2,1,0:T(8,128)} async-done(((f32[128,56,128]{2,1,0:T(8,128)}), f32[128,56,128]{2,1,0:T(8,128)}, u32[]{:S(2)}, u32[]{:S(2)}) %all-to-all-start) | async-done | bytes 3670048 | tf_op jit(solution)/shard_map/all_to_all | solution.py:95
  93.0 1.3 %slice_reduce_fusion = f32[128,2]{1,0:T(8,128)S(1)} fusion(f32[128,56,128]{2,1,0:T(8,128)} %all-to-all-done), kind=kLoop, calls=%fused_computation.53 | loop fusion | bytes 2048 | tf_op jit(solution)/shard_map/slice | solution.py:96
  94.5 2.3 %slice.396 = f32[128,48,128]{2,1,0:T(8,128)S(1)} slice(f32[128,56,128]{2,1,0:T(8,128)} %all-to-all-done), slice={[0:128], [0:48], [0:128]} | slice | bytes 6291456 | tf_op jit(solution)/shard_map/slice | solution.py:97
  96.8 1.3 %fusion.2 = f32[16,24,128]{2,0,1:T(8,128)S(1)} fusion(f32[256,24,128]{2,1,0:T(8,128)S(1)} %bitcast.42, f32[256]{0:T(256)S(1)} %eq.17), kind=kOutput, calls=%fused_computation.5 | convolution fusion | flops 150999040 | bytes 3343360 | tf_op jit(solution)/shard_map/rk,kfc->rfc/dot_general | solution.py:131
  98.1 0.8 fusion.13
  99.0 2.0 %fusion.11 = f32[6,16,16,128]{3,2,1,0:T(8,128)} fusion(f32[6,16,17,130]{3,2,1,0:T(8,128)S(1)} %copy-done.4, f32[6,16,18,129]{3,2,1,0:T(8,128)S(1)} %copy-done.3, f32[6,16,18,130]{3,2,1,0:T(8,128)S(1)} %slice_subtract_fusion, f32[6,16,16,128]{3,1,0,2:T(8,128)S(1)} %bitcast.48, f32[16,128]{1,0:T(8,128)S(1)} %copy-done.9), kind=kLoop, calls=%fused_computation.33 | loop fusion | flops 1179648 | bytes 5513216 | tf_op jit(solution)/shard_map/add | solution.py:138
  (70 shorter events, 7.4 us)
Async XLA Ops:
  0.0 12.8 %copy-start = (bf16[24,2048]{1,0:T(8,128)(2,1)S(1)}, bf16[24,2048]{1,0:T(8,128)(2,1)}, u32[]{:S(2)}) copy-start(bf16[24,2048]{1,0:T(8,128)(2,1)} %param.10) | copy-start | bytes 294916
  1.3 20.8 %copy-start.7 = (f32[1,16,128]{2,1,0:T(8,128)}, f32[1,16,128]{2,1,0:T(8,128)S(1)}, u32[]{:S(2)}) copy-start(f32[1,16,128]{2,1,0:T(8,128)S(1)} %get-tuple-element.10) | copy-start | bytes 24580
  2.7 8.5 %copy-start.11 = (s32[1,256]{1,0:T(1,128)S(1)}, s32[1,256]{1,0:T(1,128)}, u32[]{:S(2)}) copy-start(s32[1,256]{1,0:T(1,128)} %param.12) | copy-start | bytes 3076
  2.7 9.1 %copy-start.13 = (s32[1,256]{1,0:T(1,128)S(1)}, s32[1,256]{1,0:T(1,128)}, u32[]{:S(2)}) copy-start(s32[1,256]{1,0:T(1,128)} %param.13) | copy-start | bytes 3076
  2.7 9.9 %copy-start.12 = (s32[1,128]{1,0:T(1,128)S(1)}, s32[1,128]{1,0:T(1,128)}, u32[]{:S(2)}) copy-start(s32[1,128]{1,0:T(1,128)} %param.14) | copy-start | bytes 1540
  3.7 17.6 %collective-permute-start.1 = (f32[129,16,4]{0,1,2:T(8,128)S(1)}, f32[129,16,4]{0,1,2:T(8,128)S(1)}, u32[]{:S(2)}, u32[]{:S(2)}) collective-permute-start(f32[129,16,4]{0,1,2:T(8,128)S(1)} %copy.54), channel_id=1, source_target_pairs={{0,31},{1,0},{2,1},{3,2},{4,3},{5,4},{6,5},{7,6},{8,7},{9,8},{10,9... | collective-permute-start | bytes 99080 | tf_op jit(solution)/shard_map/ppermute | solution.py:28
  11.2 9.4 %collective-permute-start = (f32[129,16,4]{0,1,2:T(8,128)S(1)}, f32[129,16,4]{0,1,2:T(8,128)S(1)}, u32[]{:S(2)}, u32[]{:S(2)}) collective-permute-start(f32[129,16,4]{0,1,2:T(8,128)S(1)} %copy.53), channel_id=1, source_target_pairs={{0,1},{1,2},{2,3},{3,4},{4,5},{5,6},{6,7},{7,8},{8,9},{9,10},{10,1... | collective-permute-start | bytes 99080 | tf_op jit(solution)/shard_map/ppermute | solution.py:27
  20.4 1.8 %copy-start.2 = (f32[6,16,16,128]{3,2,1,0:T(8,128)S(1)}, f32[6,16,16,128]{3,2,1,0:T(8,128)}, u32[]{:S(2)}) copy-start(f32[6,16,16,128]{3,2,1,0:T(8,128)} %param.15) | copy-start | bytes 2359300
  28.1 19.3 %collective-permute-start.3 = (f32[129,4,136]{0,2,1:T(8,128)}, f32[129,4,136]{0,2,1:T(8,128)S(1)}, u32[]{:S(2)}, u32[]{:S(2)}) collective-permute-start(f32[129,4,136]{0,2,1:T(8,128)} %copy.58), channel_id=1, source_target_pairs={{32,0},{64,32},{96,64},{33,1},{65,33},{97,65},{34,2},{66,34},{98,6... | collective-permute-start | bytes 842120 | tf_op jit(solution)/shard_map/ppermute | solution.py:31
  29.4 19.2 %collective-permute-start.2 = (f32[129,4,136]{0,2,1:T(8,128)}, f32[129,4,136]{0,2,1:T(8,128)}, u32[]{:S(2)}, u32[]{:S(2)}) collective-permute-start(f32[129,4,136]{0,2,1:T(8,128)} %copy.57), channel_id=1, source_target_pairs={{0,32},{32,64},{64,96},{1,33},{33,65},{65,97},{2,34},{34,66},{66,9... | collective-permute-start | bytes 842120 | tf_op jit(solution)/shard_map/ppermute | solution.py:30
  37.5 12.5 %copy-start.8 = (f32[1,16,128]{2,1,0:T(8,128)S(1)}, f32[1,16,128]{2,1,0:T(8,128)}, u32[]{:S(2)}) copy-start(f32[1,16,128]{2,1,0:T(8,128)} %copy-done.7) | copy-start | bytes 24580
  37.5 55.6 %all-to-all-start = ((f32[128,56,128]{2,1,0:T(8,128)}), f32[128,56,128]{2,1,0:T(8,128)}, u32[]{:S(2)}, u32[]{:S(2)}) async-start(f32[128,56,128]{2,1,0:T(8,128)} %maximum_maximum_fusion), calls=%async_computation | async-start | bytes 7340032 | tf_op jit(solution)/shard_map/all_to_all | solution.py:95
  57.7 0.9 copy-start.5
  57.7 1.0 copy-start.6
  94.4 4.5 %copy-start.4 = (f32[6,16,17,130]{3,2,1,0:T(8,128)S(1)}, f32[6,16,17,130]{3,2,1,0:T(8,128)}, u32[]{:S(2)}) copy-start(f32[6,16,17,130]{3,2,1,0:T(8,128)} %subtract_multiply_fusion) | copy-start | bytes 2545924
  96.7 1.4 %copy-start.10 = (f32[96,24]{0,1:T(8,128)S(1)}, f32[96,24]{0,1:T(8,128)}, u32[]{:S(2)}) copy-start(f32[96,24]{0,1:T(8,128)} %param.19) | copy-start | bytes 27652
  96.7 2.2 %copy-start.3 = (f32[6,16,18,129]{3,2,1,0:T(8,128)S(1)}, f32[6,16,18,129]{3,2,1,0:T(8,128)}, u32[]{:S(2)}) copy-start(f32[6,16,18,129]{3,2,1,0:T(8,128)} %subtract_multiply_fusion.1) | copy-start | bytes 2674948
  96.7 2.2 %copy-start.9 = (f32[16,128]{1,0:T(8,128)S(1)}, f32[16,128]{1,0:T(8,128)}, u32[]{:S(2)}) copy-start(f32[16,128]{1,0:T(8,128)} %get-tuple-element.9) | copy-start | bytes 24580
  98.9 2.0 %copy-start.1 = (bf16[24,2048]{1,0:T(8,128)(2,1)S(1)}, bf16[24,2048]{1,0:T(8,128)(2,1)}, u32[]{:S(2)}) copy-start(bf16[24,2048]{1,0:T(8,128)(2,1)} %param.10) | copy-start | bytes 294916

commit v6 on v4

--- a/solution.py
+++ b/solution.py
@@ -1,6 +1,8 @@
 import jax
 import jax.numpy as jnp
 from jax import lax
+from jax.experimental import pallas as pl
+from jax.experimental.pallas import tpu as pltpu
 from jax.sharding import PartitionSpec as P
 
 
@@ -30,6 +32,59 @@
     south = lax.ppermute(block[..., -width:, :], "lat", shifted_pairs(lat_count, 1, False))
     north = lax.ppermute(block[..., :width, :], "lat", shifted_pairs(lat_count, -1, False))
     return jnp.concatenate([south, block, north], axis=-2)
+
+
+TILES_PER_STEP = 16
+
+
+def remap_kernel(src_ref, tgt_ref, atm_ref, w_ref, out_ref):
+    step = pl.program_id(0)
+    tiles, _, cells = out_ref.shape
+    slots = w_ref.shape[0] // tiles
+    fields = atm_ref.shape[1]
+    blocks = atm_ref.shape[0]
+    row_ids = lax.broadcasted_iota(jnp.int32, (8, cells), 0)
+
+    def one_tile(i, carry):
+        tail = jnp.zeros((8, cells), jnp.float32)
+        for k in range(slots):
+            s = (step * tiles + i) * slots + k
+            src = jnp.clip(src_ref[s], 0, blocks - 1)
+            tgt = tgt_ref[s]
+            part = jnp.dot(atm_ref[src], w_ref[i * slots + k], preferred_element_type=jnp.float32)
+            out_ref[i, k * fields : (k + 1) * fields, :] = jnp.where(tgt >= 0, part, jnp.float32(0.0))
+            tail = jnp.where(row_ids == k, tgt.astype(jnp.float32), tail)
+        out_ref[i, slots * fields : slots * fields + 8, :] = tail
+        return carry
+
+    lax.fori_loop(0, tiles, one_tile, 0)
+
+
+def remap_partials(atm_blocks, weights, sources, targets):
+    blocks, fields, cells = atm_blocks.shape
+    slot_total = weights.shape[0]
+    slots = 2
+    tile_count = slot_total // slots
+    rows = slots * fields + 8
+    per = TILES_PER_STEP
+    return pl.pallas_call(
+        remap_kernel,
+        out_shape=jax.ShapeDtypeStruct((tile_count, rows, cells), jnp.float32),
+        grid_spec=pltpu.PrefetchScalarGridSpec(
+            num_scalar_prefetch=2,
+            grid=(tile_count // per,),
+            in_specs=[
+                pl.BlockSpec((blocks, fields, cells), lambda g, src, tgt: (0, 0, 0)),
+                pl.BlockSpec((per * slots, cells, cells), lambda g, src, tgt: (g, 0, 0)),
+            ],
+            out_specs=pl.BlockSpec((per, rows, cells), lambda g, src, tgt: (g, 0, 0)),
+        ),
+        cost_estimate=pl.CostEstimate(
+            flops=2 * slot_total * fields * cells * cells,
+            transcendentals=0,
+            bytes_accessed=slot_total * cells * cells * 2 + tile_count * rows * cells * 4,
+        ),
+    )(sources, targets, atm_blocks, weights)
 
 
 def advect(tracer_now, east_speed, north_speed, sea_mask):
@@ -71,24 +126,15 @@
     slot_count = source_block.shape[1] // tile_count
     tracer_count, level_count, lat_rows, lon_cols = tracers.shape
 
-    atm_blocks = atm_fluxes.reshape(field_count, cell_count // block_cells, block_cells)
-    chosen = jnp.take(atm_blocks, source_block[0], axis=1)
-    partials = jnp.einsum(
-        "fsb,sbc->sfc", chosen, remap_weights[0], preferred_element_type=jnp.float32
-    )
     slot_ids = jnp.arange(tile_count * slot_count, dtype=jnp.int32)
     is_live = slot_ids % slot_count < jnp.repeat(block_count[0], slot_count)
-    partials = jnp.where(is_live[:, None, None], partials, jnp.float32(0.0))
-    targets = jnp.where(is_live, target_block[0], -1).astype(jnp.float32)
-    sent = partials.reshape(tile_count, slot_count * field_count, block_cells)
+    targets = jnp.where(is_live, target_block[0], -1)
+    atm_blocks = atm_fluxes.reshape(field_count, cell_count // block_cells, block_cells)
+    sent = remap_partials(atm_blocks.transpose(1, 0, 2), remap_weights[0], source_block[0], targets)
     arrived = lax.all_to_all(sent, ("lat", "lon"), split_axis=0, concat_axis=0, tiled=True)
-    landed = lax.all_to_all(
-        targets.reshape(tile_count, slot_count),
-        ("lat", "lon"),
-        split_axis=0,
-        concat_axis=0,
-        tiled=True,
-    )
+    landed = arrived[:, slot_count * field_count : slot_count * (field_count + 1), 0]
+    assert slot_count == 2
+    arrived = arrived[:, : slot_count * field_count]
 
     sea_here = land_mask.astype(jnp.float32)
     planes = tracer_count * level_count

time: 110 us -> 113 us (1.027)
  Pallas kernels: 0 us -> 19.9 us
  matrix products: 12.1 us -> 2.16 us
  other arithmetic: 36.7 us -> 31 us
  starting transfers between devices: 28.4 us -> 22.9 us
  waiting for transfers between devices: 15 us -> 20 us
    pallas_call x0 -> x1, Pallas kernels: none -> 19.9 us  [remap_partials(): pl.pallas_call(remap_kernel, out_shape=jax.ShapeDtypeStruct((tile_count,...]
    all_to_all x1 -> x0, starting transfers between devices: 11.7 us -> none  [coupled_step(): lax.all_to_all(targets.reshape(tile_count, slot_count), ('lat', 'lon'), s...]
    all_to_all x1, waiting for transfers between devices: 9.48 us -> 19.3 us  [coupled_step(): lax.all_to_all(sent, ('lat', 'lon'), split_axis=0, concat_axis=0, tiled=T...]
    dot_general x1 -> x0, matrix products: 7.91 us -> none  [coupled_step(): jnp.einsum('fsb,sbc->sfc', chosen, remap_weights[0], preferred_element_ty...]
    all_to_all x1, starting transfers between devices: 5.93 us -> 10.9 us  [coupled_step(): lax.all_to_all(sent, ('lat', 'lon'), split_axis=0, concat_axis=0, tiled=T...]
    ppermute x1, waiting for transfers between devices: 5.53 us -> 0.69 us  [with_halo(): lax.ppermute(block[..., -width:], 'lon', shifted_pairs(lon_count, 1, True))]
    slice x0 -> x2, local copies, waits for them, and re-layouts: none -> 3.52 us  [the longest x1 2.26 us: coupled_step(): arrived = arrived[:, :slot_count * field_count]]
    all_to_all x1 -> x0, other arithmetic: 2.24 us -> none  [coupled_step(): lax.all_to_all(targets.reshape(tile_count, slot_count), ('lat', 'lon'), s...]
  transfers between devices with their start and end apart: 6 -> 5, of which waited for: 2 -> 2; matrix products, arithmetic and copies ran while one was open for 49% -> 27% of each run, Pallas kernels for 0% -> 18%
where the time goes in v6:
time: 113 us; the launch traced here: 112 us
  other arithmetic  31 us (27%)
  starting transfers between devices  22.9 us (20%)
  waiting for transfers between devices  20 us (18%)
  Pallas kernels  19.9 us (18%)
  local copies, waits for them, and re-layouts  15.6 us (14%)
  matrix products  2.16 us (2%)
    pallas_call x1, Pallas kernels, remap_partials(): pl.pallas_call(remap_kernel, out_shape=jax.ShapeDtypeStruct((tile_count,...  19.9 us
    all_to_all x1, waiting for transfers between devices, coupled_step(): lax.all_to_all(sent, ('lat', 'lon'), split_axis=0, concat_axis=0, tiled=T...  19.3 us
    all_to_all x1, starting transfers between devices, coupled_step(): lax.all_to_all(sent, ('lat', 'lon'), split_axis=0, concat_axis=0, tiled=T...  10.9 us
    sub x3, other arithmetic, advect(): inner + east_flow[..., 1:-1, :-1] - east_flow[..., 1:-1, 1:]  7.8 us
    concatenate x2, other arithmetic, with_halo(): return jnp.concatenate([south, block, north], axis=-2)  5.55 us
    ppermute x1, starting transfers between devices, with_halo(): lax.ppermute(block[..., :width], 'lon', shifted_pairs(lon_count, -1, True))  5.15 us
    mul x4, other arithmetic, advect(): mask_east * (east_speed[:, :, :-1] * (tracer_now[..., :-1] + tracer_now[....  4.22 us
    mul x4, other arithmetic, advect(): mask_north * (north_speed[:, :-1, :] * (tracer_now[..., :-1, :] + tracer_...  4.15 us
  transfers between devices with their start and end apart: 5, of which 2 were waited for; matrix products, arithmetic and copies ran while one was open for 27% of the time, Pallas kernels for 18%

profile of v6, /device:TPU:0, one launch (start us, length us, event | category | flops | bytes accessed | tf_op | source)
XLA Modules:
  0.0 111.9 jit_solution(7315534167741405211)
XLA Ops:
  0.0 1.3 %fusion.11 = (f32[16,128]{1,0:T(8,128)}, f32[1,16,128]{2,1,0:T(8,128)S(1)}) fusion(s32[16,128]{1,0:T(8,128)} %param.18), kind=kLoop, calls=%fused_computation.64 | loop fusion | flops 2048 | bytes 24576 | tf_op jit(solution)/shard_map/convert_element_type | solution.py:139
  1.3 1.3 %pad_maximum_fusion.1 = f32[129,16,128]{2,1,0:T(8,128)S(1)} fusion(f32[1,16,128]{2,1,0:T(8,128)S(1)} %get-tuple-element.10, f32[16,16,128]{2,1,0:T(8,128)} %param.17, f32[16,16,128]{2,1,0:T(8,128)} %param.16, f32[96,16,128]{2,1,0:T(8,128)} %bitcast.33), kind=kLoop, calls=%fused_computation.23 | loop fusion | flops 792576 | bytes 2113536 | tf_op jit(solution)/shard_map/concatenate | solution.py:141
  3.7 1.7 %collective-permute-start = (f32[129,16,4]{0,1,2:T(8,128)S(1)}, f32[129,16,4]{0,1,2:T(8,128)S(1)}, u32[]{:S(2)}, u32[]{:S(2)}) collective-permute-start(f32[129,16,4]{0,1,2:T(8,128)S(1)} %copy.49), channel_id=1, source_target_pairs={{0,1},{1,2},{2,3},{3,4},{4,5},{5,6},{6,7},{7,8},{8,9},{9,10},{10,1... | collective-permute-start | bytes 99080 | tf_op jit(solution)/shard_map/ppermute | solution.py:29
  6.1 5.1 %collective-permute-start.1 = (f32[129,16,4]{0,1,2:T(8,128)S(1)}, f32[129,16,4]{0,1,2:T(8,128)S(1)}, u32[]{:S(2)}, u32[]{:S(2)}) collective-permute-start(f32[129,16,4]{0,1,2:T(8,128)S(1)} %copy.50), channel_id=1, source_target_pairs={{0,31},{1,0},{2,1},{3,2},{4,3},{5,4},{6,5},{7,6},{8,7},{9,8},{10,9... | collective-permute-start | bytes 99080 | tf_op jit(solution)/shard_map/ppermute | solution.py:30
  11.3 0.7 reshape.49
  12.0 0.7 collective-permute-done
  12.7 0.8 copy.51
  13.5 0.8 copy.52
  14.3 2.6 %pad_maximum_fusion.7 = (f32[129,4,136]{2,1,0:T(4,128)}, f32[129,4,136]{2,1,0:T(4,128)S(1)}) fusion(f32[129,16,4]{2,1,0:T(8,128)S(1)} %copy.52, f32[129,16,4]{2,1,0:T(8,128)S(1)} %copy.51, f32[1,16,128]{2,1,0:T(8,128)S(1)} %get-tuple-element.10, f32[16,16,128]{2,1,0:T(8,128)} %param.17, f32[16,16,128]{2,1,0:T(8,128)} %param.16, f32[96,16,128]{2,1,0:T(8,128)S(1)} %bitcast.34), kind=kLoop, calls=%fused_computation.35 | loop fusion | flops 701760 | bytes 1684224 | tf_op jit(solution)/shard_map/slice | solution.py:32
  17.0 2.2 %copy.53 = f32[129,4,136]{0,2,1:T(8,128)} copy(f32[129,4,136]{2,1,0:T(4,128)} %get-tuple-element.5) | data formatting | bytes 561408 | tf_op jit(solution)/shard_map/slice | solution.py:32
  19.1 1.1 %copy.54 = f32[129,4,136]{0,2,1:T(8,128)} copy(f32[129,4,136]{2,1,0:T(4,128)S(1)} %get-tuple-element.6) | data formatting | bytes 561408 | tf_op jit(solution)/shard_map/slice | solution.py:33
  20.3 1.3 %collective-permute-start.3 = (f32[129,4,136]{0,2,1:T(8,128)}, f32[129,4,136]{0,2,1:T(8,128)S(1)}, u32[]{:S(2)}, u32[]{:S(2)}) collective-permute-start(f32[129,4,136]{0,2,1:T(8,128)} %copy.54), channel_id=1, source_target_pairs={{32,0},{64,32},{96,64},{33,1},{65,33},{97,65},{34,2},{66,34},{98,6... | collective-permute-start | bytes 842120 | tf_op jit(solution)/shard_map/ppermute | solution.py:33
  21.5 3.9 %collective-permute-start.2 = (f32[129,4,136]{0,2,1:T(8,128)}, f32[129,4,136]{0,2,1:T(8,128)}, u32[]{:S(2)}, u32[]{:S(2)}) collective-permute-start(f32[129,4,136]{0,2,1:T(8,128)} %copy.53), channel_id=1, source_target_pairs={{0,32},{32,64},{64,96},{1,33},{33,65},{65,97},{2,34},{34,66},{66,9... | collective-permute-start | bytes 842120 | tf_op jit(solution)/shard_map/ppermute | solution.py:32
  25.4 1.3 %compare_select_fusion.tgt_ref = s32[256]{0:T(256)} fusion(s32[256]{0:T(256)} %bitcast.40, s32[256]{0:T(256)} %reshape.49), kind=kLoop, calls=%fused_computation.60 | loop fusion | flops 2048 | bytes 3072 | tf_op jit(solution)/shard_map/jit(_where)/select_n | solution.py:131
  27.3 19.9 %shard_map.100 = f32[128,56,128]{2,1,0:T(8,128)} custom-call(s32[256]{0:T(256)} %bitcast.39, s32[256]{0:T(256)} %compare_select_fusion.tgt_ref, bf16[16,24,128]{2,1,0:T(8,128)(2,1)} %bitcast_bitcast_fusion.atm_ref, bf16[256,128,128]{2,1,0:T(8,128)(2,1)} %bitcast.37), custom_call_target="tpu_custom_call" | custom-call | flops 201326592 | bytes 12058624 | tf_op jit(solution)/shard_map/pallas_call | solution.py:70
  47.3 10.9 %all-to-all-start = ((f32[128,56,128]{2,1,0:T(8,128)}), f32[128,56,128]{2,1,0:T(8,128)}, u32[]{:S(2)}, u32[]{:S(2)}) async-start(f32[128,56,128]{2,1,0:T(8,128)} %shard_map.100), calls=%async_computation | async-start | bytes 7340032 | tf_op jit(solution)/shard_map/all_to_all | solution.py:134
  58.2 1.1 %copy.56 = f32[129,4,136]{2,1,0:T(4,128)} copy(f32[129,4,136]{0,2,1:T(8,128)S(1)} %collective-permute-done.3) | data formatting | bytes 561408 | tf_op jit(solution)/shard_map/ppermute | solution.py:33
  59.3 1.4 %copy.55 = f32[129,4,136]{2,1,0:T(4,128)S(1)} copy(f32[129,4,136]{0,2,1:T(8,128)} %collective-permute-done.2) | data formatting | bytes 561408 | tf_op jit(solution)/shard_map/ppermute | solution.py:32
  60.7 5.2 %pad_maximum_fusion = f32[129,24,136]{2,1,0:T(8,128)S(1)} fusion(f32[129,4,136]{2,1,0:T(4,128)} %copy.56, f32[129,16,4]{2,1,0:T(8,128)S(1)} %copy.52, f32[1,16,128]{2,1,0:T(8,128)} %copy-done.6, f32[16,16,128]{2,1,0:T(8,128)} %param.17, f32[16,16,128]{2,1,0:T(8,128)} %param.16, f32[96,16,128]{2,1,0:T(8,128)S(1)} %bitcast.35, f32[129,16,4]{2,1,0:T(8,128)S(1)} %copy.51, ...), kind=kLoop, calls=%fused_computation | loop fusion | flops 2947392 | bytes 3368448 | tf_op jit(solution)/shard_map/concatenate | solution.py:34
  68.4 0.7 subtract_multiply_fusion.6
  69.7 2.5 %slice_subtract_fusion.4 = f32[6,16,22,134]{3,2,1,0:T(8,128)S(1)} fusion(f32[6,16,23,136]{3,2,1,0:T(8,128)S(1)} %subtract_multiply_fusion.6, f32[6,16,24,135]{3,2,1,0:T(8,128)S(1)} %subtract_multiply_fusion.7, f32[6,16,24,136]{3,2,1,0:T(8,128)S(1)} %bitcast.31), kind=kLoop, calls=%fused_computation.11 | loop fusion | flops 1132032 | bytes 6792192 | tf_op jit(solution)/shard_map/sub | solution.py:103
  72.9 0.7 subtract_multiply_fusion.4
  73.6 2.5 %slice_subtract_fusion.2 = f32[6,16,20,132]{3,2,1,0:T(8,128)S(1)} fusion(f32[6,16,21,134]{3,2,1,0:T(8,128)S(1)} %subtract_multiply_fusion.4, f32[6,16,22,133]{3,2,1,0:T(8,128)S(1)} %subtract_multiply_fusion.5, f32[6,16,22,134]{3,2,1,0:T(8,128)S(1)} %slice_subtract_fusion.4), kind=kLoop, calls=%fused_computation.7 | loop fusion | flops 1013760 | bytes 6082560 | tf_op jit(solution)/shard_map/sub | solution.py:103
  77.5 2.7 %slice_subtract_fusion = f32[6,16,18,130]{3,2,1,0:T(8,128)S(1)} fusion(f32[6,16,19,132]{3,2,1,0:T(8,128)S(1)} %subtract_multiply_fusion.2, f32[6,16,20,131]{3,2,1,0:T(8,128)S(1)} %subtract_multiply_fusion.3, f32[6,16,20,132]{3,2,1,0:T(8,128)S(1)} %slice_subtract_fusion.2), kind=kLoop, calls=%fused_computation.3 | loop fusion | flops 898560 | bytes 5391360 | tf_op jit(solution)/shard_map/sub | solution.py:103
  80.2 2.2 %subtract_multiply_fusion.1 = f32[6,16,18,129]{3,2,1,0:T(8,128)} fusion(f32[6,16,18,130]{3,2,1,0:T(8,128)S(1)} %slice_subtract_fusion, f32[16,18,129]{2,1,0:T(8,128)S(1)} %slice.382, f32[18,129]{1,0:T(8,128)S(1)} %slice_multiply_fusion.1), kind=kLoop, calls=%fused_computation.16 | loop fusion | flops 1560384 | bytes 2832840 | tf_op jit(solution)/shard_map/mul | solution.py:92
  82.4 2.1 %subtract_multiply_fusion = f32[6,16,17,130]{3,2,1,0:T(8,128)} fusion(f32[6,16,18,130]{3,2,1,0:T(8,128)S(1)} %slice_subtract_fusion, f32[16,17,130]{2,1,0:T(8,128)S(1)} %pad_maximum_fusion.8, f32[17,130]{1,0:T(8,128)S(1)} %slice_multiply_fusion), kind=kLoop, calls=%fused_computation.15 | loop fusion | flops 1485120 | bytes 2696200 | tf_op jit(solution)/shard_map/mul | solution.py:97
  84.5 19.3 %all-to-all-done = f32[128,56,128]{2,1,0:T(8,128)} async-done(((f32[128,56,128]{2,1,0:T(8,128)}), f32[128,56,128]{2,1,0:T(8,128)}, u32[]{:S(2)}, u32[]{:S(2)}) %all-to-all-start) | async-done | bytes 3670048 | tf_op jit(solution)/shard_map/all_to_all | solution.py:134
  103.8 1.3 %slice_reduce_fusion = f32[128,2]{1,0:T(8,128)S(1)} fusion(f32[128,56,128]{2,1,0:T(8,128)} %all-to-all-done), kind=kLoop, calls=%fused_computation.44 | loop fusion | bytes 2048 | tf_op jit(solution)/shard_map/slice | solution.py:135
  105.2 2.3 %slice.394 = f32[128,48,128]{2,1,0:T(8,128)S(1)} slice(f32[128,56,128]{2,1,0:T(8,128)} %all-to-all-done), slice={[0:128], [0:48], [0:128]} | slice | bytes 6291456 | tf_op jit(solution)/shard_map/slice | solution.py:137
  107.5 1.3 %fusion = f32[16,24,128]{2,0,1:T(8,128)S(1)} fusion(f32[256,24,128]{2,1,0:T(8,128)S(1)} %bitcast.32, f32[256]{0:T(256)S(1)} %eq.17), kind=kOutput, calls=%fused_computation.1 | convolution fusion | flops 150999040 | bytes 3343360 | tf_op jit(solution)/shard_map/rk,kfc->rfc/dot_general | solution.py:171
  108.8 0.8 fusion.3
  109.7 2.2 %fusion.2 = f32[6,16,16,128]{3,2,1,0:T(8,128)} fusion(f32[6,16,17,130]{3,2,1,0:T(8,128)S(1)} %copy-done.3, f32[6,16,18,129]{3,2,1,0:T(8,128)S(1)} %copy-done.2, f32[6,16,18,130]{3,2,1,0:T(8,128)S(1)} %slice_subtract_fusion, f32[6,16,16,128]{3,1,0,2:T(8,128)S(1)} %bitcast.38, f32[16,128]{1,0:T(8,128)S(1)} %copy-done.8), kind=kLoop, calls=%fused_computation.25 | loop fusion | flops 1179648 | bytes 5513216 | tf_op jit(solution)/shard_map/add | solution.py:178
  (53 shorter events, 7.5 us)
Async XLA Ops:
  0.0 26.7 %copy-start = (bf16[24,2048]{1,0:T(8,128)(2,1)S(1)}, bf16[24,2048]{1,0:T(8,128)(2,1)}, u32[]{:S(2)}) copy-start(bf16[24,2048]{1,0:T(8,128)(2,1)} %param.10) | copy-start | bytes 294916
  1.3 13.0 %copy-start.6 = (f32[1,16,128]{2,1,0:T(8,128)}, f32[1,16,128]{2,1,0:T(8,128)S(1)}, u32[]{:S(2)}) copy-start(f32[1,16,128]{2,1,0:T(8,128)S(1)} %get-tuple-element.10) | copy-start | bytes 24580
  2.7 8.5 %copy-start.10 = (s32[1,128]{1,0:T(1,128)S(1)}, s32[1,128]{1,0:T(1,128)}, u32[]{:S(2)}) copy-start(s32[1,128]{1,0:T(1,128)} %param.14) | copy-start | bytes 1540
  3.0 11.3 %copy-start.1 = (f32[6,16,16,128]{3,2,1,0:T(8,128)S(1)}, f32[6,16,16,128]{3,2,1,0:T(8,128)}, u32[]{:S(2)}) copy-start(f32[6,16,16,128]{3,2,1,0:T(8,128)} %param.15) | copy-start | bytes 2359300
  3.7 9.0 %collective-permute-start = (f32[129,16,4]{0,1,2:T(8,128)S(1)}, f32[129,16,4]{0,1,2:T(8,128)S(1)}, u32[]{:S(2)}, u32[]{:S(2)}) collective-permute-start(f32[129,16,4]{0,1,2:T(8,128)S(1)} %copy.49), channel_id=1, source_target_pairs={{0,1},{1,2},{2,3},{3,4},{4,5},{5,6},{6,7},{7,8},{8,9},{9,10},{10,1... | collective-permute-start | bytes 99080 | tf_op jit(solution)/shard_map/ppermute | solution.py:29
  6.1 7.5 %collective-permute-start.1 = (f32[129,16,4]{0,1,2:T(8,128)S(1)}, f32[129,16,4]{0,1,2:T(8,128)S(1)}, u32[]{:S(2)}, u32[]{:S(2)}) collective-permute-start(f32[129,16,4]{0,1,2:T(8,128)S(1)} %copy.50), channel_id=1, source_target_pairs={{0,31},{1,0},{2,1},{3,2},{4,3},{5,4},{6,5},{7,6},{8,7},{9,8},{10,9... | collective-permute-start | bytes 99080 | tf_op jit(solution)/shard_map/ppermute | solution.py:30
  20.3 37.9 %collective-permute-start.3 = (f32[129,4,136]{0,2,1:T(8,128)}, f32[129,4,136]{0,2,1:T(8,128)S(1)}, u32[]{:S(2)}, u32[]{:S(2)}) collective-permute-start(f32[129,4,136]{0,2,1:T(8,128)} %copy.54), channel_id=1, source_target_pairs={{32,0},{64,32},{96,64},{33,1},{65,33},{97,65},{34,2},{66,34},{98,6... | collective-permute-start | bytes 842120 | tf_op jit(solution)/shard_map/ppermute | solution.py:33
  21.5 37.8 %collective-permute-start.2 = (f32[129,4,136]{0,2,1:T(8,128)}, f32[129,4,136]{0,2,1:T(8,128)}, u32[]{:S(2)}, u32[]{:S(2)}) collective-permute-start(f32[129,4,136]{0,2,1:T(8,128)} %copy.53), channel_id=1, source_target_pairs={{0,32},{32,64},{64,96},{1,33},{33,65},{65,97},{2,34},{34,66},{66,9... | collective-permute-start | bytes 842120 | tf_op jit(solution)/shard_map/ppermute | solution.py:32
  47.3 56.5 %all-to-all-start = ((f32[128,56,128]{2,1,0:T(8,128)}), f32[128,56,128]{2,1,0:T(8,128)}, u32[]{:S(2)}, u32[]{:S(2)}) async-start(f32[128,56,128]{2,1,0:T(8,128)} %shard_map.100), calls=%async_computation | async-start | bytes 7340032 | tf_op jit(solution)/shard_map/all_to_all | solution.py:134
  68.4 0.9 copy-start.4
  68.4 1.0 copy-start.5
  68.4 1.0 copy-start.7
  105.2 4.5 %copy-start.3 = (f32[6,16,17,130]{3,2,1,0:T(8,128)S(1)}, f32[6,16,17,130]{3,2,1,0:T(8,128)}, u32[]{:S(2)}) copy-start(f32[6,16,17,130]{3,2,1,0:T(8,128)} %subtract_multiply_fusion) | copy-start | bytes 2545924
  107.5 1.4 %copy-start.9 = (f32[96,24]{0,1:T(8,128)S(1)}, f32[96,24]{0,1:T(8,128)}, u32[]{:S(2)}) copy-start(f32[96,24]{0,1:T(8,128)} %param.19) | copy-start | bytes 27652
  107.5 2.2 %copy-start.2 = (f32[6,16,18,129]{3,2,1,0:T(8,128)S(1)}, f32[6,16,18,129]{3,2,1,0:T(8,128)}, u32[]{:S(2)}) copy-start(f32[6,16,18,129]{3,2,1,0:T(8,128)} %subtract_multiply_fusion.1) | copy-start | bytes 2674948
  107.5 2.2 %copy-start.8 = (f32[16,128]{1,0:T(8,128)S(1)}, f32[16,128]{1,0:T(8,128)}, u32[]{:S(2)}) copy-start(f32[16,128]{1,0:T(8,128)} %get-tuple-element.9) | copy-start | bytes 24580

commit v7 on v5

--- a/solution.py
+++ b/solution.py
@@ -24,12 +24,30 @@
 def with_halo(block, width):
     lon_count = lax.axis_size("lon")
     lat_count = lax.axis_size("lat")
-    west = lax.ppermute(block[..., -width:], "lon", shifted_pairs(lon_count, 1, True))
-    east = lax.ppermute(block[..., :width], "lon", shifted_pairs(lon_count, -1, True))
-    block = jnp.concatenate([west, block, east], axis=-1)
-    south = lax.ppermute(block[..., -width:, :], "lat", shifted_pairs(lat_count, 1, False))
-    north = lax.ppermute(block[..., :width, :], "lat", shifted_pairs(lat_count, -1, False))
-    return jnp.concatenate([south, block, north], axis=-2)
+    planes, rows, cols = block.shape
+    west = lax.ppermute(
+        block[..., -width:].reshape(planes, rows * width), "lon", shifted_pairs(lon_count, 1, True)
+    )
+    east = lax.ppermute(
+        block[..., :width].reshape(planes, rows * width), "lon", shifted_pairs(lon_count, -1, True)
+    )
+    west = west.reshape(planes, rows, width)
+    east = east.reshape(planes, rows, width)
+    middle = jnp.concatenate([west, block, east], axis=-1)
+    wide_cols = cols + 2 * width
+    south = lax.ppermute(
+        middle[:, -width:, :].reshape(planes, width * wide_cols),
+        "lat",
+        shifted_pairs(lat_count, 1, False),
+    )
+    north = lax.ppermute(
+        middle[:, :width, :].reshape(planes, width * wide_cols),
+        "lat",
+        shifted_pairs(lat_count, -1, False),
+    )
+    south = south.reshape(planes, width, wide_cols)
+    north = north.reshape(planes, width, wide_cols)
+    return jnp.concatenate([south, middle, north], axis=-2)
 
 
 def advect(tracer_now, east_speed, north_speed, sea_mask):

time: 102 us -> 103 us (level)
  local copies, waits for them, and re-layouts: 16.3 us -> 18.1 us
    reshape x0 -> x12, local copies, waits for them, and re-layouts: none -> 9.61 us  [the longest x1 2.09 us: with_halo(): middle[:, -width:, :].reshape(planes, width * wide_cols)]
    ppermute x4 -> x0, local copies, waits for them, and re-layouts: 4.13 us -> none  [the longest x1 1.41 us: with_halo(): lax.ppermute(block[..., -width:, :], 'lat', shifted_pairs(lat_count, 1, F...]
    slice x5 -> x1, local copies, waits for them, and re-layouts: 5.01 us -> 1.32 us  [with_halo(): block[..., -width:].reshape(planes, rows * width)]
where the time goes in v7:
time: 103 us; the launch traced here: 102 us
  other arithmetic  33.8 us (33%)
  starting transfers between devices  22 us (21%)
  waiting for transfers between devices  19.1 us (19%)
  local copies, waits for them, and re-layouts  18.1 us (18%)
  matrix products  8.65 us (8%)
    all_to_all x1, waiting for transfers between devices, coupled_step(): lax.all_to_all(sent, ('lat', 'lon'), split_axis=0, concat_axis=0, tiled=T...  19.1 us
    all_to_all x1, starting transfers between devices, coupled_step(): lax.all_to_all(sent, ('lat', 'lon'), split_axis=0, concat_axis=0, tiled=T...  10.1 us
    sub x3, other arithmetic, advect(): inner + east_flow[..., 1:-1, :-1] - east_flow[..., 1:-1, 1:]  7.9 us
    ppermute x1, starting transfers between devices, with_halo(): lax.ppermute(block[..., :width].reshape(planes, rows * width), 'lon', shi...  6.74 us
    dot_general x1, matrix products, coupled_step(): jnp.einsum('fsb,sbc->sfc', chosen, remap_weights[0], preferred_element_ty...  6.49 us
    concatenate x2, other arithmetic, with_halo(): return jnp.concatenate([south, middle, north], axis=-2)  5.57 us
    mul x4, other arithmetic, advect(): mask_east * (east_speed[:, :, :-1] * (tracer_now[..., :-1] + tracer_now[....  4.22 us
    mul x4, other arithmetic, advect(): mask_north * (north_speed[:, :-1, :] * (tracer_now[..., :-1, :] + tracer_...  4.14 us
  transfers between devices with their start and end apart: 5, of which 1 were waited for; matrix products, arithmetic and copies ran while one was open for 40% of the time, Pallas kernels for 0%

profile of v7, /device:TPU:0, one launch (start us, length us, event | category | flops | bytes accessed | tf_op | source)
XLA Modules:
  0.0 102.1 jit_solution(14686893304113646644)
XLA Ops:
  0.0 0.7 fusion.25
  0.7 1.3 %pad_maximum_fusion.1 = f32[129,16,128]{2,1,0:T(8,128)S(1)} fusion(f32[1,16,128]{2,1,0:T(8,128)S(1)} %get-tuple-element.10, f32[16,16,128]{2,1,0:T(8,128)} %param.17, f32[16,16,128]{2,1,0:T(8,128)} %param.16, f32[96,16,128]{2,1,0:T(8,128)} %bitcast.47), kind=kLoop, calls=%fused_computation.31 | loop fusion | flops 792576 | bytes 2113536 | tf_op jit(solution)/shard_map/concatenate | solution.py:119
  2.1 1.3 %fusion.24 = (f32[129,16,4]{2,1,0:T(8,128)S(1)}, f32[129,16,4]{2,1,0:T(8,128)}) fusion(f32[129,16,128]{2,1,0:T(8,128)S(1)} %pad_maximum_fusion.1), kind=kLoop, calls=%fused_computation.83 | loop fusion | bytes 132096 | tf_op jit(solution)/shard_map/slice | solution.py:29
  3.4 1.7 %reshape.192 = f32[129,64]{1,0:T(8,128)S(1)} reshape(f32[129,16,4]{2,1,0:T(8,128)} %get-tuple-element.8) | data formatting | bytes 66048 | tf_op jit(solution)/shard_map/reshape | solution.py:32
  5.2 6.7 %collective-permute-start.1 = (f32[129,64]{0,1:T(8,128)S(1)}, f32[129,64]{0,1:T(8,128)S(1)}, u32[]{:S(2)}, u32[]{:S(2)}) collective-permute-start(f32[129,64]{0,1:T(8,128)S(1)} %copy.27), channel_id=1, source_target_pairs={{0,31},{1,0},{2,1},{3,2},{4,3},{5,4},{6,5},{7,6},{8,7},{9,8},{10,9... | collective-permute-start | bytes 99080 | tf_op jit(solution)/shard_map/ppermute | solution.py:31
  14.2 1.0 gather_fusion
  15.2 6.5 %broadcast_select_fusion = f32[256,24,128]{2,1,0:T(8,128)} fusion(bf16[1,256,128,128]{3,2,1,0:T(8,128)(2,1)} %param.11, bf16[256,24,128]{2,1,0:T(8,128)(2,1)S(1)} %gather_fusion, pred[256]{0:T(512)(128)(4,1)S(1)} %get-tuple-element.11, pred[256]{0:T(512)(128)(4,1)S(1)} %get-tuple-element.12), kind=kOutput, calls=%fused_computation.29 | convolution fusion | flops 202899456 | bytes 13107712 | tf_op jit(solution)/shard_map/fsb,sbc->sfc/dot_general | solution.py:94
  21.9 0.8 copy.20
  22.7 0.8 copy.21
  23.5 2.6 %pad_maximum_fusion.7 = (f32[129,4,136]{2,1,0:T(4,128)}, f32[129,4,136]{2,1,0:T(4,128)S(1)}) fusion(f32[129,16,4]{2,1,0:T(8,128)S(1)} %copy.21, f32[129,16,4]{2,1,0:T(8,128)S(1)} %copy.20, f32[1,16,128]{2,1,0:T(8,128)S(1)} %get-tuple-element.10, f32[16,16,128]{2,1,0:T(8,128)} %param.17, f32[16,16,128]{2,1,0:T(8,128)} %param.16, f32[96,16,128]{2,1,0:T(8,128)S(1)} %bitcast.48), kind=kLoop, calls=%fused_computation.44 | loop fusion | flops 701760 | bytes 1684224 | tf_op jit(solution)/shard_map/slice | solution.py:39
  26.1 2.1 %reshape.171 = f32[129,544]{1,0:T(8,128)} reshape(f32[129,4,136]{2,1,0:T(4,128)} %get-tuple-element.5) | data formatting | bytes 561408 | tf_op jit(solution)/shard_map/reshape | solution.py:39
  28.2 1.1 %reshape.173 = f32[129,544]{1,0:T(8,128)} reshape(f32[129,4,136]{2,1,0:T(4,128)S(1)} %get-tuple-element.6) | data formatting | bytes 561408 | tf_op jit(solution)/shard_map/reshape | solution.py:44
  29.3 1.3 %collective-permute-start.3 = (f32[129,544]{1,0:T(8,128)}, f32[129,544]{1,0:T(8,128)S(1)}, u32[]{:S(2)}, u32[]{:S(2)}) collective-permute-start(f32[129,544]{1,0:T(8,128)} %reshape.173), channel_id=1, source_target_pairs={{32,0},{64,32},{96,64},{33,1},{65,33},{97,65},{34,2},{66,34},{98,6... | collective-permute-start | bytes 842120 | tf_op jit(solution)/shard_map/ppermute | solution.py:43
  30.6 3.8 %collective-permute-start.2 = (f32[129,544]{1,0:T(8,128)}, f32[129,544]{1,0:T(8,128)}, u32[]{:S(2)}, u32[]{:S(2)}) collective-permute-start(f32[129,544]{1,0:T(8,128)} %reshape.171), channel_id=1, source_target_pairs={{0,32},{32,64},{64,96},{1,33},{33,65},{65,97},{2,34},{34,66},{66,9... | collective-permute-start | bytes 842120 | tf_op jit(solution)/shard_map/ppermute | solution.py:38
  34.5 4.0 %maximum_maximum_fusion = f32[128,56,128]{2,1,0:T(8,128)} fusion(f32[128,2,128]{2,1,0:T(2,128)S(1)} %broadcast_in_dim.66, f32[128,48,128]{2,1,0:T(8,128)} %bitcast.51, f32[56]{0:T(128)S(1)} %pad.2.clone), kind=kLoop, calls=%fused_computation.3 | loop fusion | flops 1835008 | bytes 6947040 | tf_op jit(solution)/shard_map/concatenate | solution.py:105
  38.5 10.1 %all-to-all-start = ((f32[128,56,128]{2,1,0:T(8,128)}), f32[128,56,128]{2,1,0:T(8,128)}, u32[]{:S(2)}, u32[]{:S(2)}) async-start(f32[128,56,128]{2,1,0:T(8,128)} %maximum_maximum_fusion), calls=%async_computation | async-start | bytes 7340032 | tf_op jit(solution)/shard_map/all_to_all | solution.py:113
  48.6 1.2 %reshape.174 = f32[129,4,136]{2,1,0:T(4,128)} reshape(f32[129,544]{1,0:T(8,128)S(1)} %collective-permute-done.3) | data formatting | bytes 561408 | tf_op jit(solution)/shard_map/reshape | solution.py:49
  49.8 1.4 %reshape.172 = f32[129,4,136]{2,1,0:T(4,128)S(1)} reshape(f32[129,544]{1,0:T(8,128)} %collective-permute-done.2) | data formatting | bytes 561408 | tf_op jit(solution)/shard_map/reshape | solution.py:48
  51.2 5.3 %pad_maximum_fusion = f32[129,24,136]{2,1,0:T(8,128)S(1)} fusion(f32[129,4,136]{2,1,0:T(4,128)} %reshape.174, f32[129,16,4]{2,1,0:T(8,128)S(1)} %copy.21, f32[1,16,128]{2,1,0:T(8,128)S(1)} %get-tuple-element.10, f32[16,16,128]{2,1,0:T(8,128)} %param.17, f32[16,16,128]{2,1,0:T(8,128)} %param.16, f32[96,16,128]{2,1,0:T(8,128)S(1)} %bitcast.49, ...), kind=kLoop, calls=%fused_computation.4 | loop fusion | flops 2947392 | bytes 3368448 | tf_op jit(solution)/shard_map/concatenate | solution.py:50
  60.2 2.5 %slice_subtract_fusion.4 = f32[6,16,22,134]{3,2,1,0:T(8,128)S(1)} fusion(f32[6,16,23,136]{3,2,1,0:T(8,128)S(1)} %subtract_multiply_fusion.6, f32[6,16,24,135]{3,2,1,0:T(8,128)S(1)} %subtract_multiply_fusion.7, f32[6,16,24,136]{3,2,1,0:T(8,128)S(1)} %bitcast.45), kind=kLoop, calls=%fused_computation.15 | loop fusion | flops 1132032 | bytes 6792192 | tf_op jit(solution)/shard_map/sub | solution.py:66
  62.7 0.7 subtract_multiply_fusion.5
  63.4 0.7 subtract_multiply_fusion.4
  64.1 2.6 %slice_subtract_fusion.2 = f32[6,16,20,132]{3,2,1,0:T(8,128)S(1)} fusion(f32[6,16,21,134]{3,2,1,0:T(8,128)S(1)} %subtract_multiply_fusion.4, f32[6,16,22,133]{3,2,1,0:T(8,128)S(1)} %subtract_multiply_fusion.5, f32[6,16,22,134]{3,2,1,0:T(8,128)S(1)} %slice_subtract_fusion.4), kind=kLoop, calls=%fused_computation.11 | loop fusion | flops 1013760 | bytes 6082560 | tf_op jit(solution)/shard_map/sub | solution.py:66
  68.1 2.7 %slice_subtract_fusion = f32[6,16,18,130]{3,2,1,0:T(8,128)S(1)} fusion(f32[6,16,19,132]{3,2,1,0:T(8,128)S(1)} %subtract_multiply_fusion.2, f32[6,16,20,131]{3,2,1,0:T(8,128)S(1)} %subtract_multiply_fusion.3, f32[6,16,20,132]{3,2,1,0:T(8,128)S(1)} %slice_subtract_fusion.2), kind=kLoop, calls=%fused_computation.7 | loop fusion | flops 898560 | bytes 5391360 | tf_op jit(solution)/shard_map/sub | solution.py:66
  70.9 2.2 %subtract_multiply_fusion.1 = f32[6,16,18,129]{3,2,1,0:T(8,128)} fusion(f32[6,16,18,130]{3,2,1,0:T(8,128)S(1)} %slice_subtract_fusion, f32[16,18,129]{2,1,0:T(8,128)S(1)} %slice.384, f32[18,129]{1,0:T(8,128)S(1)} %slice_multiply_fusion.1), kind=kLoop, calls=%fused_computation.20 | loop fusion | flops 1560384 | bytes 2832840 | tf_op jit(solution)/shard_map/mul | solution.py:55
  73.0 2.1 %subtract_multiply_fusion = f32[6,16,17,130]{3,2,1,0:T(8,128)} fusion(f32[6,16,18,130]{3,2,1,0:T(8,128)S(1)} %slice_subtract_fusion, f32[16,17,130]{2,1,0:T(8,128)S(1)} %pad_maximum_fusion.8, f32[17,130]{1,0:T(8,128)S(1)} %slice_multiply_fusion), kind=kLoop, calls=%fused_computation.19 | loop fusion | flops 1485120 | bytes 2696200 | tf_op jit(solution)/shard_map/mul | solution.py:60
  75.1 19.1 %all-to-all-done = f32[128,56,128]{2,1,0:T(8,128)} async-done(((f32[128,56,128]{2,1,0:T(8,128)}), f32[128,56,128]{2,1,0:T(8,128)}, u32[]{:S(2)}, u32[]{:S(2)}) %all-to-all-start) | async-done | bytes 3670048 | tf_op jit(solution)/shard_map/all_to_all | solution.py:113
  94.2 1.3 %slice_reduce_fusion = f32[128,2]{1,0:T(8,128)S(1)} fusion(f32[128,56,128]{2,1,0:T(8,128)} %all-to-all-done), kind=kLoop, calls=%fused_computation.53 | loop fusion | bytes 2048 | tf_op jit(solution)/shard_map/slice | solution.py:114
  95.6 2.3 %slice.396 = f32[128,48,128]{2,1,0:T(8,128)S(1)} slice(f32[128,56,128]{2,1,0:T(8,128)} %all-to-all-done), slice={[0:128], [0:48], [0:128]} | slice | bytes 6291456 | tf_op jit(solution)/shard_map/slice | solution.py:115
  97.9 1.3 %fusion.2 = f32[16,24,128]{2,0,1:T(8,128)S(1)} fusion(f32[256,24,128]{2,1,0:T(8,128)S(1)} %bitcast.46, f32[256]{0:T(256)S(1)} %eq.17), kind=kOutput, calls=%fused_computation.5 | convolution fusion | flops 150999040 | bytes 3343360 | tf_op jit(solution)/shard_map/rk,kfc->rfc/dot_general | solution.py:149
  99.3 0.8 fusion.13
  100.1 2.0 %fusion.11 = f32[6,16,16,128]{3,2,1,0:T(8,128)} fusion(f32[6,16,17,130]{3,2,1,0:T(8,128)S(1)} %copy-done.4, f32[6,16,18,129]{3,2,1,0:T(8,128)S(1)} %copy-done.3, f32[6,16,18,130]{3,2,1,0:T(8,128)S(1)} %slice_subtract_fusion, f32[6,16,16,128]{3,1,0,2:T(8,128)S(1)} %bitcast.52, f32[16,128]{1,0:T(8,128)S(1)} %get-tuple-element.9), kind=kLoop, calls=%fused_computation.33 | loop fusion | flops 1179648 | bytes 5513216 | tf_op jit(solution)/shard_map/add | solution.py:156
  (68 shorter events, 7.8 us)
Async XLA Ops:
  0.0 14.2 %copy-start = (bf16[24,2048]{1,0:T(8,128)(2,1)S(1)}, bf16[24,2048]{1,0:T(8,128)(2,1)}, u32[]{:S(2)}) copy-start(bf16[24,2048]{1,0:T(8,128)(2,1)} %param.10) | copy-start | bytes 294916
  2.1 10.5 %copy-start.8 = (s32[1,256]{1,0:T(1,128)S(1)}, s32[1,256]{1,0:T(1,128)}, u32[]{:S(2)}) copy-start(s32[1,256]{1,0:T(1,128)} %param.12) | copy-start | bytes 3076
  2.1 11.0 %copy-start.10 = (s32[1,256]{1,0:T(1,128)S(1)}, s32[1,256]{1,0:T(1,128)}, u32[]{:S(2)}) copy-start(s32[1,256]{1,0:T(1,128)} %param.13) | copy-start | bytes 3076
  3.4 10.5 %copy-start.9 = (s32[1,128]{1,0:T(1,128)S(1)}, s32[1,128]{1,0:T(1,128)}, u32[]{:S(2)}) copy-start(s32[1,128]{1,0:T(1,128)} %param.14) | copy-start | bytes 1540
  5.2 17.5 %collective-permute-start.1 = (f32[129,64]{0,1:T(8,128)S(1)}, f32[129,64]{0,1:T(8,128)S(1)}, u32[]{:S(2)}, u32[]{:S(2)}) collective-permute-start(f32[129,64]{0,1:T(8,128)S(1)} %copy.27), channel_id=1, source_target_pairs={{0,31},{1,0},{2,1},{3,2},{4,3},{5,4},{6,5},{7,6},{8,7},{9,8},{10,9... | collective-permute-start | bytes 99080 | tf_op jit(solution)/shard_map/ppermute | solution.py:31
  12.5 9.4 %collective-permute-start = (f32[129,64]{0,1:T(8,128)S(1)}, f32[129,64]{0,1:T(8,128)S(1)}, u32[]{:S(2)}, u32[]{:S(2)}) collective-permute-start(f32[129,64]{0,1:T(8,128)S(1)} %copy.26), channel_id=1, source_target_pairs={{0,1},{1,2},{2,3},{3,4},{4,5},{5,6},{6,7},{7,8},{8,9},{9,10},{10,1... | collective-permute-start | bytes 99080 | tf_op jit(solution)/shard_map/ppermute | solution.py:28
  21.7 1.8 %copy-start.2 = (f32[6,16,16,128]{3,2,1,0:T(8,128)S(1)}, f32[6,16,16,128]{3,2,1,0:T(8,128)}, u32[]{:S(2)}) copy-start(f32[6,16,16,128]{3,2,1,0:T(8,128)} %param.15) | copy-start | bytes 2359300
  29.3 19.4 %collective-permute-start.3 = (f32[129,544]{1,0:T(8,128)}, f32[129,544]{1,0:T(8,128)S(1)}, u32[]{:S(2)}, u32[]{:S(2)}) collective-permute-start(f32[129,544]{1,0:T(8,128)} %reshape.173), channel_id=1, source_target_pairs={{32,0},{64,32},{96,64},{33,1},{65,33},{97,65},{34,2},{66,34},{98,6... | collective-permute-start | bytes 842120 | tf_op jit(solution)/shard_map/ppermute | solution.py:43
  30.6 19.3 %collective-permute-start.2 = (f32[129,544]{1,0:T(8,128)}, f32[129,544]{1,0:T(8,128)}, u32[]{:S(2)}, u32[]{:S(2)}) collective-permute-start(f32[129,544]{1,0:T(8,128)} %reshape.171), channel_id=1, source_target_pairs={{0,32},{32,64},{64,96},{1,33},{33,65},{65,97},{2,34},{34,66},{66,9... | collective-permute-start | bytes 842120 | tf_op jit(solution)/shard_map/ppermute | solution.py:38
  38.5 55.7 %all-to-all-start = ((f32[128,56,128]{2,1,0:T(8,128)}), f32[128,56,128]{2,1,0:T(8,128)}, u32[]{:S(2)}, u32[]{:S(2)}) async-start(f32[128,56,128]{2,1,0:T(8,128)} %maximum_maximum_fusion), calls=%async_computation | async-start | bytes 7340032 | tf_op jit(solution)/shard_map/all_to_all | solution.py:113
  58.9 0.9 copy-start.5
  58.9 1.0 copy-start.6
  95.6 4.5 %copy-start.4 = (f32[6,16,17,130]{3,2,1,0:T(8,128)S(1)}, f32[6,16,17,130]{3,2,1,0:T(8,128)}, u32[]{:S(2)}) copy-start(f32[6,16,17,130]{3,2,1,0:T(8,128)} %subtract_multiply_fusion) | copy-start | bytes 2545924
  97.9 1.4 %copy-start.7 = (f32[96,24]{0,1:T(8,128)S(1)}, f32[96,24]{0,1:T(8,128)}, u32[]{:S(2)}) copy-start(f32[96,24]{0,1:T(8,128)} %param.19) | copy-start | bytes 27652
  97.9 2.2 %copy-start.3 = (f32[6,16,18,129]{3,2,1,0:T(8,128)S(1)}, f32[6,16,18,129]{3,2,1,0:T(8,128)}, u32[]{:S(2)}) copy-start(f32[6,16,18,129]{3,2,1,0:T(8,128)} %subtract_multiply_fusion.1) | copy-start | bytes 2674948
  100.1 2.0 %copy-start.1 = (bf16[24,2048]{1,0:T(8,128)(2,1)S(1)}, bf16[24,2048]{1,0:T(8,128)(2,1)}, u32[]{:S(2)}) copy-start(bf16[24,2048]{1,0:T(8,128)(2,1)} %param.10) | copy-start | bytes 294916

commit v8 on v7

--- a/solution.py
+++ b/solution.py
@@ -89,26 +89,41 @@
     slot_count = source_block.shape[1] // tile_count
     tracer_count, level_count, lat_rows, lon_cols = tracers.shape
 
+    slot_ids = jnp.arange(tile_count * slot_count, dtype=jnp.int32)
+    is_live = slot_ids % slot_count < jnp.repeat(block_count[0], slot_count)
+    targets = jnp.where(is_live, target_block[0], -1).astype(jnp.float32)
     atm_blocks = atm_fluxes.reshape(field_count, cell_count // block_cells, block_cells)
     chosen = jnp.take(atm_blocks, source_block[0], axis=1)
-    partials = jnp.einsum(
-        "fsb,sbc->sfc", chosen, remap_weights[0], preferred_element_type=jnp.float32
+    chosen = chosen.transpose(1, 0, 2).reshape(tile_count, slot_count, field_count, block_cells)
+    zero_block = jnp.zeros((tile_count, field_count, block_cells), chosen.dtype)
+    diagonal = []
+    for k in range(slot_count):
+        diagonal.append(
+            jnp.concatenate(
+                [chosen[:, k] if j == k else zero_block for j in range(slot_count)], axis=-1
+            )
+        )
+    diagonal.append(jnp.zeros((tile_count, 8, slot_count * block_cells), chosen.dtype))
+    lhs = jnp.concatenate(diagonal, axis=1)
+    stacked_weights = remap_weights[0].reshape(tile_count, slot_count * block_cells, block_cells)
+    product = jnp.einsum(
+        "trb,tbc->trc", lhs, stacked_weights, preferred_element_type=jnp.float32
     )
-    slot_ids = jnp.arange(tile_count * slot_count, dtype=jnp.int32)
-    is_live = slot_ids % slot_count < jnp.repeat(block_count[0], slot_count)
-    partials = jnp.where(is_live[:, None, None], partials, jnp.float32(0.0))
-    targets = jnp.where(is_live, target_block[0], -1).astype(jnp.float32)
-    rows_part = jnp.broadcast_to(
-        targets.reshape(tile_count, slot_count, 1), (tile_count, slot_count, block_cells)
-    )
-    pad_rows = jnp.zeros((tile_count, 8 - slot_count, block_cells), jnp.float32)
-    sent = jnp.concatenate(
-        [
-            partials.reshape(tile_count, slot_count * field_count, block_cells),
-            rows_part,
-            pad_rows,
-        ],
-        axis=1,
+    row_ids = jnp.arange(slot_count * field_count + 8)
+    slot_of_row = row_ids // field_count
+    live_rows = is_live.reshape(tile_count, slot_count)
+    tgt_rows = targets.reshape(tile_count, slot_count)
+    kept = jnp.zeros((tile_count, slot_count * field_count + 8), jnp.bool_)
+    tail = jnp.zeros((tile_count, slot_count * field_count + 8), jnp.float32)
+    for k in range(slot_count):
+        kept = kept | ((slot_of_row == k)[None, :] & live_rows[:, k : k + 1])
+        tail = jnp.where(
+            (row_ids == slot_count * field_count + k)[None, :], tgt_rows[:, k : k + 1], tail
+        )
+    sent = jnp.where(
+        (row_ids < slot_count * field_count)[None, :, None],
+        jnp.where(kept[:, :, None], product, jnp.float32(0.0)),
+        tail[:, :, None],
     )
     arrived = lax.all_to_all(sent, ("lat", "lon"), split_axis=0, concat_axis=0, tiled=True)
     landed = arrived[:, slot_count * field_count : slot_count * (field_count + 1), 0]

time: 103 us -> 101 us (0.981)
  waiting for transfers between devices: 19.1 us -> 21.3 us
  other arithmetic: 33.8 us -> 31.6 us
  starting transfers between devices: 22 us -> 19.9 us
  matrix products: 8.65 us -> 9.72 us
    concatenate x1 -> x0, other arithmetic: 4 us -> none  [coupled_step(): jnp.concatenate([partials.reshape(tile_count, slot_count * field_count, b...]
    ppermute x1, waiting for transfers between devices: 0.01 us -> 2.1 us  [with_halo(): lax.ppermute(block[..., -width:].reshape(planes, rows * width), 'lon', sh...]
    all_to_all x1, starting transfers between devices: 10.1 us -> 8.04 us  [coupled_step(): lax.all_to_all(sent, ('lat', 'lon'), split_axis=0, concat_axis=0, tiled=T...]
    squeeze x0 -> x1, local copies, waits for them, and re-layouts: none -> 1.41 us  [coupled_step(): chosen[:, k]]
    reshape x2, local copies, waits for them, and re-layouts: 1.75 us -> 0.56 us  [with_halo(): block[..., :width].reshape(planes, rows * width)]
    dot_general x1, matrix products: 6.49 us -> 7.56 us  [coupled_step(): jnp.einsum('trb,tbc->trc', lhs, stacked_weights, preferred_element_type=j...]
  transfers between devices with their start and end apart: 5 -> 5, of which waited for: 1 -> 2; matrix products, arithmetic and copies ran while one was open for 40% -> 41% of each run, Pallas kernels for 0% -> 0%
where the time goes in v8:
time: 101 us
  other arithmetic  31.6 us (31%)
  waiting for transfers between devices  21.3 us (21%)
  starting transfers between devices  19.9 us (20%)
  local copies, waits for them, and re-layouts  17.4 us (17%)
  matrix products  9.72 us (10%)
    all_to_all x1, waiting for transfers between devices, coupled_step(): lax.all_to_all(sent, ('lat', 'lon'), split_axis=0, concat_axis=0, tiled=T...  19.2 us
    all_to_all x1, starting transfers between devices, coupled_step(): lax.all_to_all(sent, ('lat', 'lon'), split_axis=0, concat_axis=0, tiled=T...  8.04 us
    sub x3, other arithmetic, advect(): inner + east_flow[..., 1:-1, :-1] - east_flow[..., 1:-1, 1:]  7.8 us
    dot_general x1, matrix products, coupled_step(): jnp.einsum('trb,tbc->trc', lhs, stacked_weights, preferred_element_type=j...  7.56 us
    ppermute x1, starting transfers between devices, with_halo(): lax.ppermute(block[..., :width].reshape(planes, rows * width), 'lon', shi...  6.74 us
    concatenate x2, other arithmetic, with_halo(): return jnp.concatenate([south, middle, north], axis=-2)  5.57 us
    mul x4, other arithmetic, advect(): mask_east * (east_speed[:, :, :-1] * (tracer_now[..., :-1] + tracer_now[....  4.2 us
    mul x4, other arithmetic, advect(): mask_north * (north_speed[:, :-1, :] * (tracer_now[..., :-1, :] + tracer_...  4.16 us
  transfers between devices with their start and end apart: 5, of which 2 were waited for; matrix products, arithmetic and copies ran while one was open for 41% of the time, Pallas kernels for 0%

profile of v8, /device:TPU:0, one launch (start us, length us, event | category | flops | bytes accessed | tf_op | source)
XLA Modules:
  0.0 100.6 jit_solution(12488144239565091710)
XLA Ops:
  0.0 0.7 fusion.33
  0.7 1.3 %pad_maximum_fusion.1 = f32[129,16,128]{2,1,0:T(8,128)S(1)} fusion(f32[1,16,128]{2,1,0:T(8,128)S(1)} %get-tuple-element.16, f32[16,16,128]{2,1,0:T(8,128)} %param.17, f32[16,16,128]{2,1,0:T(8,128)} %param.16, f32[96,16,128]{2,1,0:T(8,128)} %bitcast.47), kind=kLoop, calls=%fused_computation.41 | loop fusion | flops 792576 | bytes 2113536 | tf_op jit(solution)/shard_map/concatenate | solution.py:134
  3.0 6.7 %collective-permute-start.1 = (f32[129,64]{0,1:T(8,128)S(1)}, f32[129,64]{0,1:T(8,128)S(1)}, u32[]{:S(2)}, u32[]{:S(2)}) collective-permute-start(f32[129,64]{0,1:T(8,128)S(1)} %copy.42), channel_id=1, source_target_pairs={{0,31},{1,0},{2,1},{3,2},{4,3},{5,4},{6,5},{7,6},{8,7},{9,8},{10,9... | collective-permute-start | bytes 99080 | tf_op jit(solution)/shard_map/ppermute | solution.py:31
  12.4 1.0 gather_fusion
  13.4 0.9 broadcast_select_fusion
  14.3 1.4 %slice_bitcast_fusion.1 = (bf16[128,24,128]{2,1,0:T(8,128)(2,1)}, bf16[128,24,128]{2,1,0:T(8,128)(2,1)}) fusion(bf16[128,2,24,128]{3,2,1,0:T(8,128)(2,1)S(1)} %bitcast.51), kind=kLoop, calls=%fused_computation.43 | loop fusion | bytes 3145728 | tf_op jit(solution)/shard_map/squeeze | solution.py:103
  15.8 0.7 select_select_fusion.1
  16.8 2.1 %collective-permute-done = f32[129,64]{0,1:T(8,128)S(1)} collective-permute-done((f32[129,64]{0,1:T(8,128)S(1)}, f32[129,64]{0,1:T(8,128)S(1)}, u32[]{:S(2)}, u32[]{:S(2)}) %collective-permute-start) | collective-permute-done | bytes 33056 | tf_op jit(solution)/shard_map/ppermute | solution.py:28
  18.9 0.8 copy.32
  19.7 0.8 copy.33
  20.5 2.6 %pad_maximum_fusion.7 = (f32[129,4,136]{2,1,0:T(4,128)}, f32[129,4,136]{2,1,0:T(4,128)S(1)}) fusion(f32[129,16,4]{2,1,0:T(8,128)S(1)} %copy.33, f32[129,16,4]{2,1,0:T(8,128)S(1)} %copy.32, f32[1,16,128]{2,1,0:T(8,128)S(1)} %get-tuple-element.16, f32[16,16,128]{2,1,0:T(8,128)} %param.17, f32[16,16,128]{2,1,0:T(8,128)} %param.16, f32[96,16,128]{2,1,0:T(8,128)S(1)} %bitcast.48), kind=kLoop, calls=%fused_computation.55 | loop fusion | flops 701760 | bytes 1684224 | tf_op jit(solution)/shard_map/slice | solution.py:39
  23.2 2.1 %reshape.262 = f32[129,544]{1,0:T(8,128)} reshape(f32[129,4,136]{2,1,0:T(4,128)} %get-tuple-element.9) | data formatting | bytes 561408 | tf_op jit(solution)/shard_map/reshape | solution.py:39
  25.3 1.1 %reshape.264 = f32[129,544]{1,0:T(8,128)} reshape(f32[129,4,136]{2,1,0:T(4,128)S(1)} %get-tuple-element.10) | data formatting | bytes 561408 | tf_op jit(solution)/shard_map/reshape | solution.py:44
  26.4 1.3 %collective-permute-start.3 = (f32[129,544]{1,0:T(8,128)}, f32[129,544]{1,0:T(8,128)S(1)}, u32[]{:S(2)}, u32[]{:S(2)}) collective-permute-start(f32[129,544]{1,0:T(8,128)} %reshape.264), channel_id=1, source_target_pairs={{32,0},{64,32},{96,64},{33,1},{65,33},{97,65},{34,2},{66,34},{98,6... | collective-permute-start | bytes 842120 | tf_op jit(solution)/shard_map/ppermute | solution.py:43
  27.7 3.8 %collective-permute-start.2 = (f32[129,544]{1,0:T(8,128)}, f32[129,544]{1,0:T(8,128)}, u32[]{:S(2)}, u32[]{:S(2)}) collective-permute-start(f32[129,544]{1,0:T(8,128)} %reshape.262), channel_id=1, source_target_pairs={{0,32},{32,64},{64,96},{1,33},{33,65},{65,97},{2,34},{34,66},{66,9... | collective-permute-start | bytes 842120 | tf_op jit(solution)/shard_map/ppermute | solution.py:38
  31.4 7.6 %select_select_fusion = f32[128,56,128]{2,1,0:T(8,128)} fusion(f32[128,56]{1,0:T(8,128)S(1)} %copy-done.7, pred[56]{0:T(512)(128)(4,1)S(1)} %iota_compare_fusion.6, pred[128,56]{1,0:T(8,128)(4,1)S(1)} %copy.34, bf16[128,256,128]{2,1,0:T(8,128)(2,1)} %bitcast.57, bf16[128,24,128]{2,1,0:T(8,128)(2,1)} %get-tuple-element.12, ...), kind=kOutput, calls=%fused_computation.14 | convolution fusion | flops 493617152 | bytes 13667496 | tf_op jit(solution)/shard_map/trb,tbc->trc/dot_general | solution.py:109
  39.0 8.0 %all-to-all-start = ((f32[128,56,128]{2,1,0:T(8,128)}), f32[128,56,128]{2,1,0:T(8,128)}, u32[]{:S(2)}, u32[]{:S(2)}) async-start(f32[128,56,128]{2,1,0:T(8,128)} %select_select_fusion), calls=%async_computation | async-start | bytes 7340032 | tf_op jit(solution)/shard_map/all_to_all | solution.py:128
  47.1 1.2 %reshape.265 = f32[129,4,136]{2,1,0:T(4,128)} reshape(f32[129,544]{1,0:T(8,128)S(1)} %collective-permute-done.3) | data formatting | bytes 561408 | tf_op jit(solution)/shard_map/reshape | solution.py:49
  48.2 1.4 %reshape.263 = f32[129,4,136]{2,1,0:T(4,128)S(1)} reshape(f32[129,544]{1,0:T(8,128)} %collective-permute-done.2) | data formatting | bytes 561408 | tf_op jit(solution)/shard_map/reshape | solution.py:48
  49.6 5.3 %pad_maximum_fusion = f32[129,24,136]{2,1,0:T(8,128)S(1)} fusion(f32[129,4,136]{2,1,0:T(4,128)} %reshape.265, f32[129,16,4]{2,1,0:T(8,128)S(1)} %copy.33, f32[1,16,128]{2,1,0:T(8,128)S(1)} %get-tuple-element.16, f32[16,16,128]{2,1,0:T(8,128)} %param.17, f32[16,16,128]{2,1,0:T(8,128)} %param.16, f32[96,16,128]{2,1,0:T(8,128)S(1)} %bitcast.49, ...), kind=kLoop, calls=%fused_computation.15 | loop fusion | flops 2947392 | bytes 3368448 | tf_op jit(solution)/shard_map/concatenate | solution.py:50
  58.6 2.5 %slice_subtract_fusion.4 = f32[6,16,22,134]{3,2,1,0:T(8,128)S(1)} fusion(f32[6,16,23,136]{3,2,1,0:T(8,128)S(1)} %subtract_multiply_fusion.6, f32[6,16,24,135]{3,2,1,0:T(8,128)S(1)} %subtract_multiply_fusion.7, f32[6,16,24,136]{3,2,1,0:T(8,128)S(1)} %bitcast.45), kind=kLoop, calls=%fused_computation.26 | loop fusion | flops 1132032 | bytes 6792192 | tf_op jit(solution)/shard_map/sub | solution.py:66
  61.8 0.7 subtract_multiply_fusion.4
  62.5 2.5 %slice_subtract_fusion.2 = f32[6,16,20,132]{3,2,1,0:T(8,128)S(1)} fusion(f32[6,16,21,134]{3,2,1,0:T(8,128)S(1)} %subtract_multiply_fusion.4, f32[6,16,22,133]{3,2,1,0:T(8,128)S(1)} %subtract_multiply_fusion.5, f32[6,16,22,134]{3,2,1,0:T(8,128)S(1)} %slice_subtract_fusion.4), kind=kLoop, calls=%fused_computation.22 | loop fusion | flops 1013760 | bytes 6082560 | tf_op jit(solution)/shard_map/sub | solution.py:66
  66.4 2.7 %slice_subtract_fusion = f32[6,16,18,130]{3,2,1,0:T(8,128)S(1)} fusion(f32[6,16,19,132]{3,2,1,0:T(8,128)S(1)} %subtract_multiply_fusion.2, f32[6,16,20,131]{3,2,1,0:T(8,128)S(1)} %subtract_multiply_fusion.3, f32[6,16,20,132]{3,2,1,0:T(8,128)S(1)} %slice_subtract_fusion.2), kind=kLoop, calls=%fused_computation.18 | loop fusion | flops 898560 | bytes 5391360 | tf_op jit(solution)/shard_map/sub | solution.py:66
  69.2 2.2 %subtract_multiply_fusion.1 = f32[6,16,18,129]{3,2,1,0:T(8,128)} fusion(f32[6,16,18,130]{3,2,1,0:T(8,128)S(1)} %slice_subtract_fusion, f32[16,18,129]{2,1,0:T(8,128)S(1)} %slice.420, f32[18,129]{1,0:T(8,128)S(1)} %slice_multiply_fusion.1), kind=kLoop, calls=%fused_computation.31 | loop fusion | flops 1560384 | bytes 2832840 | tf_op jit(solution)/shard_map/mul | solution.py:55
  71.3 2.1 %subtract_multiply_fusion = f32[6,16,17,130]{3,2,1,0:T(8,128)} fusion(f32[6,16,18,130]{3,2,1,0:T(8,128)S(1)} %slice_subtract_fusion, f32[16,17,130]{2,1,0:T(8,128)S(1)} %pad_maximum_fusion.8, f32[17,130]{1,0:T(8,128)S(1)} %slice_multiply_fusion), kind=kLoop, calls=%fused_computation.30 | loop fusion | flops 1485120 | bytes 2696200 | tf_op jit(solution)/shard_map/mul | solution.py:60
  73.4 19.2 %all-to-all-done = f32[128,56,128]{2,1,0:T(8,128)} async-done(((f32[128,56,128]{2,1,0:T(8,128)}), f32[128,56,128]{2,1,0:T(8,128)}, u32[]{:S(2)}, u32[]{:S(2)}) %all-to-all-start) | async-done | bytes 3670048 | tf_op jit(solution)/shard_map/all_to_all | solution.py:128
  92.7 1.3 %slice_reduce_fusion = f32[128,2]{1,0:T(8,128)S(1)} fusion(f32[128,56,128]{2,1,0:T(8,128)} %all-to-all-done), kind=kLoop, calls=%fused_computation.64 | loop fusion | bytes 2048 | tf_op jit(solution)/shard_map/slice | solution.py:129
  94.1 2.3 %slice.438 = f32[128,48,128]{2,1,0:T(8,128)S(1)} slice(f32[128,56,128]{2,1,0:T(8,128)} %all-to-all-done), slice={[0:128], [0:48], [0:128]} | slice | bytes 6291456 | tf_op jit(solution)/shard_map/slice | solution.py:130
  96.3 1.3 %fusion.12 = f32[16,24,128]{2,0,1:T(8,128)S(1)} fusion(f32[256,24,128]{2,1,0:T(8,128)S(1)} %bitcast.46, f32[256]{0:T(256)S(1)} %eq.55), kind=kOutput, calls=%fused_computation.16 | convolution fusion | flops 150999040 | bytes 3343360 | tf_op jit(solution)/shard_map/rk,kfc->rfc/dot_general | solution.py:164
  97.7 0.8 fusion.19
  98.6 2.0 %fusion.18 = f32[6,16,16,128]{3,2,1,0:T(8,128)} fusion(f32[6,16,17,130]{3,2,1,0:T(8,128)S(1)} %copy-done.4, f32[6,16,18,129]{3,2,1,0:T(8,128)S(1)} %copy-done.3, f32[6,16,18,130]{3,2,1,0:T(8,128)S(1)} %slice_subtract_fusion, f32[6,16,16,128]{3,1,0,2:T(8,128)S(1)} %bitcast.52, f32[16,128]{1,0:T(8,128)S(1)} %get-tuple-element.15), kind=kLoop, calls=%fused_computation.45 | loop fusion | flops 1179648 | bytes 5513216 | tf_op jit(solution)/shard_map/add | solution.py:171
  (77 shorter events, 9.5 us)
Async XLA Ops:
  0.0 12.4 %copy-start = (bf16[24,2048]{1,0:T(8,128)(2,1)S(1)}, bf16[24,2048]{1,0:T(8,128)(2,1)}, u32[]{:S(2)}) copy-start(bf16[24,2048]{1,0:T(8,128)(2,1)} %param.10) | copy-start | bytes 294916
  2.1 8.4 %copy-start.10 = (s32[1,256]{1,0:T(1,128)S(1)}, s32[1,256]{1,0:T(1,128)}, u32[]{:S(2)}) copy-start(s32[1,256]{1,0:T(1,128)} %param.12) | copy-start | bytes 3076
  2.1 8.4 %copy-start.9 = (s32[1,128]{1,0:T(1,128)S(1)}, s32[1,128]{1,0:T(1,128)}, u32[]{:S(2)}) copy-start(s32[1,128]{1,0:T(1,128)} %param.14) | copy-start | bytes 1540
  2.1 9.2 %copy-start.11 = (s32[1,256]{1,0:T(1,128)S(1)}, s32[1,256]{1,0:T(1,128)}, u32[]{:S(2)}) copy-start(s32[1,256]{1,0:T(1,128)} %param.13) | copy-start | bytes 3076
  3.0 16.7 %collective-permute-start.1 = (f32[129,64]{0,1:T(8,128)S(1)}, f32[129,64]{0,1:T(8,128)S(1)}, u32[]{:S(2)}, u32[]{:S(2)}) collective-permute-start(f32[129,64]{0,1:T(8,128)S(1)} %copy.42), channel_id=1, source_target_pairs={{0,31},{1,0},{2,1},{3,2},{4,3},{5,4},{6,5},{7,6},{8,7},{9,8},{10,9... | collective-permute-start | bytes 99080 | tf_op jit(solution)/shard_map/ppermute | solution.py:31
  10.3 8.6 %collective-permute-start = (f32[129,64]{0,1:T(8,128)S(1)}, f32[129,64]{0,1:T(8,128)S(1)}, u32[]{:S(2)}, u32[]{:S(2)}) collective-permute-start(f32[129,64]{0,1:T(8,128)S(1)} %copy.41), channel_id=1, source_target_pairs={{0,1},{1,2},{2,3},{3,4},{4,5},{5,6},{6,7},{7,8},{8,9},{9,10},{10,1... | collective-permute-start | bytes 99080 | tf_op jit(solution)/shard_map/ppermute | solution.py:28
  14.3 6.2 %copy-start.2 = (f32[6,16,16,128]{3,2,1,0:T(8,128)S(1)}, f32[6,16,16,128]{3,2,1,0:T(8,128)}, u32[]{:S(2)}) copy-start(f32[6,16,16,128]{3,2,1,0:T(8,128)} %param.15) | copy-start | bytes 2359300
  20.5 10.9 %copy-start.7 = (f32[128,56]{1,0:T(8,128)S(1)}, f32[128,56]{1,0:T(8,128)}, u32[]{:S(2)}) copy-start(f32[128,56]{1,0:T(8,128)} %select_select_fusion.1) | copy-start | bytes 86020
  26.4 20.7 %collective-permute-start.3 = (f32[129,544]{1,0:T(8,128)}, f32[129,544]{1,0:T(8,128)S(1)}, u32[]{:S(2)}, u32[]{:S(2)}) collective-permute-start(f32[129,544]{1,0:T(8,128)} %reshape.264), channel_id=1, source_target_pairs={{32,0},{64,32},{96,64},{33,1},{65,33},{97,65},{34,2},{66,34},{98,6... | collective-permute-start | bytes 842120 | tf_op jit(solution)/shard_map/ppermute | solution.py:43
  27.7 20.6 %collective-permute-start.2 = (f32[129,544]{1,0:T(8,128)}, f32[129,544]{1,0:T(8,128)}, u32[]{:S(2)}, u32[]{:S(2)}) collective-permute-start(f32[129,544]{1,0:T(8,128)} %reshape.262), channel_id=1, source_target_pairs={{0,32},{32,64},{64,96},{1,33},{33,65},{65,97},{2,34},{34,66},{66,9... | collective-permute-start | bytes 842120 | tf_op jit(solution)/shard_map/ppermute | solution.py:38
  39.0 53.7 %all-to-all-start = ((f32[128,56,128]{2,1,0:T(8,128)}), f32[128,56,128]{2,1,0:T(8,128)}, u32[]{:S(2)}, u32[]{:S(2)}) async-start(f32[128,56,128]{2,1,0:T(8,128)} %select_select_fusion), calls=%async_computation | async-start | bytes 7340032 | tf_op jit(solution)/shard_map/all_to_all | solution.py:128
  57.3 0.9 copy-start.5
  57.3 1.0 copy-start.6
  94.0 4.5 %copy-start.4 = (f32[6,16,17,130]{3,2,1,0:T(8,128)S(1)}, f32[6,16,17,130]{3,2,1,0:T(8,128)}, u32[]{:S(2)}) copy-start(f32[6,16,17,130]{3,2,1,0:T(8,128)} %subtract_multiply_fusion) | copy-start | bytes 2545924
  96.3 1.4 %copy-start.8 = (f32[96,24]{0,1:T(8,128)S(1)}, f32[96,24]{0,1:T(8,128)}, u32[]{:S(2)}) copy-start(f32[96,24]{0,1:T(8,128)} %param.19) | copy-start | bytes 27652
  96.3 2.2 %copy-start.3 = (f32[6,16,18,129]{3,2,1,0:T(8,128)S(1)}, f32[6,16,18,129]{3,2,1,0:T(8,128)}, u32[]{:S(2)}) copy-start(f32[6,16,18,129]{3,2,1,0:T(8,128)} %subtract_multiply_fusion.1) | copy-start | bytes 2674948
  98.5 2.0 %copy-start.1 = (bf16[24,2048]{1,0:T(8,128)(2,1)S(1)}, bf16[24,2048]{1,0:T(8,128)(2,1)}, u32[]{:S(2)}) copy-start(bf16[24,2048]{1,0:T(8,128)(2,1)} %param.10) | copy-start | bytes 294916

commit v9 on v8

--- a/solution.py
+++ b/solution.py
@@ -106,9 +106,7 @@
     diagonal.append(jnp.zeros((tile_count, 8, slot_count * block_cells), chosen.dtype))
     lhs = jnp.concatenate(diagonal, axis=1)
     stacked_weights = remap_weights[0].reshape(tile_count, slot_count * block_cells, block_cells)
-    product = jnp.einsum(
-        "trb,tbc->trc", lhs, stacked_weights, preferred_element_type=jnp.float32
-    )
+    product = jnp.einsum("trb,tbc->trc", lhs, stacked_weights, preferred_element_type=jnp.float32)
     row_ids = jnp.arange(slot_count * field_count + 8)
     slot_of_row = row_ids // field_count
     live_rows = is_live.reshape(tile_count, slot_count)
@@ -126,8 +124,8 @@
         tail[:, :, None],
     )
     arrived = lax.all_to_all(sent, ("lat", "lon"), split_axis=0, concat_axis=0, tiled=True)
+    arrived_all = arrived
     landed = arrived[:, slot_count * field_count : slot_count * (field_count + 1), 0]
-    arrived = arrived[:, : slot_count * field_count]
 
     sea_here = land_mask.astype(jnp.float32)
     planes = tracer_count * level_count
@@ -156,15 +154,24 @@
             mask_wide[cut:end_r, cut:end_c],
         )
 
-    arrived = arrived.reshape(tile_count * slot_count, field_count, block_cells)
-    landed = landed.reshape(tile_count * slot_count)
-    chooser = (landed[None, :] == jnp.arange(lat_rows, dtype=jnp.float32)[:, None]).astype(
-        jnp.float32
-    )
+    groups = (slot_count * field_count + 8) // 8
+    per_slot = field_count // 8
+    chooser = (
+        landed[None, :, :] == jnp.arange(lat_rows, dtype=jnp.float32)[:, None, None]
+    ).astype(jnp.float32)
+    group_ids = jnp.arange(groups)
+    placement = (
+        group_ids[None, None, :]
+        == (jnp.arange(slot_count)[:, None, None] * per_slot + jnp.arange(per_slot)[None, :, None])
+    ).astype(jnp.float32)
+    picker = jnp.einsum("rtk,kjg->rjtg", chooser, placement)
     ocean_flux = jnp.einsum(
-        "rk,kfc->rfc", chooser, arrived, precision=lax.Precision.HIGHEST,
+        "rjtg,tgic->rjic",
+        picker,
+        arrived_all.reshape(tile_count, groups, 8, block_cells),
+        precision=lax.Precision.HIGHEST,
         preferred_element_type=jnp.float32,
-    )
+    ).reshape(lat_rows, field_count, block_cells)
     source = jnp.einsum(
         "pf,ifj->pij", coupling, ocean_flux, precision=lax.Precision.HIGHEST
     ).reshape(tracer_count, level_count, lat_rows, lon_cols)

time: 101 us -> 117 us (1.16)
  the two profiles are of different devices: /device:TPU:0 before, /device:TPU:1 now
where the time goes in v9:
time: 117 us; the launch traced here: 116 us
  waiting for transfers between devices  33 us (28%)
  other arithmetic  31 us (26%)
  starting transfers between devices  25.2 us (22%)
  local copies, waits for them, and re-layouts  13.8 us (12%)
  matrix products  12.9 us (11%)
    ppermute x1, waiting for transfers between devices, with_halo(): lax.ppermute(middle[:, :width, :].reshape(planes, width * wide_cols), 'la...  33 us
    all_to_all x1, starting transfers between devices, coupled_step(): lax.all_to_all(sent, ('lat', 'lon'), split_axis=0, concat_axis=0, tiled=T...  10.6 us
    sub x3, other arithmetic, advect(): inner + east_flow[..., 1:-1, :-1] - east_flow[..., 1:-1, 1:]  7.8 us
    ppermute x1, starting transfers between devices, with_halo(): lax.ppermute(block[..., :width].reshape(planes, rows * width), 'lon', shi...  7.17 us
    dot_general x1, matrix products, coupled_step(): jnp.einsum('trb,tbc->trc', lhs, stacked_weights, preferred_element_type=j...  6.83 us
    concatenate x2, other arithmetic, with_halo(): return jnp.concatenate([south, middle, north], axis=-2)  5.57 us
    dot_general x1, matrix products, coupled_step(): jnp.einsum('rjtg,tgic->rjic', picker, arrived_all.reshape(tile_count, gro...  4.91 us
    ppermute x1, starting transfers between devices, with_halo(): lax.ppermute(middle[:, -width:, :].reshape(planes, width * wide_cols), 'l...  4.32 us
  transfers between devices with their start and end apart: 5, of which 1 were waited for; matrix products, arithmetic and copies ran while one was open for 39% of the time, Pallas kernels for 0%

profile of v9, /device:TPU:1, one launch (start us, length us, event | category | flops | bytes accessed | tf_op | source)
XLA Modules:
  0.0 116.3 jit_solution(1204603874864574524)
XLA Ops:
  0.0 0.7 fusion.40
  0.7 1.3 %pad_maximum_fusion.1 = f32[129,16,128]{2,1,0:T(8,128)S(1)} fusion(f32[1,16,128]{2,1,0:T(8,128)S(1)} %get-tuple-element.16, f32[16,16,128]{2,1,0:T(8,128)} %param.17, f32[16,16,128]{2,1,0:T(8,128)} %param.16, f32[96,16,128]{2,1,0:T(8,128)} %bitcast.63), kind=kLoop, calls=%fused_computation.43 | loop fusion | flops 792576 | bytes 2113536 | tf_op jit(solution)/shard_map/concatenate | solution.py:132
  3.0 7.2 %collective-permute-start.1 = (f32[129,64]{0,1:T(8,128)S(1)}, f32[129,64]{0,1:T(8,128)S(1)}, u32[]{:S(2)}, u32[]{:S(2)}) collective-permute-start(f32[129,64]{0,1:T(8,128)S(1)} %copy.55), channel_id=1, source_target_pairs={{0,31},{1,0},{2,1},{3,2},{4,3},{5,4},{6,5},{7,6},{8,7},{9,8},{10,9... | collective-permute-start | bytes 99080 | tf_op jit(solution)/shard_map/ppermute | solution.py:31
  13.1 1.0 gather_fusion
  14.0 0.9 broadcast_select_fusion
  15.4 6.8 %select_select_fusion = f32[128,56,128]{2,1,0:T(8,128)} fusion(f32[128,56]{1,0:T(8,128)S(1)} %select_select_fusion.1, pred[56]{0:T(512)(128)(4,1)S(1)} %iota_compare_fusion.5, pred[128,56]{1,0:T(8,128)(4,1)S(1)} %copy.42, bf16[128,256,128]{2,1,0:T(8,128)(2,1)} %bitcast.75, bf16[128,24,128]{2,1,0:T(8,128)(2,1)S(1)} %get-tuple-element.12, ...), kind=kOutput, calls=%fused_computation.17 | convolution fusion | flops 493617152 | bytes 13667496 | tf_op jit(solution)/shard_map/trb,tbc->trc/dot_general | solution.py:109
  22.3 10.6 %all-to-all-start = ((f32[128,56,128]{2,1,0:T(8,128)}), f32[128,56,128]{2,1,0:T(8,128)}, u32[]{:S(2)}, u32[]{:S(2)}) async-start(f32[128,56,128]{2,1,0:T(8,128)} %select_select_fusion), calls=%async_computation | async-start | bytes 7340032 | tf_op jit(solution)/shard_map/all_to_all | solution.py:126
  32.9 0.8 copy.40
  33.7 0.8 copy.41
  34.5 2.6 %pad_maximum_fusion.7 = (f32[129,4,136]{2,1,0:T(4,128)}, f32[129,4,136]{2,1,0:T(4,128)S(1)}) fusion(f32[129,16,4]{2,1,0:T(8,128)S(1)} %copy.41, f32[129,16,4]{2,1,0:T(8,128)S(1)} %copy.40, f32[1,16,128]{2,1,0:T(8,128)S(1)} %get-tuple-element.16, f32[16,16,128]{2,1,0:T(8,128)} %param.17, f32[16,16,128]{2,1,0:T(8,128)} %param.16, f32[96,16,128]{2,1,0:T(8,128)S(1)} %bitcast.64), kind=kLoop, calls=%fused_computation.57 | loop fusion | flops 701760 | bytes 1684224 | tf_op jit(solution)/shard_map/slice | solution.py:39
  37.1 2.1 %reshape.294 = f32[129,544]{1,0:T(8,128)} reshape(f32[129,4,136]{2,1,0:T(4,128)} %get-tuple-element.9) | data formatting | bytes 561408 | tf_op jit(solution)/shard_map/reshape | solution.py:39
  39.2 1.1 reshape.296
  40.3 3.0 %collective-permute-start.3 = (f32[129,544]{1,0:T(8,128)}, f32[129,544]{1,0:T(8,128)S(1)}, u32[]{:S(2)}, u32[]{:S(2)}) collective-permute-start(f32[129,544]{1,0:T(8,128)} %reshape.296), channel_id=1, source_target_pairs={{32,0},{64,32},{96,64},{33,1},{65,33},{97,65},{34,2},{66,34},{98,6... | collective-permute-start | bytes 842120 | tf_op jit(solution)/shard_map/ppermute | solution.py:43
  43.3 4.3 %collective-permute-start.2 = (f32[129,544]{1,0:T(8,128)}, f32[129,544]{1,0:T(8,128)}, u32[]{:S(2)}, u32[]{:S(2)}) collective-permute-start(f32[129,544]{1,0:T(8,128)} %reshape.294), channel_id=1, source_target_pairs={{0,32},{32,64},{64,96},{1,33},{33,65},{65,97},{2,34},{34,66},{66,9... | collective-permute-start | bytes 842120 | tf_op jit(solution)/shard_map/ppermute | solution.py:38
  47.7 33.0 %collective-permute-done.3 = f32[129,544]{1,0:T(8,128)S(1)} collective-permute-done((f32[129,544]{1,0:T(8,128)}, f32[129,544]{1,0:T(8,128)S(1)}, u32[]{:S(2)}, u32[]{:S(2)}) %collective-permute-start.3) | collective-permute-done | bytes 280736 | tf_op jit(solution)/shard_map/ppermute | solution.py:43
  80.6 1.2 %reshape.297 = f32[129,4,136]{2,1,0:T(4,128)} reshape(f32[129,544]{1,0:T(8,128)S(1)} %collective-permute-done.3) | data formatting | bytes 561408 | tf_op jit(solution)/shard_map/reshape | solution.py:49
  81.8 1.4 %reshape.295 = f32[129,4,136]{2,1,0:T(4,128)S(1)} reshape(f32[129,544]{1,0:T(8,128)} %collective-permute-done.2) | data formatting | bytes 561408 | tf_op jit(solution)/shard_map/reshape | solution.py:48
  83.2 5.3 %pad_maximum_fusion = f32[129,24,136]{2,1,0:T(8,128)S(1)} fusion(f32[129,4,136]{2,1,0:T(4,128)} %reshape.297, f32[129,16,4]{2,1,0:T(8,128)S(1)} %copy.41, f32[1,16,128]{2,1,0:T(8,128)S(1)} %get-tuple-element.16, f32[16,16,128]{2,1,0:T(8,128)} %param.17, f32[16,16,128]{2,1,0:T(8,128)} %param.16, f32[96,16,128]{2,1,0:T(8,128)S(1)} %bitcast.65, ...), kind=kLoop, calls=%fused_computation.18 | loop fusion | flops 2947392 | bytes 3368448 | tf_op jit(solution)/shard_map/concatenate | solution.py:50
  90.2 0.7 subtract_multiply_fusion.7
  90.9 0.7 subtract_multiply_fusion.6
  92.2 2.5 %slice_subtract_fusion.4 = f32[6,16,22,134]{3,2,1,0:T(8,128)S(1)} fusion(f32[6,16,23,136]{3,2,1,0:T(8,128)S(1)} %subtract_multiply_fusion.6, f32[6,16,24,135]{3,2,1,0:T(8,128)S(1)} %subtract_multiply_fusion.7, f32[6,16,24,136]{3,2,1,0:T(8,128)S(1)} %bitcast.62), kind=kLoop, calls=%fused_computation.27 | loop fusion | flops 1132032 | bytes 6792192 | tf_op jit(solution)/shard_map/sub | solution.py:66
  94.7 0.7 subtract_multiply_fusion.5
  95.4 0.7 subtract_multiply_fusion.4
  96.1 2.5 %slice_subtract_fusion.2 = f32[6,16,20,132]{3,2,1,0:T(8,128)S(1)} fusion(f32[6,16,21,134]{3,2,1,0:T(8,128)S(1)} %subtract_multiply_fusion.4, f32[6,16,22,133]{3,2,1,0:T(8,128)S(1)} %subtract_multiply_fusion.5, f32[6,16,22,134]{3,2,1,0:T(8,128)S(1)} %slice_subtract_fusion.4), kind=kLoop, calls=%fused_computation.23 | loop fusion | flops 1013760 | bytes 6082560 | tf_op jit(solution)/shard_map/sub | solution.py:66
  99.3 0.7 subtract_multiply_fusion.2
  100.0 2.7 %slice_subtract_fusion = f32[6,16,18,130]{3,2,1,0:T(8,128)S(1)} fusion(f32[6,16,19,132]{3,2,1,0:T(8,128)S(1)} %subtract_multiply_fusion.2, f32[6,16,20,131]{3,2,1,0:T(8,128)S(1)} %subtract_multiply_fusion.3, f32[6,16,20,132]{3,2,1,0:T(8,128)S(1)} %slice_subtract_fusion.2), kind=kLoop, calls=%fused_computation.19 | loop fusion | flops 898560 | bytes 5391360 | tf_op jit(solution)/shard_map/sub | solution.py:66
  102.7 2.1 %subtract_multiply_fusion.1 = f32[6,16,18,129]{3,2,1,0:T(8,128)} fusion(f32[6,16,18,130]{3,2,1,0:T(8,128)S(1)} %slice_subtract_fusion, f32[16,18,129]{2,1,0:T(8,128)S(1)} %slice.416, f32[18,129]{1,0:T(8,128)S(1)} %slice_multiply_fusion.1), kind=kLoop, calls=%fused_computation.32 | loop fusion | flops 1560384 | bytes 2832840 | tf_op jit(solution)/shard_map/mul | solution.py:55
  104.8 2.2 %subtract_multiply_fusion = f32[6,16,17,130]{3,2,1,0:T(8,128)} fusion(f32[6,16,18,130]{3,2,1,0:T(8,128)S(1)} %slice_subtract_fusion, f32[16,17,130]{2,1,0:T(8,128)S(1)} %pad_maximum_fusion.8, f32[17,130]{1,0:T(8,128)S(1)} %slice_multiply_fusion), kind=kLoop, calls=%fused_computation.31 | loop fusion | flops 1485120 | bytes 2696200 | tf_op jit(solution)/shard_map/mul | solution.py:60
  107.0 1.1 slice.433
  108.5 4.9 %fusion.12 = f32[16,3,8,128,1]{3,0,4,2,1:T(8,128)S(1)} fusion(f32[128,7,8,128]{3,2,1,0:T(8,128)} %bitcast.19, f32[16,3,128,7,1]{2,3,0,1,4:T(8,128)S(1)} %convolution_bitcast_fusion), kind=kOutput, calls=%fused_computation.14 | convolution fusion | flops 528482304 | bytes 4038656 | tf_op jit(solution)/shard_map/rjtg,tgic->rjic/dot_general | solution.py:168
  113.4 0.8 fusion.20
  114.3 2.0 %fusion.19 = f32[6,16,16,128]{3,2,1,0:T(8,128)} fusion(f32[6,16,17,130]{3,2,1,0:T(8,128)S(1)} %copy-done.4, f32[6,16,18,129]{3,2,1,0:T(8,128)S(1)} %copy-done.3, f32[6,16,18,130]{3,2,1,0:T(8,128)S(1)} %slice_subtract_fusion, f32[6,16,16,128]{3,1,0,2:T(8,128)S(1)} %bitcast.68, f32[16,128]{1,0:T(8,128)S(1)} %get-tuple-element.15), kind=kLoop, calls=%fused_computation.47 | loop fusion | flops 1179648 | bytes 5513216 | tf_op jit(solution)/shard_map/add | solution.py:178
  (77 shorter events, 7.4 us)
Async XLA Ops:
  0.0 13.0 %copy-start = (bf16[24,2048]{1,0:T(8,128)(2,1)S(1)}, bf16[24,2048]{1,0:T(8,128)(2,1)}, u32[]{:S(2)}) copy-start(bf16[24,2048]{1,0:T(8,128)(2,1)} %param.10) | copy-start | bytes 294916
  2.1 8.8 %copy-start.9 = (s32[1,256]{1,0:T(1,128)S(1)}, s32[1,256]{1,0:T(1,128)}, u32[]{:S(2)}) copy-start(s32[1,256]{1,0:T(1,128)} %param.12) | copy-start | bytes 3076
  2.1 8.8 %copy-start.8 = (s32[1,128]{1,0:T(1,128)S(1)}, s32[1,128]{1,0:T(1,128)}, u32[]{:S(2)}) copy-start(s32[1,128]{1,0:T(1,128)} %param.14) | copy-start | bytes 1540
  2.4 9.5 %copy-start.10 = (s32[1,256]{1,0:T(1,128)S(1)}, s32[1,256]{1,0:T(1,128)}, u32[]{:S(2)}) copy-start(s32[1,256]{1,0:T(1,128)} %param.13) | copy-start | bytes 3076
  3.0 30.7 %collective-permute-start.1 = (f32[129,64]{0,1:T(8,128)S(1)}, f32[129,64]{0,1:T(8,128)S(1)}, u32[]{:S(2)}, u32[]{:S(2)}) collective-permute-start(f32[129,64]{0,1:T(8,128)S(1)} %copy.55), channel_id=1, source_target_pairs={{0,31},{1,0},{2,1},{3,2},{4,3},{5,4},{6,5},{7,6},{8,7},{9,8},{10,9... | collective-permute-start | bytes 99080 | tf_op jit(solution)/shard_map/ppermute | solution.py:31
  10.7 22.1 %collective-permute-start = (f32[129,64]{0,1:T(8,128)S(1)}, f32[129,64]{0,1:T(8,128)S(1)}, u32[]{:S(2)}, u32[]{:S(2)}) collective-permute-start(f32[129,64]{0,1:T(8,128)S(1)} %copy.54), channel_id=1, source_target_pairs={{0,1},{1,2},{2,3},{3,4},{4,5},{5,6},{6,7},{7,8},{8,9},{9,10},{10,1... | collective-permute-start | bytes 99080 | tf_op jit(solution)/shard_map/ppermute | solution.py:28
  22.3 84.7 %all-to-all-start = ((f32[128,56,128]{2,1,0:T(8,128)}), f32[128,56,128]{2,1,0:T(8,128)}, u32[]{:S(2)}, u32[]{:S(2)}) async-start(f32[128,56,128]{2,1,0:T(8,128)} %select_select_fusion), calls=%async_computation | async-start | bytes 7340032 | tf_op jit(solution)/shard_map/all_to_all | solution.py:126
  32.8 1.7 %copy-start.2 = (f32[6,16,16,128]{3,2,1,0:T(8,128)S(1)}, f32[6,16,16,128]{3,2,1,0:T(8,128)}, u32[]{:S(2)}) copy-start(f32[6,16,16,128]{3,2,1,0:T(8,128)} %param.15) | copy-start | bytes 2359300
  40.3 40.4 %collective-permute-start.3 = (f32[129,544]{1,0:T(8,128)}, f32[129,544]{1,0:T(8,128)S(1)}, u32[]{:S(2)}, u32[]{:S(2)}) collective-permute-start(f32[129,544]{1,0:T(8,128)} %reshape.296), channel_id=1, source_target_pairs={{32,0},{64,32},{96,64},{33,1},{65,33},{97,65},{34,2},{66,34},{98,6... | collective-permute-start | bytes 842120 | tf_op jit(solution)/shard_map/ppermute | solution.py:43
  43.3 38.5 %collective-permute-start.2 = (f32[129,544]{1,0:T(8,128)}, f32[129,544]{1,0:T(8,128)}, u32[]{:S(2)}, u32[]{:S(2)}) collective-permute-start(f32[129,544]{1,0:T(8,128)} %reshape.294), channel_id=1, source_target_pairs={{0,32},{32,64},{64,96},{1,33},{33,65},{65,97},{2,34},{34,66},{66,9... | collective-permute-start | bytes 842120 | tf_op jit(solution)/shard_map/ppermute | solution.py:38
  90.9 0.9 copy-start.5
  90.9 1.0 copy-start.6
  107.0 6.4 %copy-start.7 = (f32[96,24]{0,1:T(8,128)S(1)}, f32[96,24]{0,1:T(8,128)}, u32[]{:S(2)}) copy-start(f32[96,24]{0,1:T(8,128)} %param.19) | copy-start | bytes 27652
  108.5 5.8 %copy-start.3 = (f32[6,16,18,129]{3,2,1,0:T(8,128)S(1)}, f32[6,16,18,129]{3,2,1,0:T(8,128)}, u32[]{:S(2)}) copy-start(f32[6,16,18,129]{3,2,1,0:T(8,128)} %subtract_multiply_fusion.1) | copy-start | bytes 2674948
  108.5 5.8 %copy-start.4 = (f32[6,16,17,130]{3,2,1,0:T(8,128)S(1)}, f32[6,16,17,130]{3,2,1,0:T(8,128)}, u32[]{:S(2)}) copy-start(f32[6,16,17,130]{3,2,1,0:T(8,128)} %subtract_multiply_fusion) | copy-start | bytes 2545924
  114.3 2.0 %copy-start.1 = (bf16[24,2048]{1,0:T(8,128)(2,1)S(1)}, bf16[24,2048]{1,0:T(8,128)(2,1)}, u32[]{:S(2)}) copy-start(bf16[24,2048]{1,0:T(8,128)(2,1)} %param.10) | copy-start | bytes 294916

commit v10 on v8

--- a/solution.py
+++ b/solution.py
@@ -21,29 +21,40 @@
     return pairs
 
 
-def with_halo(block, width):
+def with_halo(parts, width):
     lon_count = lax.axis_size("lon")
     lat_count = lax.axis_size("lat")
-    planes, rows, cols = block.shape
+    rows, cols = parts[0].shape[-2:]
+    planes = sum(p.shape[0] for p in parts)
+    east_edge = jnp.concatenate([p[..., -width:] for p in parts], axis=0)
+    west_edge = jnp.concatenate([p[..., :width] for p in parts], axis=0)
     west = lax.ppermute(
-        block[..., -width:].reshape(planes, rows * width), "lon", shifted_pairs(lon_count, 1, True)
+        east_edge.reshape(planes, rows * width), "lon", shifted_pairs(lon_count, 1, True)
     )
     east = lax.ppermute(
-        block[..., :width].reshape(planes, rows * width), "lon", shifted_pairs(lon_count, -1, True)
+        west_edge.reshape(planes, rows * width), "lon", shifted_pairs(lon_count, -1, True)
     )
+    west_flat, east_flat = west, east
     west = west.reshape(planes, rows, width)
     east = east.reshape(planes, rows, width)
-    middle = jnp.concatenate([west, block, east], axis=-1)
     wide_cols = cols + 2 * width
-    south = lax.ppermute(
-        middle[:, -width:, :].reshape(planes, width * wide_cols),
-        "lat",
-        shifted_pairs(lat_count, 1, False),
-    )
-    north = lax.ppermute(
-        middle[:, :width, :].reshape(planes, width * wide_cols),
-        "lat",
-        shifted_pairs(lat_count, -1, False),
+    top_rows = jnp.concatenate([p[:, -width:, :] for p in parts], axis=0)
+    bottom_rows = jnp.concatenate([p[:, :width, :] for p in parts], axis=0)
+    top = jnp.concatenate(
+        [west[:, -width:, :], top_rows, east[:, -width:, :]], axis=-1
+    ).reshape(planes, width * wide_cols)
+    bottom = jnp.concatenate(
+        [west[:, :width, :], bottom_rows, east[:, :width, :]], axis=-1
+    ).reshape(planes, width * wide_cols)
+    south = lax.ppermute(top, "lat", shifted_pairs(lat_count, 1, False))
+    north = lax.ppermute(bottom, "lat", shifted_pairs(lat_count, -1, False))
+    middle = jnp.concatenate(
+        [
+            west_flat.reshape(planes, rows, width),
+            jnp.concatenate(parts, axis=0),
+            east_flat.reshape(planes, rows, width),
+        ],
+        axis=-1,
     )
     south = south.reshape(planes, width, wide_cols)
     north = north.reshape(planes, width, wide_cols)
@@ -106,9 +117,7 @@
     diagonal.append(jnp.zeros((tile_count, 8, slot_count * block_cells), chosen.dtype))
     lhs = jnp.concatenate(diagonal, axis=1)
     stacked_weights = remap_weights[0].reshape(tile_count, slot_count * block_cells, block_cells)
-    product = jnp.einsum(
-        "trb,tbc->trc", lhs, stacked_weights, preferred_element_type=jnp.float32
-    )
+    product = jnp.einsum("trb,tbc->trc", lhs, stacked_weights, preferred_element_type=jnp.float32)
     row_ids = jnp.arange(slot_count * field_count + 8)
     slot_of_row = row_ids // field_count
     live_rows = is_live.reshape(tile_count, slot_count)
@@ -131,15 +140,12 @@
 
     sea_here = land_mask.astype(jnp.float32)
     planes = tracer_count * level_count
-    stacked = jnp.concatenate(
-        [
-            tracers.reshape(planes, lat_rows, lon_cols),
-            east_velocity,
-            north_velocity,
-            sea_here[None],
-        ],
-        axis=0,
-    )
+    stacked = [
+        tracers.reshape(planes, lat_rows, lon_cols),
+        east_velocity,
+        north_velocity,
+        sea_here[None],
+    ]
     wide = with_halo(stacked, NSUB)
     tracer_now = wide[:planes].reshape(tracer_count, level_count, lat_rows + 2 * NSUB, lon_cols + 2 * NSUB)
     east_wide = wide[planes : planes + level_count]

time: 101 us -> 101 us (level)
  local copies, waits for them, and re-layouts: 17.4 us -> 22.7 us
  other arithmetic: 31.6 us -> 28.3 us
  waiting for transfers between devices: 21.3 us -> 18 us
  starting transfers between devices: 19.9 us -> 21.5 us
    slice x1 -> x19, local copies, waits for them, and re-layouts: 0.34 us -> 5.93 us  [the longest x7 3.06 us: with_halo(): east_edge = jnp.concatenate([p[..., -width:] for p in parts], axis=0)]
    slice x1 -> x0, other arithmetic: 2.64 us -> none  [with_halo(): middle[:, -width:, :].reshape(planes, width * wide_cols)]
    all_to_all x1, waiting for transfers between devices: 19.2 us -> 16.7 us  [coupled_step(): lax.all_to_all(sent, ('lat', 'lon'), split_axis=0, concat_axis=0, tiled=T...]
    reshape x6 -> x4, local copies, waits for them, and re-layouts: 4.3 us -> 2.22 us  [the longest x1 1.1 us: with_halo(): bottom = jnp.concatenate([west[:, :width, :], bottom_rows, east[:, :width...]
    all_to_all x1, starting transfers between devices: 8.04 us -> 9.62 us  [coupled_step(): lax.all_to_all(sent, ('lat', 'lon'), split_axis=0, concat_axis=0, tiled=T...]
  transfers between devices with their start and end apart: 5 -> 5, of which waited for: 2 -> 2; matrix products, arithmetic and copies ran while one was open for 41% -> 43% of each run, Pallas kernels for 0% -> 0%
where the time goes in v10:
time: 101 us
  other arithmetic  28.3 us (28%)
  local copies, waits for them, and re-layouts  22.7 us (22%)
  starting transfers between devices  21.5 us (21%)
  waiting for transfers between devices  18 us (18%)
  matrix products  9.54 us (9%)
    all_to_all x1, waiting for transfers between devices, coupled_step(): lax.all_to_all(sent, ('lat', 'lon'), split_axis=0, concat_axis=0, tiled=T...  16.7 us
    all_to_all x1, starting transfers between devices, coupled_step(): lax.all_to_all(sent, ('lat', 'lon'), split_axis=0, concat_axis=0, tiled=T...  9.62 us
    sub x3, other arithmetic, advect(): inner + east_flow[..., 1:-1, :-1] - east_flow[..., 1:-1, 1:]  7.8 us
    dot_general x1, matrix products, coupled_step(): jnp.einsum('trb,tbc->trc', lhs, stacked_weights, preferred_element_type=j...  7.38 us
    ppermute x1, starting transfers between devices, with_halo(): lax.ppermute(west_edge.reshape(planes, rows * width), 'lon', shifted_pair...  6.74 us
    concatenate x2, other arithmetic, with_halo(): return jnp.concatenate([south, middle, north], axis=-2)  5.39 us
    mul x4, other arithmetic, advect(): mask_east * (east_speed[:, :, :-1] * (tracer_now[..., :-1] + tracer_now[....  4.21 us
    mul x4, other arithmetic, advect(): mask_north * (north_speed[:, :-1, :] * (tracer_now[..., :-1, :] + tracer_...  4.14 us
  transfers between devices with their start and end apart: 5, of which 2 were waited for; matrix products, arithmetic and copies ran while one was open for 43% of the time, Pallas kernels for 0%

profile of v10, /device:TPU:0, one launch (start us, length us, event | category | flops | bytes accessed | tf_op | source)
XLA Modules:
  0.0 100.7 jit_solution(5457023054100758601)
XLA Ops:
  0.0 0.8 fusion.40
  1.1 1.1 %fusion.36 = (f32[16,16,4]{2,1,0:T(8,128)S(1)}, f32[16,16,4]{2,1,0:T(8,128)S(1)}) fusion(f32[16,16,128]{2,1,0:T(8,128)} %param.16), kind=kLoop, calls=%fused_computation.111 | loop fusion | bytes 16384 | tf_op jit(solution)/shard_map/slice | solution.py:29
  2.3 1.1 %fusion.37 = (f32[16,16,4]{2,1,0:T(8,128)S(1)}, f32[16,16,4]{2,1,0:T(8,128)S(1)}) fusion(f32[16,16,128]{2,1,0:T(8,128)} %param.17), kind=kLoop, calls=%fused_computation.112 | loop fusion | bytes 16384 | tf_op jit(solution)/shard_map/slice | solution.py:29
  4.4 6.7 %collective-permute-start.1 = (f32[129,64]{0,1:T(8,128)S(1)}, f32[129,64]{0,1:T(8,128)S(1)}, u32[]{:S(2)}, u32[]{:S(2)}) collective-permute-start(f32[129,64]{0,1:T(8,128)S(1)} %reshape.262), channel_id=1, source_target_pairs={{0,31},{1,0},{2,1},{3,2},{4,3},{5,4},{6,5},{7,6},{8,7},{9,8},{10,9... | collective-permute-start | bytes 99080 | tf_op jit(solution)/shard_map/ppermute | solution.py:34
  15.7 1.0 gather_fusion
  16.7 0.9 broadcast_select_fusion
  17.6 1.4 %slice_bitcast_fusion.1 = (bf16[128,24,128]{2,1,0:T(8,128)(2,1)}, bf16[128,24,128]{2,1,0:T(8,128)(2,1)}) fusion(bf16[128,2,24,128]{3,2,1,0:T(8,128)(2,1)S(1)} %bitcast.55), kind=kLoop, calls=%fused_computation.42 | loop fusion | bytes 3145728 | tf_op jit(solution)/shard_map/squeeze | solution.py:114
  19.5 1.3 %collective-permute-done = f32[129,64]{0,1:T(8,128)S(1)} collective-permute-done((f32[129,64]{0,1:T(8,128)S(1)}, f32[129,64]{0,1:T(8,128)S(1)}, u32[]{:S(2)}, u32[]{:S(2)}) %collective-permute-start) | collective-permute-done | bytes 33056 | tf_op jit(solution)/shard_map/ppermute | solution.py:31
  21.9 1.1 %reshape.264 = f32[129,544]{1,0:T(8,128)} reshape(f32[129,4,136]{2,1,0:T(4,128)S(1)} %pad_maximum_fusion.1) | data formatting | bytes 561408 | tf_op jit(solution)/shard_map/reshape | solution.py:45
  24.0 1.1 %reshape.266 = f32[129,544]{1,0:T(8,128)} reshape(f32[129,4,136]{2,1,0:T(4,128)S(1)} %pad_maximum_fusion.2) | data formatting | bytes 561408 | tf_op jit(solution)/shard_map/reshape | solution.py:48
  25.1 1.3 %collective-permute-start.3 = (f32[129,544]{1,0:T(8,128)}, f32[129,544]{1,0:T(8,128)}, u32[]{:S(2)}, u32[]{:S(2)}) collective-permute-start(f32[129,544]{1,0:T(8,128)} %reshape.266), channel_id=1, source_target_pairs={{32,0},{64,32},{96,64},{33,1},{65,33},{97,65},{34,2},{66,34},{98,6... | collective-permute-start | bytes 842120 | tf_op jit(solution)/shard_map/ppermute | solution.py:50
  26.4 3.8 %collective-permute-start.2 = (f32[129,544]{1,0:T(8,128)}, f32[129,544]{1,0:T(8,128)}, u32[]{:S(2)}, u32[]{:S(2)}) collective-permute-start(f32[129,544]{1,0:T(8,128)} %reshape.264), channel_id=1, source_target_pairs={{0,32},{32,64},{64,96},{1,33},{33,65},{65,97},{2,34},{34,66},{66,9... | collective-permute-start | bytes 842120 | tf_op jit(solution)/shard_map/ppermute | solution.py:49
  30.2 7.4 %select_select_fusion = f32[128,56,128]{2,1,0:T(8,128)} fusion(f32[128,56]{1,0:T(8,128)S(1)} %select_select_fusion.1, pred[56]{0:T(512)(128)(4,1)S(1)} %iota_compare_fusion.6, pred[128,56]{1,0:T(8,128)(4,1)S(1)} %copy.64, bf16[128,256,128]{2,1,0:T(8,128)(2,1)} %bitcast.61, bf16[128,24,128]{2,1,0:T(8,128)(2,1)} %get-tuple-element.10, ...), kind=kOutput, calls=%fused_computation.14 | convolution fusion | flops 493617152 | bytes 13667496 | tf_op jit(solution)/shard_map/trb,tbc->trc/dot_general | solution.py:120
  37.5 9.6 %all-to-all-start = ((f32[128,56,128]{2,1,0:T(8,128)}), f32[128,56,128]{2,1,0:T(8,128)}, u32[]{:S(2)}, u32[]{:S(2)}) async-start(f32[128,56,128]{2,1,0:T(8,128)} %select_select_fusion), calls=%async_computation | async-start | bytes 7340032 | tf_op jit(solution)/shard_map/all_to_all | solution.py:137
  47.2 0.8 copy.60
  48.0 0.8 copy.61
  48.7 2.2 %reshape.267 = f32[129,4,136]{2,1,0:T(4,128)} reshape(f32[129,544]{1,0:T(8,128)} %collective-permute-done.3) | data formatting | bytes 561408 | tf_op jit(solution)/shard_map/reshape | solution.py:60
  50.9 1.4 %reshape.265 = f32[129,4,136]{2,1,0:T(4,128)S(1)} reshape(f32[129,544]{1,0:T(8,128)} %collective-permute-done.2) | data formatting | bytes 561408 | tf_op jit(solution)/shard_map/reshape | solution.py:59
  52.3 5.1 %pad_maximum_fusion = f32[129,24,136]{2,1,0:T(8,128)S(1)} fusion(f32[129,4,136]{2,1,0:T(4,128)} %reshape.267, f32[129,16,4]{2,1,0:T(8,128)S(1)} %copy.61, f32[1,16,128]{2,1,0:T(8,128)S(1)} %get-tuple-element.28, f32[16,16,128]{2,1,0:T(8,128)} %param.17, f32[16,16,128]{2,1,0:T(8,128)} %param.16, f32[96,16,128]{2,1,0:T(8,128)S(1)} %bitcast.52, ...), kind=kLoop, calls=%fused_computation.15 | loop fusion | flops 2947392 | bytes 3368448 | tf_op jit(solution)/shard_map/concatenate | solution.py:61
  59.8 0.7 subtract_multiply_fusion.6
  61.1 2.5 %slice_subtract_fusion.4 = f32[6,16,22,134]{3,2,1,0:T(8,128)S(1)} fusion(f32[6,16,23,136]{3,2,1,0:T(8,128)S(1)} %subtract_multiply_fusion.6, f32[6,16,24,135]{3,2,1,0:T(8,128)S(1)} %subtract_multiply_fusion.7, f32[6,16,24,136]{3,2,1,0:T(8,128)S(1)} %bitcast.49), kind=kLoop, calls=%fused_computation.26 | loop fusion | flops 1132032 | bytes 6792192 | tf_op jit(solution)/shard_map/sub | solution.py:77
  64.3 0.7 subtract_multiply_fusion.4
  65.0 2.5 %slice_subtract_fusion.2 = f32[6,16,20,132]{3,2,1,0:T(8,128)S(1)} fusion(f32[6,16,21,134]{3,2,1,0:T(8,128)S(1)} %subtract_multiply_fusion.4, f32[6,16,22,133]{3,2,1,0:T(8,128)S(1)} %subtract_multiply_fusion.5, f32[6,16,22,134]{3,2,1,0:T(8,128)S(1)} %slice_subtract_fusion.4), kind=kLoop, calls=%fused_computation.22 | loop fusion | flops 1013760 | bytes 6082560 | tf_op jit(solution)/shard_map/sub | solution.py:77
  68.9 2.7 %slice_subtract_fusion = f32[6,16,18,130]{3,2,1,0:T(8,128)S(1)} fusion(f32[6,16,19,132]{3,2,1,0:T(8,128)S(1)} %subtract_multiply_fusion.2, f32[6,16,20,131]{3,2,1,0:T(8,128)S(1)} %subtract_multiply_fusion.3, f32[6,16,20,132]{3,2,1,0:T(8,128)S(1)} %slice_subtract_fusion.2), kind=kLoop, calls=%fused_computation.18 | loop fusion | flops 898560 | bytes 5391360 | tf_op jit(solution)/shard_map/sub | solution.py:77
  71.7 2.2 %subtract_multiply_fusion.1 = f32[6,16,18,129]{3,2,1,0:T(8,128)} fusion(f32[6,16,18,130]{3,2,1,0:T(8,128)S(1)} %slice_subtract_fusion, f32[16,18,129]{2,1,0:T(8,128)S(1)} %slice.494, f32[18,129]{1,0:T(8,128)S(1)} %slice_multiply_fusion.1), kind=kLoop, calls=%fused_computation.31 | loop fusion | flops 1560384 | bytes 2832840 | tf_op jit(solution)/shard_map/mul | solution.py:66
  73.8 2.1 %subtract_multiply_fusion = f32[6,16,17,130]{3,2,1,0:T(8,128)} fusion(f32[6,16,18,130]{3,2,1,0:T(8,128)S(1)} %slice_subtract_fusion, f32[16,17,130]{2,1,0:T(8,128)S(1)} %pad_maximum_fusion.3, f32[17,130]{1,0:T(8,128)S(1)} %slice_multiply_fusion), kind=kLoop, calls=%fused_computation.30 | loop fusion | flops 1485120 | bytes 2696200 | tf_op jit(solution)/shard_map/mul | solution.py:71
  75.9 16.7 %all-to-all-done = f32[128,56,128]{2,1,0:T(8,128)} async-done(((f32[128,56,128]{2,1,0:T(8,128)}), f32[128,56,128]{2,1,0:T(8,128)}, u32[]{:S(2)}, u32[]{:S(2)}) %all-to-all-start) | async-done | bytes 3670048 | tf_op jit(solution)/shard_map/all_to_all | solution.py:137
  92.6 1.3 %slice_reduce_fusion = f32[128,2]{1,0:T(8,128)S(1)} fusion(f32[128,56,128]{2,1,0:T(8,128)} %all-to-all-done), kind=kLoop, calls=%fused_computation.59 | loop fusion | bytes 2048 | tf_op jit(solution)/shard_map/slice | solution.py:138
  94.0 2.3 %slice.512 = f32[128,48,128]{2,1,0:T(8,128)S(1)} slice(f32[128,56,128]{2,1,0:T(8,128)} %all-to-all-done), slice={[0:128], [0:48], [0:128]} | slice | bytes 6291456 | tf_op jit(solution)/shard_map/slice | solution.py:139
  96.3 1.3 %fusion.12 = f32[16,24,128]{2,0,1:T(8,128)S(1)} fusion(f32[256,24,128]{2,1,0:T(8,128)S(1)} %bitcast.54, f32[256]{0:T(256)S(1)} %eq.55), kind=kOutput, calls=%fused_computation.16 | convolution fusion | flops 150999040 | bytes 3343360 | tf_op jit(solution)/shard_map/rk,kfc->rfc/dot_general | solution.py:170
  97.6 0.8 fusion.19
  98.5 2.2 %fusion.18 = f32[6,16,16,128]{3,2,1,0:T(8,128)} fusion(f32[6,16,17,130]{3,2,1,0:T(8,128)S(1)} %copy-done.4, f32[6,16,18,129]{3,2,1,0:T(8,128)S(1)} %copy-done.3, f32[6,16,18,130]{3,2,1,0:T(8,128)S(1)} %slice_subtract_fusion, f32[6,16,16,128]{3,1,0,2:T(8,128)S(1)} %bitcast.56, f32[16,128]{1,0:T(8,128)S(1)} %get-tuple-element.27), kind=kLoop, calls=%fused_computation.44 | loop fusion | flops 1179648 | bytes 5513216 | tf_op jit(solution)/shard_map/add | solution.py:177
  (107 shorter events, 13.3 us)
Async XLA Ops:
  0.0 15.7 %copy-start = (bf16[24,2048]{1,0:T(8,128)(2,1)S(1)}, bf16[24,2048]{1,0:T(8,128)(2,1)}, u32[]{:S(2)}) copy-start(bf16[24,2048]{1,0:T(8,128)(2,1)} %param.10) | copy-start | bytes 294916
  0.0 3.6 %copy-start.2 = (f32[6,16,16,128]{3,2,1,0:T(8,128)S(1)}, f32[6,16,16,128]{3,2,1,0:T(8,128)}, u32[]{:S(2)}) copy-start(f32[6,16,16,128]{3,2,1,0:T(8,128)} %param.15) | copy-start | bytes 2359300
  3.6 9.4 %copy-start.5 = (f32[16,16,128]{2,1,0:T(8,128)S(1)}, f32[16,16,128]{2,1,0:T(8,128)}, u32[]{:S(2)}) copy-start(f32[16,16,128]{2,1,0:T(8,128)} %param.17) | copy-start | bytes 393220
  3.6 9.4 %copy-start.7 = (f32[16,16,128]{2,1,0:T(8,128)S(1)}, f32[16,16,128]{2,1,0:T(8,128)}, u32[]{:S(2)}) copy-start(f32[16,16,128]{2,1,0:T(8,128)} %param.16) | copy-start | bytes 393220
  3.9 9.9 %copy-start.15 = (s32[1,256]{1,0:T(1,128)S(1)}, s32[1,256]{1,0:T(1,128)}, u32[]{:S(2)}) copy-start(s32[1,256]{1,0:T(1,128)} %param.12) | copy-start | bytes 3076
  3.9 9.9 %copy-start.14 = (s32[1,128]{1,0:T(1,128)S(1)}, s32[1,128]{1,0:T(1,128)}, u32[]{:S(2)}) copy-start(s32[1,128]{1,0:T(1,128)} %param.14) | copy-start | bytes 1540
  3.9 10.7 %copy-start.16 = (s32[1,256]{1,0:T(1,128)S(1)}, s32[1,256]{1,0:T(1,128)}, u32[]{:S(2)}) copy-start(s32[1,256]{1,0:T(1,128)} %param.13) | copy-start | bytes 3076
  4.4 15.0 %collective-permute-start.1 = (f32[129,64]{0,1:T(8,128)S(1)}, f32[129,64]{0,1:T(8,128)S(1)}, u32[]{:S(2)}, u32[]{:S(2)}) collective-permute-start(f32[129,64]{0,1:T(8,128)S(1)} %reshape.262), channel_id=1, source_target_pairs={{0,31},{1,0},{2,1},{3,2},{4,3},{5,4},{6,5},{7,6},{8,7},{9,8},{10,9... | collective-permute-start | bytes 99080 | tf_op jit(solution)/shard_map/ppermute | solution.py:34
  12.3 8.6 %collective-permute-start = (f32[129,64]{0,1:T(8,128)S(1)}, f32[129,64]{0,1:T(8,128)S(1)}, u32[]{:S(2)}, u32[]{:S(2)}) collective-permute-start(f32[129,64]{0,1:T(8,128)S(1)} %reshape.260), channel_id=1, source_target_pairs={{0,1},{1,2},{2,3},{3,4},{4,5},{5,6},{6,7},{7,8},{8,9},{9,10},{10,1... | collective-permute-start | bytes 99080 | tf_op jit(solution)/shard_map/ppermute | solution.py:31
  19.0 4.4 %copy-start.10 = (f32[16,4,128]{2,1,0:T(4,128)S(1)}, f32[16,4,128]{2,1,0:T(4,128)}, u32[]{:S(2)}) copy-start(f32[16,4,128]{2,1,0:T(4,128)} %get-tuple-element.16) | copy-start | bytes 98308
  19.0 4.4 %copy-start.11 = (f32[16,4,128]{2,1,0:T(4,128)S(1)}, f32[16,4,128]{2,1,0:T(4,128)}, u32[]{:S(2)}) copy-start(f32[16,4,128]{2,1,0:T(4,128)} %get-tuple-element.33) | copy-start | bytes 98308
  19.0 4.4 %copy-start.13 = (f32[1,4,128]{2,1,0:T(4,128)S(1)}, f32[1,4,128]{2,1,0:T(4,128)}, u32[]{:S(2)}) copy-start(f32[1,4,128]{2,1,0:T(4,128)} %get-tuple-element.30) | copy-start | bytes 6148
  21.9 8.3 %copy-start.9 = (bf16[128,24,128]{2,1,0:T(8,128)(2,1)S(1)}, bf16[128,24,128]{2,1,0:T(8,128)(2,1)}, u32[]{:S(2)}) copy-start(bf16[128,24,128]{2,1,0:T(8,128)(2,1)} %get-tuple-element.9) | copy-start | bytes 2359300
  25.1 23.7 %collective-permute-start.3 = (f32[129,544]{1,0:T(8,128)}, f32[129,544]{1,0:T(8,128)}, u32[]{:S(2)}, u32[]{:S(2)}) collective-permute-start(f32[129,544]{1,0:T(8,128)} %reshape.266), channel_id=1, source_target_pairs={{32,0},{64,32},{96,64},{33,1},{65,33},{97,65},{34,2},{66,34},{98,6... | collective-permute-start | bytes 842120 | tf_op jit(solution)/shard_map/ppermute | solution.py:50
  26.4 24.5 %collective-permute-start.2 = (f32[129,544]{1,0:T(8,128)}, f32[129,544]{1,0:T(8,128)}, u32[]{:S(2)}, u32[]{:S(2)}) collective-permute-start(f32[129,544]{1,0:T(8,128)} %reshape.264), channel_id=1, source_target_pairs={{0,32},{32,64},{64,96},{1,33},{33,65},{65,97},{2,34},{34,66},{66,9... | collective-permute-start | bytes 842120 | tf_op jit(solution)/shard_map/ppermute | solution.py:49
  37.5 55.1 %all-to-all-start = ((f32[128,56,128]{2,1,0:T(8,128)}), f32[128,56,128]{2,1,0:T(8,128)}, u32[]{:S(2)}, u32[]{:S(2)}) async-start(f32[128,56,128]{2,1,0:T(8,128)} %select_select_fusion), calls=%async_computation | async-start | bytes 7340032 | tf_op jit(solution)/shard_map/all_to_all | solution.py:137
  59.8 0.9 copy-start.6
  59.8 1.0 copy-start.8
  94.0 4.5 %copy-start.4 = (f32[6,16,17,130]{3,2,1,0:T(8,128)S(1)}, f32[6,16,17,130]{3,2,1,0:T(8,128)}, u32[]{:S(2)}) copy-start(f32[6,16,17,130]{3,2,1,0:T(8,128)} %subtract_multiply_fusion) | copy-start | bytes 2545924
  96.3 1.4 %copy-start.12 = (f32[96,24]{0,1:T(8,128)S(1)}, f32[96,24]{0,1:T(8,128)}, u32[]{:S(2)}) copy-start(f32[96,24]{0,1:T(8,128)} %param.19) | copy-start | bytes 27652
  96.3 2.2 %copy-start.3 = (f32[6,16,18,129]{3,2,1,0:T(8,128)S(1)}, f32[6,16,18,129]{3,2,1,0:T(8,128)}, u32[]{:S(2)}) copy-start(f32[6,16,18,129]{3,2,1,0:T(8,128)} %subtract_multiply_fusion.1) | copy-start | bytes 2674948
  98.5 2.2 %copy-start.1 = (bf16[24,2048]{1,0:T(8,128)(2,1)S(1)}, bf16[24,2048]{1,0:T(8,128)(2,1)}, u32[]{:S(2)}) copy-start(bf16[24,2048]{1,0:T(8,128)(2,1)} %param.10) | copy-start | bytes 294916

commit v11 on v8

--- a/solution.py
+++ b/solution.py
@@ -33,18 +33,16 @@
     )
     west = west.reshape(planes, rows, width)
     east = east.reshape(planes, rows, width)
+    wide_cols = cols + 2 * width
+    top = jnp.concatenate(
+        [west[:, -width:, :], block[:, -width:, :], east[:, -width:, :]], axis=-1
+    ).reshape(planes, width * wide_cols)
+    bottom = jnp.concatenate(
+        [west[:, :width, :], block[:, :width, :], east[:, :width, :]], axis=-1
+    ).reshape(planes, width * wide_cols)
+    south = lax.ppermute(top, "lat", shifted_pairs(lat_count, 1, False))
+    north = lax.ppermute(bottom, "lat", shifted_pairs(lat_count, -1, False))
     middle = jnp.concatenate([west, block, east], axis=-1)
-    wide_cols = cols + 2 * width
-    south = lax.ppermute(
-        middle[:, -width:, :].reshape(planes, width * wide_cols),
-        "lat",
-        shifted_pairs(lat_count, 1, False),
-    )
-    north = lax.ppermute(
-        middle[:, :width, :].reshape(planes, width * wide_cols),
-        "lat",
-        shifted_pairs(lat_count, -1, False),
-    )
     south = south.reshape(planes, width, wide_cols)
     north = north.reshape(planes, width, wide_cols)
     return jnp.concatenate([south, middle, north], axis=-2)
@@ -162,11 +160,11 @@
         jnp.float32
     )
     ocean_flux = jnp.einsum(
-        "rk,kfc->rfc", chooser, arrived, precision=lax.Precision.HIGHEST,
+        "rk,kfc->rfc", chooser, arrived, precision=lax.Precision.HIGH,
         preferred_element_type=jnp.float32,
     )
     source = jnp.einsum(
-        "pf,ifj->pij", coupling, ocean_flux, precision=lax.Precision.HIGHEST
+        "pf,ifj->pij", coupling, ocean_flux, precision=lax.Precision.HIGH
     ).reshape(tracer_count, level_count, lat_rows, lon_cols)
     return tracer_now + sea_here * source
 

time: 101 us -> 96.6 us (0.956)
  other arithmetic: 31.6 us -> 29.3 us
  waiting for transfers between devices: 21.3 us -> 19.5 us
    slice x1 -> x0, other arithmetic: 2.64 us -> none  [with_halo(): middle[:, -width:, :].reshape(planes, width * wide_cols)]
    all_to_all x1, waiting for transfers between devices: 19.2 us -> 16.6 us  [coupled_step(): lax.all_to_all(sent, ('lat', 'lon'), split_axis=0, concat_axis=0, tiled=T...]
    reshape x2, local copies, waits for them, and re-layouts: 3.2 us -> 1.38 us  [the longest x1 1.06 us: with_halo(): bottom = jnp.concatenate([west[:, :width, :], block[:, :width, :], east[:...]
    slice x0 -> x7, local copies, waits for them, and re-layouts: none -> 1.08 us  [the longest x2 0.25 us: with_halo(): east[:, -width:, :]]
  transfers between devices with their start and end apart: 5 -> 5, of which waited for: 2 -> 2; matrix products, arithmetic and copies ran while one was open for 41% -> 44% of each run, Pallas kernels for 0% -> 0%
where the time goes in v11:
time: 96.6 us; the launch traced here: 95.8 us
  other arithmetic  29.3 us (30%)
  starting transfers between devices  19.8 us (20%)
  waiting for transfers between devices  19.5 us (20%)
  local copies, waits for them, and re-layouts  17.7 us (18%)
  matrix products  8.85 us (9%)
    all_to_all x1, waiting for transfers between devices, coupled_step(): lax.all_to_all(sent, ('lat', 'lon'), split_axis=0, concat_axis=0, tiled=T...  16.6 us
    all_to_all x1, starting transfers between devices, coupled_step(): lax.all_to_all(sent, ('lat', 'lon'), split_axis=0, concat_axis=0, tiled=T...  7.87 us
    sub x3, other arithmetic, advect(): inner + east_flow[..., 1:-1, :-1] - east_flow[..., 1:-1, 1:]  7.8 us
    dot_general x1, matrix products, coupled_step(): jnp.einsum('trb,tbc->trc', lhs, stacked_weights, preferred_element_type=j...  7.4 us
    ppermute x1, starting transfers between devices, with_halo(): lax.ppermute(block[..., :width].reshape(planes, rows * width), 'lon', shi...  6.74 us
    concatenate x2, other arithmetic, with_halo(): return jnp.concatenate([south, middle, north], axis=-2)  5.58 us
    mul x4, other arithmetic, advect(): mask_east * (east_speed[:, :, :-1] * (tracer_now[..., :-1] + tracer_now[....  4.23 us
    mul x4, other arithmetic, advect(): mask_north * (north_speed[:, :-1, :] * (tracer_now[..., :-1, :] + tracer_...  4.15 us
  transfers between devices with their start and end apart: 5, of which 2 were waited for; matrix products, arithmetic and copies ran while one was open for 44% of the time, Pallas kernels for 0%

profile of v11, /device:TPU:0, one launch (start us, length us, event | category | flops | bytes accessed | tf_op | source)
XLA Modules:
  0.0 95.8 jit_solution(6985042691437868853)
XLA Ops:
  0.0 0.7 fusion.36
  0.7 1.3 %pad_maximum_fusion.1 = f32[129,16,128]{2,1,0:T(8,128)S(1)} fusion(f32[1,16,128]{2,1,0:T(8,128)S(1)} %get-tuple-element.20, f32[16,16,128]{2,1,0:T(8,128)} %param.17, f32[16,16,128]{2,1,0:T(8,128)} %param.16, f32[96,16,128]{2,1,0:T(8,128)} %bitcast.47), kind=kLoop, calls=%fused_computation.41 | loop fusion | flops 792576 | bytes 2113536 | tf_op jit(solution)/shard_map/concatenate | solution.py:132
  3.0 6.7 %collective-permute-start.1 = (f32[129,64]{0,1:T(8,128)S(1)}, f32[129,64]{0,1:T(8,128)S(1)}, u32[]{:S(2)}, u32[]{:S(2)}) collective-permute-start(f32[129,64]{0,1:T(8,128)S(1)} %copy.54), channel_id=1, source_target_pairs={{0,31},{1,0},{2,1},{3,2},{4,3},{5,4},{6,5},{7,6},{8,7},{9,8},{10,9... | collective-permute-start | bytes 99080 | tf_op jit(solution)/shard_map/ppermute | solution.py:31
  12.5 1.0 %gather_fusion = bf16[256,24,128]{2,1,0:T(8,128)(2,1)S(1)} fusion(bf16[24,16,128]{2,0,1:T(8,128)(2,1)S(1)} %copy_bitcast_fusion, s32[1024]{0:T(1024)S(1)} %pad_clamp_fusion), kind=kCustom, calls=%fused_computation | custom fusion | bytes 3146752 | tf_op jit(solution)/shard_map/jit(_take)/gather | solution.py:94
  13.5 0.9 broadcast_select_fusion
  14.4 1.2 %slice_bitcast_fusion.1 = (bf16[128,24,128]{2,1,0:T(8,128)(2,1)S(1)}, bf16[128,24,128]{2,1,0:T(8,128)(2,1)}) fusion(bf16[128,2,24,128]{3,2,1,0:T(8,128)(2,1)S(1)} %bitcast.50), kind=kLoop, calls=%fused_computation.43 | loop fusion | bytes 3145728 | tf_op jit(solution)/shard_map/squeeze | solution.py:101
  16.0 2.8 %collective-permute-done = f32[129,64]{0,1:T(8,128)S(1)} collective-permute-done((f32[129,64]{0,1:T(8,128)S(1)}, f32[129,64]{0,1:T(8,128)S(1)}, u32[]{:S(2)}, u32[]{:S(2)}) %collective-permute-start) | collective-permute-done | bytes 33056 | tf_op jit(solution)/shard_map/ppermute | solution.py:28
  21.2 1.1 %reshape.264 = f32[129,544]{1,0:T(8,128)} reshape(f32[129,4,136]{2,1,0:T(4,128)S(1)} %pad_maximum_fusion.3) | data formatting | bytes 561408 | tf_op jit(solution)/shard_map/reshape | solution.py:42
  22.3 1.3 %collective-permute-start.3 = (f32[129,544]{1,0:T(8,128)}, f32[129,544]{1,0:T(8,128)}, u32[]{:S(2)}, u32[]{:S(2)}) collective-permute-start(f32[129,544]{1,0:T(8,128)} %reshape.264), channel_id=1, source_target_pairs={{32,0},{64,32},{96,64},{33,1},{65,33},{97,65},{34,2},{66,34},{98,6... | collective-permute-start | bytes 842120 | tf_op jit(solution)/shard_map/ppermute | solution.py:44
  23.6 3.8 %collective-permute-start.2 = (f32[129,544]{1,0:T(8,128)S(1)}, f32[129,544]{1,0:T(8,128)}, u32[]{:S(2)}, u32[]{:S(2)}) collective-permute-start(f32[129,544]{1,0:T(8,128)S(1)} %reshape.262), channel_id=1, source_target_pairs={{0,32},{32,64},{64,96},{1,33},{33,65},{65,97},{2,34},{34,66},{66,9... | collective-permute-start | bytes 842120 | tf_op jit(solution)/shard_map/ppermute | solution.py:43
  27.4 7.4 %select_select_fusion = f32[128,56,128]{2,1,0:T(8,128)} fusion(f32[128,56]{1,0:T(8,128)S(1)} %select_select_fusion.1, pred[56]{0:T(512)(128)(4,1)S(1)} %iota_compare_fusion.6, pred[128,56]{1,0:T(8,128)(4,1)S(1)} %copy.46, bf16[128,256,128]{2,1,0:T(8,128)(2,1)} %bitcast.56, bf16[128,24,128]{2,1,0:T(8,128)(2,1)} %get-tuple-element.10, ...), kind=kOutput, calls=%fused_computation.14 | convolution fusion | flops 493617152 | bytes 13667496 | tf_op jit(solution)/shard_map/trb,tbc->trc/dot_general | solution.py:107
  34.8 7.9 %all-to-all-start = ((f32[128,56,128]{2,1,0:T(8,128)}), f32[128,56,128]{2,1,0:T(8,128)}, u32[]{:S(2)}, u32[]{:S(2)}) async-start(f32[128,56,128]{2,1,0:T(8,128)} %select_select_fusion), calls=%async_computation | async-start | bytes 7340032 | tf_op jit(solution)/shard_map/all_to_all | solution.py:126
  42.7 0.8 copy.42
  43.5 0.8 copy.43
  44.3 2.2 %reshape.265 = f32[129,4,136]{2,1,0:T(4,128)} reshape(f32[129,544]{1,0:T(8,128)} %collective-permute-done.3) | data formatting | bytes 561408 | tf_op jit(solution)/shard_map/reshape | solution.py:47
  46.5 1.4 %reshape.263 = f32[129,4,136]{2,1,0:T(4,128)S(1)} reshape(f32[129,544]{1,0:T(8,128)} %collective-permute-done.2) | data formatting | bytes 561408 | tf_op jit(solution)/shard_map/reshape | solution.py:46
  47.9 5.3 %pad_maximum_fusion = f32[129,24,136]{2,1,0:T(8,128)S(1)} fusion(f32[129,4,136]{2,1,0:T(4,128)} %reshape.265, f32[129,16,4]{2,1,0:T(8,128)S(1)} %copy.43, f32[1,16,128]{2,1,0:T(8,128)S(1)} %get-tuple-element.20, f32[16,16,128]{2,1,0:T(8,128)} %param.17, f32[16,16,128]{2,1,0:T(8,128)} %param.16, f32[96,16,128]{2,1,0:T(8,128)S(1)} %bitcast.48, ...), kind=kLoop, calls=%fused_computation.15 | loop fusion | flops 2947392 | bytes 3368448 | tf_op jit(solution)/shard_map/concatenate | solution.py:48
  54.8 0.7 subtract_multiply_fusion.7
  55.6 0.7 subtract_multiply_fusion.6
  56.8 2.5 %slice_subtract_fusion.4 = f32[6,16,22,134]{3,2,1,0:T(8,128)S(1)} fusion(f32[6,16,23,136]{3,2,1,0:T(8,128)S(1)} %subtract_multiply_fusion.6, f32[6,16,24,135]{3,2,1,0:T(8,128)S(1)} %subtract_multiply_fusion.7, f32[6,16,24,136]{3,2,1,0:T(8,128)S(1)} %bitcast.45), kind=kLoop, calls=%fused_computation.26 | loop fusion | flops 1132032 | bytes 6792192 | tf_op jit(solution)/shard_map/sub | solution.py:64
  59.3 0.7 subtract_multiply_fusion.5
  60.0 0.7 subtract_multiply_fusion.4
  60.7 2.5 %slice_subtract_fusion.2 = f32[6,16,20,132]{3,2,1,0:T(8,128)S(1)} fusion(f32[6,16,21,134]{3,2,1,0:T(8,128)S(1)} %subtract_multiply_fusion.4, f32[6,16,22,133]{3,2,1,0:T(8,128)S(1)} %subtract_multiply_fusion.5, f32[6,16,22,134]{3,2,1,0:T(8,128)S(1)} %slice_subtract_fusion.4), kind=kLoop, calls=%fused_computation.22 | loop fusion | flops 1013760 | bytes 6082560 | tf_op jit(solution)/shard_map/sub | solution.py:64
  64.0 0.7 subtract_multiply_fusion.2
  64.6 2.7 %slice_subtract_fusion = f32[6,16,18,130]{3,2,1,0:T(8,128)S(1)} fusion(f32[6,16,19,132]{3,2,1,0:T(8,128)S(1)} %subtract_multiply_fusion.2, f32[6,16,20,131]{3,2,1,0:T(8,128)S(1)} %subtract_multiply_fusion.3, f32[6,16,20,132]{3,2,1,0:T(8,128)S(1)} %slice_subtract_fusion.2), kind=kLoop, calls=%fused_computation.18 | loop fusion | flops 898560 | bytes 5391360 | tf_op jit(solution)/shard_map/sub | solution.py:64
  67.4 2.2 %subtract_multiply_fusion.1 = f32[6,16,18,129]{3,2,1,0:T(8,128)} fusion(f32[6,16,18,130]{3,2,1,0:T(8,128)S(1)} %slice_subtract_fusion, f32[16,18,129]{2,1,0:T(8,128)S(1)} %slice.442, f32[18,129]{1,0:T(8,128)S(1)} %slice_multiply_fusion.1), kind=kLoop, calls=%fused_computation.31 | loop fusion | flops 1560384 | bytes 2832840 | tf_op jit(solution)/shard_map/mul | solution.py:53
  69.6 2.1 %subtract_multiply_fusion = f32[6,16,17,130]{3,2,1,0:T(8,128)} fusion(f32[6,16,18,130]{3,2,1,0:T(8,128)S(1)} %slice_subtract_fusion, f32[16,17,130]{2,1,0:T(8,128)S(1)} %pad_maximum_fusion.4, f32[17,130]{1,0:T(8,128)S(1)} %slice_multiply_fusion), kind=kLoop, calls=%fused_computation.30 | loop fusion | flops 1485120 | bytes 2696200 | tf_op jit(solution)/shard_map/mul | solution.py:58
  71.7 16.6 %all-to-all-done = f32[128,56,128]{2,1,0:T(8,128)} async-done(((f32[128,56,128]{2,1,0:T(8,128)}), f32[128,56,128]{2,1,0:T(8,128)}, u32[]{:S(2)}, u32[]{:S(2)}) %all-to-all-start) | async-done | bytes 3670048 | tf_op jit(solution)/shard_map/all_to_all | solution.py:126
  88.3 1.3 %slice_reduce_fusion = f32[128,2]{1,0:T(8,128)S(1)} fusion(f32[128,56,128]{2,1,0:T(8,128)} %all-to-all-done), kind=kLoop, calls=%fused_computation.60 | loop fusion | bytes 2048 | tf_op jit(solution)/shard_map/slice | solution.py:127
  89.7 2.3 %slice.460 = f32[128,48,128]{2,1,0:T(8,128)S(1)} slice(f32[128,56,128]{2,1,0:T(8,128)} %all-to-all-done), slice={[0:128], [0:48], [0:128]} | slice | bytes 6291456 | tf_op jit(solution)/shard_map/slice | solution.py:128
  92.0 0.9 fusion.12
  93.8 2.0 %fusion.18 = f32[6,16,16,128]{3,2,1,0:T(8,128)} fusion(f32[6,16,17,130]{3,2,1,0:T(8,128)S(1)} %copy-done.4, f32[6,16,18,129]{3,2,1,0:T(8,128)S(1)} %copy-done.3, f32[6,16,18,130]{3,2,1,0:T(8,128)S(1)} %slice_subtract_fusion, f32[6,16,16,128]{3,1,0,2:T(8,128)S(1)} %bitcast.51, f32[16,128]{1,0:T(8,128)S(1)} %get-tuple-element.19), kind=kLoop, calls=%fused_computation.45 | loop fusion | flops 1179648 | bytes 5513216 | tf_op jit(solution)/shard_map/add | solution.py:169
  (83 shorter events, 10.0 us)
Async XLA Ops:
  0.0 12.5 %copy-start = (bf16[24,2048]{1,0:T(8,128)(2,1)S(1)}, bf16[24,2048]{1,0:T(8,128)(2,1)}, u32[]{:S(2)}) copy-start(bf16[24,2048]{1,0:T(8,128)(2,1)} %param.10) | copy-start | bytes 294916
  2.4 8.1 %copy-start.9 = (s32[1,256]{1,0:T(1,128)S(1)}, s32[1,256]{1,0:T(1,128)}, u32[]{:S(2)}) copy-start(s32[1,256]{1,0:T(1,128)} %param.12) | copy-start | bytes 3076
  2.4 8.2 %copy-start.8 = (s32[1,128]{1,0:T(1,128)S(1)}, s32[1,128]{1,0:T(1,128)}, u32[]{:S(2)}) copy-start(s32[1,128]{1,0:T(1,128)} %param.14) | copy-start | bytes 1540
  2.5 8.9 %copy-start.10 = (s32[1,256]{1,0:T(1,128)S(1)}, s32[1,256]{1,0:T(1,128)}, u32[]{:S(2)}) copy-start(s32[1,256]{1,0:T(1,128)} %param.13) | copy-start | bytes 3076
  3.0 13.0 %collective-permute-start.1 = (f32[129,64]{0,1:T(8,128)S(1)}, f32[129,64]{0,1:T(8,128)S(1)}, u32[]{:S(2)}, u32[]{:S(2)}) collective-permute-start(f32[129,64]{0,1:T(8,128)S(1)} %copy.54), channel_id=1, source_target_pairs={{0,31},{1,0},{2,1},{3,2},{4,3},{5,4},{6,5},{7,6},{8,7},{9,8},{10,9... | collective-permute-start | bytes 99080 | tf_op jit(solution)/shard_map/ppermute | solution.py:31
  10.3 8.6 %collective-permute-start = (f32[129,64]{0,1:T(8,128)S(1)}, f32[129,64]{0,1:T(8,128)S(1)}, u32[]{:S(2)}, u32[]{:S(2)}) collective-permute-start(f32[129,64]{0,1:T(8,128)S(1)} %copy.53), channel_id=1, source_target_pairs={{0,1},{1,2},{2,3},{3,4},{4,5},{5,6},{6,7},{7,8},{8,9},{9,10},{10,1... | collective-permute-start | bytes 99080 | tf_op jit(solution)/shard_map/ppermute | solution.py:28
  22.3 22.0 %collective-permute-start.3 = (f32[129,544]{1,0:T(8,128)}, f32[129,544]{1,0:T(8,128)}, u32[]{:S(2)}, u32[]{:S(2)}) collective-permute-start(f32[129,544]{1,0:T(8,128)} %reshape.264), channel_id=1, source_target_pairs={{32,0},{64,32},{96,64},{33,1},{65,33},{97,65},{34,2},{66,34},{98,6... | collective-permute-start | bytes 842120 | tf_op jit(solution)/shard_map/ppermute | solution.py:44
  23.6 22.9 %collective-permute-start.2 = (f32[129,544]{1,0:T(8,128)S(1)}, f32[129,544]{1,0:T(8,128)}, u32[]{:S(2)}, u32[]{:S(2)}) collective-permute-start(f32[129,544]{1,0:T(8,128)S(1)} %reshape.262), channel_id=1, source_target_pairs={{0,32},{32,64},{64,96},{1,33},{33,65},{65,97},{2,34},{34,66},{66,9... | collective-permute-start | bytes 842120 | tf_op jit(solution)/shard_map/ppermute | solution.py:43
  34.8 53.5 %all-to-all-start = ((f32[128,56,128]{2,1,0:T(8,128)}), f32[128,56,128]{2,1,0:T(8,128)}, u32[]{:S(2)}, u32[]{:S(2)}) async-start(f32[128,56,128]{2,1,0:T(8,128)} %select_select_fusion), calls=%async_computation | async-start | bytes 7340032 | tf_op jit(solution)/shard_map/all_to_all | solution.py:126
  42.7 5.2 %copy-start.2 = (f32[6,16,16,128]{3,2,1,0:T(8,128)S(1)}, f32[6,16,16,128]{3,2,1,0:T(8,128)}, u32[]{:S(2)}) copy-start(f32[6,16,16,128]{3,2,1,0:T(8,128)} %param.15) | copy-start | bytes 2359300
  55.5 0.9 copy-start.5
  55.5 1.0 %copy-start.6 = (f32[16,16,128]{2,1,0:T(8,128)S(1)}, f32[16,16,128]{2,1,0:T(8,128)}, u32[]{:S(2)}) copy-start(f32[16,16,128]{2,1,0:T(8,128)} %param.16) | copy-start | bytes 393220
  89.7 3.8 %copy-start.4 = (f32[6,16,17,130]{3,2,1,0:T(8,128)S(1)}, f32[6,16,17,130]{3,2,1,0:T(8,128)}, u32[]{:S(2)}) copy-start(f32[6,16,17,130]{3,2,1,0:T(8,128)} %subtract_multiply_fusion) | copy-start | bytes 2545924
  92.0 1.0 %copy-start.7 = (f32[96,24]{0,1:T(8,128)S(1)}, f32[96,24]{0,1:T(8,128)}, u32[]{:S(2)}) copy-start(f32[96,24]{0,1:T(8,128)} %param.19) | copy-start | bytes 27652
  92.0 1.8 %copy-start.3 = (f32[6,16,18,129]{3,2,1,0:T(8,128)S(1)}, f32[6,16,18,129]{3,2,1,0:T(8,128)}, u32[]{:S(2)}) copy-start(f32[6,16,18,129]{3,2,1,0:T(8,128)} %subtract_multiply_fusion.1) | copy-start | bytes 2674948
  93.5 2.3 %copy-start.1 = (bf16[24,2048]{1,0:T(8,128)(2,1)S(1)}, bf16[24,2048]{1,0:T(8,128)(2,1)}, u32[]{:S(2)}) copy-start(bf16[24,2048]{1,0:T(8,128)(2,1)} %param.10) | copy-start | bytes 294916

commit v12 on v11

--- a/solution.py
+++ b/solution.py
@@ -24,7 +24,7 @@
 def with_halo(block, width):
     lon_count = lax.axis_size("lon")
     lat_count = lax.axis_size("lat")
-    planes, rows, cols = block.shape
+    planes, rows, _ = block.shape
     west = lax.ppermute(
         block[..., -width:].reshape(planes, rows * width), "lon", shifted_pairs(lon_count, 1, True)
     )
@@ -33,18 +33,15 @@
     )
     west = west.reshape(planes, rows, width)
     east = east.reshape(planes, rows, width)
-    wide_cols = cols + 2 * width
     top = jnp.concatenate(
         [west[:, -width:, :], block[:, -width:, :], east[:, -width:, :]], axis=-1
-    ).reshape(planes, width * wide_cols)
+    )
     bottom = jnp.concatenate(
         [west[:, :width, :], block[:, :width, :], east[:, :width, :]], axis=-1
-    ).reshape(planes, width * wide_cols)
+    )
     south = lax.ppermute(top, "lat", shifted_pairs(lat_count, 1, False))
     north = lax.ppermute(bottom, "lat", shifted_pairs(lat_count, -1, False))
     middle = jnp.concatenate([west, block, east], axis=-1)
-    south = south.reshape(planes, width, wide_cols)
-    north = north.reshape(planes, width, wide_cols)
     return jnp.concatenate([south, middle, north], axis=-2)
 
 
@@ -160,11 +157,11 @@
         jnp.float32
     )
     ocean_flux = jnp.einsum(
-        "rk,kfc->rfc", chooser, arrived, precision=lax.Precision.HIGH,
+        "rk,kfc->rfc", chooser, arrived, precision=lax.Precision.HIGHEST,
         preferred_element_type=jnp.float32,
     )
     source = jnp.einsum(
-        "pf,ifj->pij", coupling, ocean_flux, precision=lax.Precision.HIGH
+        "pf,ifj->pij", coupling, ocean_flux, precision=lax.Precision.HIGHEST
     ).reshape(tracer_count, level_count, lat_rows, lon_cols)
     return tracer_now + sea_here * source
 

time: 96.6 us -> 96.7 us (level)
  local copies, waits for them, and re-layouts: 17.7 us -> 12.4 us
  waiting for transfers between devices: 19.5 us -> 23.1 us
  other arithmetic: 29.3 us -> 31 us
    reshape x4 -> x0, local copies, waits for them, and re-layouts: 4.93 us -> none  [the longest x1 2.17 us: with_halo(): north = north.reshape(planes, width, wide_cols)]
    all_to_all x1, waiting for transfers between devices: 16.6 us -> 20.2 us  [coupled_step(): lax.all_to_all(sent, ('lat', 'lon'), split_axis=0, concat_axis=0, tiled=T...]
  transfers between devices with their start and end apart: 5 -> 5, of which waited for: 2 -> 2; matrix products, arithmetic and copies ran while one was open for 44% -> 41% of each run, Pallas kernels for 0% -> 0%
where the time goes in v12:
time: 96.7 us; the launch traced here: 96 us
  other arithmetic  31 us (32%)
  waiting for transfers between devices  23.1 us (24%)
  starting transfers between devices  19.8 us (20%)
  local copies, waits for them, and re-layouts  12.4 us (13%)
  matrix products  9 us (9%)
    all_to_all x1, waiting for transfers between devices, coupled_step(): lax.all_to_all(sent, ('lat', 'lon'), split_axis=0, concat_axis=0, tiled=T...  20.2 us
    all_to_all x1, starting transfers between devices, coupled_step(): lax.all_to_all(sent, ('lat', 'lon'), split_axis=0, concat_axis=0, tiled=T...  8.68 us
    sub x3, other arithmetic, advect(): inner + east_flow[..., 1:-1, :-1] - east_flow[..., 1:-1, 1:]  7.8 us
    dot_general x1, matrix products, coupled_step(): jnp.einsum('trb,tbc->trc', lhs, stacked_weights, preferred_element_type=j...  6.83 us
    ppermute x1, starting transfers between devices, with_halo(): lax.ppermute(block[..., :width].reshape(planes, rows * width), 'lon', shi...  6.74 us
    concatenate x2, other arithmetic, with_halo(): return jnp.concatenate([south, middle, north], axis=-2)  5.57 us
    mul x4, other arithmetic, advect(): mask_east * (east_speed[:, :, :-1] * (tracer_now[..., :-1] + tracer_now[....  4.22 us
    mul x4, other arithmetic, advect(): mask_north * (north_speed[:, :-1, :] * (tracer_now[..., :-1, :] + tracer_...  4.15 us
  transfers between devices with their start and end apart: 5, of which 2 were waited for; matrix products, arithmetic and copies ran while one was open for 41% of the time, Pallas kernels for 0%

profile of v12, /device:TPU:0, one launch (start us, length us, event | category | flops | bytes accessed | tf_op | source)
XLA Modules:
  0.0 96.0 jit_solution(8868402948092646881)
XLA Ops:
  0.0 0.7 fusion.36
  0.7 1.3 %pad_maximum_fusion.1 = f32[129,16,128]{2,1,0:T(8,128)S(1)} fusion(f32[1,16,128]{2,1,0:T(8,128)S(1)} %get-tuple-element.20, f32[16,16,128]{2,1,0:T(8,128)} %param.17, f32[16,16,128]{2,1,0:T(8,128)} %param.16, f32[96,16,128]{2,1,0:T(8,128)} %bitcast.47), kind=kLoop, calls=%fused_computation.41 | loop fusion | flops 792576 | bytes 2113536 | tf_op jit(solution)/shard_map/concatenate | solution.py:129
  3.0 6.7 %collective-permute-start.1 = (f32[129,64]{0,1:T(8,128)S(1)}, f32[129,64]{0,1:T(8,128)S(1)}, u32[]{:S(2)}, u32[]{:S(2)}) collective-permute-start(f32[129,64]{0,1:T(8,128)S(1)} %copy.59), channel_id=1, source_target_pairs={{0,31},{1,0},{2,1},{3,2},{4,3},{5,4},{6,5},{7,6},{8,7},{9,8},{10,9... | collective-permute-start | bytes 99080 | tf_op jit(solution)/shard_map/ppermute | solution.py:31
  12.5 1.0 %gather_fusion = bf16[256,24,128]{2,1,0:T(8,128)(2,1)S(1)} fusion(bf16[24,16,128]{2,0,1:T(8,128)(2,1)S(1)} %copy_bitcast_fusion, s32[1024]{0:T(1024)S(1)} %pad_clamp_fusion), kind=kCustom, calls=%fused_computation | custom fusion | bytes 3146752 | tf_op jit(solution)/shard_map/jit(_take)/gather | solution.py:91
  13.5 0.9 broadcast_select_fusion
  14.4 1.2 %slice_bitcast_fusion.1 = (bf16[128,24,128]{2,1,0:T(8,128)(2,1)S(1)}, bf16[128,24,128]{2,1,0:T(8,128)(2,1)}) fusion(bf16[128,2,24,128]{3,2,1,0:T(8,128)(2,1)S(1)} %bitcast.50), kind=kLoop, calls=%fused_computation.43 | loop fusion | bytes 3145728 | tf_op jit(solution)/shard_map/squeeze | solution.py:98
  16.0 2.8 %collective-permute-done = f32[129,64]{0,1:T(8,128)S(1)} collective-permute-done((f32[129,64]{0,1:T(8,128)S(1)}, f32[129,64]{0,1:T(8,128)S(1)}, u32[]{:S(2)}, u32[]{:S(2)}) %collective-permute-start) | collective-permute-done | bytes 33056 | tf_op jit(solution)/shard_map/ppermute | solution.py:28
  19.9 1.3 %pad_maximum_fusion.3 = f32[129,4,136]{2,1,0:T(4,128)} fusion(f32[129,4,4]{2,1,0:T(4,128)S(1)} %copy.50, f32[129,4,128]{2,1,0:T(4,128)S(1)} %get-tuple-element.12, f32[129,4,4]{2,1,0:T(4,128)S(1)} %copy.49), kind=kLoop, calls=%fused_computation.51 | loop fusion | flops 140352 | bytes 561408 | tf_op jit(solution)/shard_map/concatenate | solution.py:39
  21.3 1.3 %collective-permute-start.3 = (f32[129,4,136]{2,1,0:T(4,128)}, f32[129,4,136]{2,1,0:T(4,128)}, u32[]{:S(2)}, u32[]{:S(2)}) collective-permute-start(f32[129,4,136]{2,1,0:T(4,128)} %pad_maximum_fusion.3), channel_id=1, source_target_pairs={{32,0},{64,32},{96,64},{33,1},{65,33},{97,65},{34,2},{66,34},{98,6... | collective-permute-start | bytes 842120 | tf_op jit(solution)/shard_map/ppermute | solution.py:43
  22.6 1.3 %pad_maximum_fusion.2 = f32[129,4,136]{2,1,0:T(4,128)} fusion(f32[129,4,4]{2,1,0:T(4,128)S(1)} %copy.46, f32[129,4,128]{2,1,0:T(4,128)S(1)} %get-tuple-element.11, f32[129,4,4]{2,1,0:T(4,128)S(1)} %copy.45), kind=kLoop, calls=%fused_computation.50 | loop fusion | flops 140352 | bytes 561408 | tf_op jit(solution)/shard_map/concatenate | solution.py:36
  23.9 3.1 %collective-permute-start.2 = (f32[129,4,136]{2,1,0:T(4,128)}, f32[129,4,136]{2,1,0:T(4,128)S(1)}, u32[]{:S(2)}, u32[]{:S(2)}) collective-permute-start(f32[129,4,136]{2,1,0:T(4,128)} %pad_maximum_fusion.2), channel_id=1, source_target_pairs={{0,32},{32,64},{64,96},{1,33},{33,65},{65,97},{2,34},{34,66},{66,9... | collective-permute-start | bytes 842120 | tf_op jit(solution)/shard_map/ppermute | solution.py:42
  27.0 6.8 %select_select_fusion = f32[128,56,128]{2,1,0:T(8,128)} fusion(f32[128,56]{1,0:T(8,128)S(1)} %select_select_fusion.1, pred[56]{0:T(512)(128)(4,1)S(1)} %iota_compare_fusion.6, pred[128,56]{1,0:T(8,128)(4,1)S(1)} %copy.51, bf16[128,256,128]{2,1,0:T(8,128)(2,1)} %bitcast.56, bf16[128,24,128]{2,1,0:T(8,128)(2,1)S(1)} %copy-done.7, ...), kind=kOutput, calls=%fused_computation.14 | convolution fusion | flops 493617152 | bytes 13667496 | tf_op jit(solution)/shard_map/trb,tbc->trc/dot_general | solution.py:104
  33.8 8.7 %all-to-all-start = ((f32[128,56,128]{2,1,0:T(8,128)}), f32[128,56,128]{2,1,0:T(8,128)}, u32[]{:S(2)}, u32[]{:S(2)}) async-start(f32[128,56,128]{2,1,0:T(8,128)} %select_select_fusion), calls=%async_computation | async-start | bytes 7340032 | tf_op jit(solution)/shard_map/all_to_all | solution.py:123
  42.5 0.7 copy.47
  43.2 0.7 copy.48
  44.0 5.3 %pad_maximum_fusion = f32[129,24,136]{2,1,0:T(8,128)S(1)} fusion(f32[129,4,136]{2,1,0:T(4,128)} %collective-permute-done.3, f32[129,16,4]{2,1,0:T(8,128)S(1)} %copy.48, f32[1,16,128]{2,1,0:T(8,128)S(1)} %get-tuple-element.20, f32[16,16,128]{2,1,0:T(8,128)} %param.17, f32[16,16,128]{2,1,0:T(8,128)} %param.16, f32[96,16,128]{2,1,0:T(8,128)S(1)} %bitcast.48, ...), kind=kLoop, calls=%fused_computation.15 | loop fusion | flops 2947392 | bytes 3368448 | tf_op jit(solution)/shard_map/concatenate | solution.py:45
  51.0 0.7 subtract_multiply_fusion.7
  51.7 0.7 subtract_multiply_fusion.6
  53.0 2.5 %slice_subtract_fusion.4 = f32[6,16,22,134]{3,2,1,0:T(8,128)S(1)} fusion(f32[6,16,23,136]{3,2,1,0:T(8,128)S(1)} %subtract_multiply_fusion.6, f32[6,16,24,135]{3,2,1,0:T(8,128)S(1)} %subtract_multiply_fusion.7, f32[6,16,24,136]{3,2,1,0:T(8,128)S(1)} %bitcast.45), kind=kLoop, calls=%fused_computation.26 | loop fusion | flops 1132032 | bytes 6792192 | tf_op jit(solution)/shard_map/sub | solution.py:61
  55.5 0.7 subtract_multiply_fusion.5
  56.2 0.7 subtract_multiply_fusion.4
  56.9 2.5 %slice_subtract_fusion.2 = f32[6,16,20,132]{3,2,1,0:T(8,128)S(1)} fusion(f32[6,16,21,134]{3,2,1,0:T(8,128)S(1)} %subtract_multiply_fusion.4, f32[6,16,22,133]{3,2,1,0:T(8,128)S(1)} %subtract_multiply_fusion.5, f32[6,16,22,134]{3,2,1,0:T(8,128)S(1)} %slice_subtract_fusion.4), kind=kLoop, calls=%fused_computation.22 | loop fusion | flops 1013760 | bytes 6082560 | tf_op jit(solution)/shard_map/sub | solution.py:61
  60.1 0.7 subtract_multiply_fusion.2
  60.8 2.7 %slice_subtract_fusion = f32[6,16,18,130]{3,2,1,0:T(8,128)S(1)} fusion(f32[6,16,19,132]{3,2,1,0:T(8,128)S(1)} %subtract_multiply_fusion.2, f32[6,16,20,131]{3,2,1,0:T(8,128)S(1)} %subtract_multiply_fusion.3, f32[6,16,20,132]{3,2,1,0:T(8,128)S(1)} %slice_subtract_fusion.2), kind=kLoop, calls=%fused_computation.18 | loop fusion | flops 898560 | bytes 5391360 | tf_op jit(solution)/shard_map/sub | solution.py:61
  63.6 2.2 %subtract_multiply_fusion.1 = f32[6,16,18,129]{3,2,1,0:T(8,128)} fusion(f32[6,16,18,130]{3,2,1,0:T(8,128)S(1)} %slice_subtract_fusion, f32[16,18,129]{2,1,0:T(8,128)S(1)} %slice.442, f32[18,129]{1,0:T(8,128)S(1)} %slice_multiply_fusion.1), kind=kLoop, calls=%fused_computation.31 | loop fusion | flops 1560384 | bytes 2832840 | tf_op jit(solution)/shard_map/mul | solution.py:50
  65.8 2.1 %subtract_multiply_fusion = f32[6,16,17,130]{3,2,1,0:T(8,128)} fusion(f32[6,16,18,130]{3,2,1,0:T(8,128)S(1)} %slice_subtract_fusion, f32[16,17,130]{2,1,0:T(8,128)S(1)} %pad_maximum_fusion.4, f32[17,130]{1,0:T(8,128)S(1)} %slice_multiply_fusion), kind=kLoop, calls=%fused_computation.30 | loop fusion | flops 1485120 | bytes 2696200 | tf_op jit(solution)/shard_map/mul | solution.py:55
  67.8 20.2 %all-to-all-done = f32[128,56,128]{2,1,0:T(8,128)} async-done(((f32[128,56,128]{2,1,0:T(8,128)}), f32[128,56,128]{2,1,0:T(8,128)}, u32[]{:S(2)}, u32[]{:S(2)}) %all-to-all-start) | async-done | bytes 3670048 | tf_op jit(solution)/shard_map/all_to_all | solution.py:123
  88.1 1.3 %slice_reduce_fusion = f32[128,2]{1,0:T(8,128)S(1)} fusion(f32[128,56,128]{2,1,0:T(8,128)} %all-to-all-done), kind=kLoop, calls=%fused_computation.60 | loop fusion | bytes 2048 | tf_op jit(solution)/shard_map/slice | solution.py:124
  89.5 2.3 %slice.460 = f32[128,48,128]{2,1,0:T(8,128)S(1)} slice(f32[128,56,128]{2,1,0:T(8,128)} %all-to-all-done), slice={[0:128], [0:48], [0:128]} | slice | bytes 6291456 | tf_op jit(solution)/shard_map/slice | solution.py:125
  91.8 1.3 %fusion.12 = f32[16,24,128]{2,0,1:T(8,128)S(1)} fusion(f32[256,24,128]{2,1,0:T(8,128)S(1)} %bitcast.46, f32[256]{0:T(256)S(1)} %eq.55), kind=kOutput, calls=%fused_computation.16 | convolution fusion | flops 150999040 | bytes 3343360 | tf_op jit(solution)/shard_map/rk,kfc->rfc/dot_general | solution.py:159
  93.1 0.8 fusion.19
  94.0 2.0 %fusion.18 = f32[6,16,16,128]{3,2,1,0:T(8,128)} fusion(f32[6,16,17,130]{3,2,1,0:T(8,128)S(1)} %copy-done.4, f32[6,16,18,129]{3,2,1,0:T(8,128)S(1)} %copy-done.3, f32[6,16,18,130]{3,2,1,0:T(8,128)S(1)} %slice_subtract_fusion, f32[6,16,16,128]{3,1,0,2:T(8,128)S(1)} %bitcast.51, f32[16,128]{1,0:T(8,128)S(1)} %get-tuple-element.19), kind=kLoop, calls=%fused_computation.45 | loop fusion | flops 1179648 | bytes 5513216 | tf_op jit(solution)/shard_map/add | solution.py:166
  (81 shorter events, 8.0 us)
Async XLA Ops:
  0.0 12.5 %copy-start = (bf16[24,2048]{1,0:T(8,128)(2,1)S(1)}, bf16[24,2048]{1,0:T(8,128)(2,1)}, u32[]{:S(2)}) copy-start(bf16[24,2048]{1,0:T(8,128)(2,1)} %param.10) | copy-start | bytes 294916
  2.4 8.1 %copy-start.10 = (s32[1,256]{1,0:T(1,128)S(1)}, s32[1,256]{1,0:T(1,128)}, u32[]{:S(2)}) copy-start(s32[1,256]{1,0:T(1,128)} %param.12) | copy-start | bytes 3076
  2.4 8.2 %copy-start.9 = (s32[1,128]{1,0:T(1,128)S(1)}, s32[1,128]{1,0:T(1,128)}, u32[]{:S(2)}) copy-start(s32[1,128]{1,0:T(1,128)} %param.14) | copy-start | bytes 1540
  2.5 8.9 %copy-start.11 = (s32[1,256]{1,0:T(1,128)S(1)}, s32[1,256]{1,0:T(1,128)}, u32[]{:S(2)}) copy-start(s32[1,256]{1,0:T(1,128)} %param.13) | copy-start | bytes 3076
  3.0 13.0 %collective-permute-start.1 = (f32[129,64]{0,1:T(8,128)S(1)}, f32[129,64]{0,1:T(8,128)S(1)}, u32[]{:S(2)}, u32[]{:S(2)}) collective-permute-start(f32[129,64]{0,1:T(8,128)S(1)} %copy.59), channel_id=1, source_target_pairs={{0,31},{1,0},{2,1},{3,2},{4,3},{5,4},{6,5},{7,6},{8,7},{9,8},{10,9... | collective-permute-start | bytes 99080 | tf_op jit(solution)/shard_map/ppermute | solution.py:31
  10.3 8.6 %collective-permute-start = (f32[129,64]{0,1:T(8,128)S(1)}, f32[129,64]{0,1:T(8,128)S(1)}, u32[]{:S(2)}, u32[]{:S(2)}) collective-permute-start(f32[129,64]{0,1:T(8,128)S(1)} %copy.58), channel_id=1, source_target_pairs={{0,1},{1,2},{2,3},{3,4},{4,5},{5,6},{6,7},{7,8},{8,9},{9,10},{10,1... | collective-permute-start | bytes 99080 | tf_op jit(solution)/shard_map/ppermute | solution.py:28
  19.9 7.0 %copy-start.7 = (bf16[128,24,128]{2,1,0:T(8,128)(2,1)S(1)}, bf16[128,24,128]{2,1,0:T(8,128)(2,1)}, u32[]{:S(2)}) copy-start(bf16[128,24,128]{2,1,0:T(8,128)(2,1)} %get-tuple-element.10) | copy-start | bytes 2359300
  21.3 22.7 %collective-permute-start.3 = (f32[129,4,136]{2,1,0:T(4,128)}, f32[129,4,136]{2,1,0:T(4,128)}, u32[]{:S(2)}, u32[]{:S(2)}) collective-permute-start(f32[129,4,136]{2,1,0:T(4,128)} %pad_maximum_fusion.3), channel_id=1, source_target_pairs={{32,0},{64,32},{96,64},{33,1},{65,33},{97,65},{34,2},{66,34},{98,6... | collective-permute-start | bytes 842120 | tf_op jit(solution)/shard_map/ppermute | solution.py:43
  23.9 20.1 %collective-permute-start.2 = (f32[129,4,136]{2,1,0:T(4,128)}, f32[129,4,136]{2,1,0:T(4,128)S(1)}, u32[]{:S(2)}, u32[]{:S(2)}) collective-permute-start(f32[129,4,136]{2,1,0:T(4,128)} %pad_maximum_fusion.2), channel_id=1, source_target_pairs={{0,32},{32,64},{64,96},{1,33},{33,65},{65,97},{2,34},{34,66},{66,9... | collective-permute-start | bytes 842120 | tf_op jit(solution)/shard_map/ppermute | solution.py:42
  33.8 54.3 %all-to-all-start = ((f32[128,56,128]{2,1,0:T(8,128)}), f32[128,56,128]{2,1,0:T(8,128)}, u32[]{:S(2)}, u32[]{:S(2)}) async-start(f32[128,56,128]{2,1,0:T(8,128)} %select_select_fusion), calls=%async_computation | async-start | bytes 7340032 | tf_op jit(solution)/shard_map/all_to_all | solution.py:123
  42.5 1.5 %copy-start.2 = (f32[6,16,16,128]{3,2,1,0:T(8,128)S(1)}, f32[6,16,16,128]{3,2,1,0:T(8,128)}, u32[]{:S(2)}) copy-start(f32[6,16,16,128]{3,2,1,0:T(8,128)} %param.15) | copy-start | bytes 2359300
  51.7 0.9 copy-start.5
  51.7 1.0 %copy-start.6 = (f32[16,16,128]{2,1,0:T(8,128)S(1)}, f32[16,16,128]{2,1,0:T(8,128)}, u32[]{:S(2)}) copy-start(f32[16,16,128]{2,1,0:T(8,128)} %param.16) | copy-start | bytes 393220
  89.5 4.5 %copy-start.4 = (f32[6,16,17,130]{3,2,1,0:T(8,128)S(1)}, f32[6,16,17,130]{3,2,1,0:T(8,128)}, u32[]{:S(2)}) copy-start(f32[6,16,17,130]{3,2,1,0:T(8,128)} %subtract_multiply_fusion) | copy-start | bytes 2545924
  91.8 1.4 %copy-start.8 = (f32[96,24]{0,1:T(8,128)S(1)}, f32[96,24]{0,1:T(8,128)}, u32[]{:S(2)}) copy-start(f32[96,24]{0,1:T(8,128)} %param.19) | copy-start | bytes 27652
  91.8 2.2 %copy-start.3 = (f32[6,16,18,129]{3,2,1,0:T(8,128)S(1)}, f32[6,16,18,129]{3,2,1,0:T(8,128)}, u32[]{:S(2)}) copy-start(f32[6,16,18,129]{3,2,1,0:T(8,128)} %subtract_multiply_fusion.1) | copy-start | bytes 2674948
  94.0 2.0 %copy-start.1 = (bf16[24,2048]{1,0:T(8,128)(2,1)S(1)}, bf16[24,2048]{1,0:T(8,128)(2,1)}, u32[]{:S(2)}) copy-start(bf16[24,2048]{1,0:T(8,128)(2,1)} %param.10) | copy-start | bytes 294916

commit v13 on v10

--- a/solution.py
+++ b/solution.py
@@ -21,44 +21,30 @@
     return pairs
 
 
-def with_halo(parts, width):
+def with_halo(block, width):
     lon_count = lax.axis_size("lon")
     lat_count = lax.axis_size("lat")
-    rows, cols = parts[0].shape[-2:]
+    parts = block
+    rows, _ = parts[0].shape[-2:]
     planes = sum(p.shape[0] for p in parts)
-    east_edge = jnp.concatenate([p[..., -width:] for p in parts], axis=0)
-    west_edge = jnp.concatenate([p[..., :width] for p in parts], axis=0)
-    west = lax.ppermute(
-        east_edge.reshape(planes, rows * width), "lon", shifted_pairs(lon_count, 1, True)
-    )
-    east = lax.ppermute(
-        west_edge.reshape(planes, rows * width), "lon", shifted_pairs(lon_count, -1, True)
-    )
-    west_flat, east_flat = west, east
-    west = west.reshape(planes, rows, width)
-    east = east.reshape(planes, rows, width)
-    wide_cols = cols + 2 * width
+    tall_rows = rows + 2 * width
     top_rows = jnp.concatenate([p[:, -width:, :] for p in parts], axis=0)
     bottom_rows = jnp.concatenate([p[:, :width, :] for p in parts], axis=0)
-    top = jnp.concatenate(
-        [west[:, -width:, :], top_rows, east[:, -width:, :]], axis=-1
-    ).reshape(planes, width * wide_cols)
-    bottom = jnp.concatenate(
-        [west[:, :width, :], bottom_rows, east[:, :width, :]], axis=-1
-    ).reshape(planes, width * wide_cols)
-    south = lax.ppermute(top, "lat", shifted_pairs(lat_count, 1, False))
-    north = lax.ppermute(bottom, "lat", shifted_pairs(lat_count, -1, False))
-    middle = jnp.concatenate(
-        [
-            west_flat.reshape(planes, rows, width),
-            jnp.concatenate(parts, axis=0),
-            east_flat.reshape(planes, rows, width),
-        ],
-        axis=-1,
-    )
-    south = south.reshape(planes, width, wide_cols)
-    north = north.reshape(planes, width, wide_cols)
-    return jnp.concatenate([south, middle, north], axis=-2)
+    south = lax.ppermute(top_rows, "lat", shifted_pairs(lat_count, 1, False))
+    north = lax.ppermute(bottom_rows, "lat", shifted_pairs(lat_count, -1, False))
+    block = jnp.concatenate(parts, axis=0)
+    east_edge = jnp.concatenate(
+        [south[..., -width:], block[..., -width:], north[..., -width:]], axis=1
+    ).reshape(planes, tall_rows * width)
+    west_edge = jnp.concatenate(
+        [south[..., :width], block[..., :width], north[..., :width]], axis=1
+    ).reshape(planes, tall_rows * width)
+    west = lax.ppermute(east_edge, "lon", shifted_pairs(lon_count, 1, True))
+    east = lax.ppermute(west_edge, "lon", shifted_pairs(lon_count, -1, True))
+    tall = jnp.concatenate([south, block, north], axis=1)
+    west = west.reshape(planes, tall_rows, width)
+    east = east.reshape(planes, tall_rows, width)
+    return jnp.concatenate([west, tall, east], axis=-1)
 
 
 def advect(tracer_now, east_speed, north_speed, sea_mask):

time: 101 us -> 103 us (1.020)
  other arithmetic: 28.3 us -> 36.1 us
  starting transfers between devices: 21.5 us -> 18.1 us
  waiting for transfers between devices: 18 us -> 16.1 us
    concatenate x6 -> x7, other arithmetic: 6.63 us -> 12.7 us  [the longest x2 7.23 us: with_halo(): return jnp.concatenate([west, tall, east], axis=-1)]
    all_to_all x1, starting transfers between devices: 9.62 us -> 6.28 us  [coupled_step(): lax.all_to_all(sent, ('lat', 'lon'), split_axis=0, concat_axis=0, tiled=T...]
    reshape x10 -> x8, local copies, waits for them, and re-layouts: 7.36 us -> 5.99 us  [the longest x2 2.23 us: with_halo(): east = east.reshape(planes, tall_rows, width)]
    ppermute x4, waiting for transfers between devices: 1.35 us -> 0.01 us  [the longest x1 0.01 us: with_halo(): west = lax.ppermute(east_edge, 'lon', shifted_pairs(lon_count, 1, True))]
    select_n x2, other arithmetic: 0.93 us -> 2.06 us  [coupled_step(): chosen = jnp.take(atm_blocks, source_block[0], axis=1)]
    gather x1, local copies, waits for them, and re-layouts: 0.98 us -> 2.04 us  [coupled_step(): chosen = jnp.take(atm_blocks, source_block[0], axis=1)]
    slice x16 -> x3, local copies, waits for them, and re-layouts: 4.61 us -> 4.09 us  [the longest x1 1.93 us: with_halo(): south[..., -width:]]
  transfers between devices with their start and end apart: 5 -> 5, of which waited for: 2 -> 1; matrix products, arithmetic and copies ran while one was open for 43% -> 51% of each run, Pallas kernels for 0% -> 0%
where the time goes in v13:
time: 103 us; the launch traced here: 102 us
  other arithmetic  36.1 us (35%)
  local copies, waits for them, and re-layouts  21.7 us (21%)
  starting transfers between devices  18.1 us (18%)
  waiting for transfers between devices  16.1 us (16%)
  matrix products  9.77 us (9%)
    all_to_all x1, waiting for transfers between devices, coupled_step(): lax.all_to_all(sent, ('lat', 'lon'), split_axis=0, concat_axis=0, tiled=T...  16.1 us
    sub x3, other arithmetic, advect(): inner + east_flow[..., 1:-1, :-1] - east_flow[..., 1:-1, 1:]  7.8 us
    dot_general x1, matrix products, coupled_step(): jnp.einsum('trb,tbc->trc', lhs, stacked_weights, preferred_element_type=j...  7.61 us
    concatenate x2, other arithmetic, with_halo(): return jnp.concatenate([west, tall, east], axis=-1)  7.23 us
    all_to_all x1, starting transfers between devices, coupled_step(): lax.all_to_all(sent, ('lat', 'lon'), split_axis=0, concat_axis=0, tiled=T...  6.28 us
    ppermute x1, starting transfers between devices, with_halo(): east = lax.ppermute(west_edge, 'lon', shifted_pairs(lon_count, -1, True))  5.14 us
    mul x4, other arithmetic, advect(): mask_east * (east_speed[:, :, :-1] * (tracer_now[..., :-1] + tracer_now[....  4.22 us
    mul x4, other arithmetic, advect(): mask_north * (north_speed[:, :-1, :] * (tracer_now[..., :-1, :] + tracer_...  4.15 us
  transfers between devices with their start and end apart: 5, of which 1 were waited for; matrix products, arithmetic and copies ran while one was open for 51% of the time, Pallas kernels for 0%

profile of v13, /device:TPU:0, one launch (start us, length us, event | category | flops | bytes accessed | tf_op | source)
XLA Modules:
  0.0 102.3 jit_solution(12696173353756755492)
XLA Ops:
  0.8 1.2 %fusion.33 = (f32[96,4,128]{2,1,0:T(4,128)S(1)}, f32[96,4,128]{2,1,0:T(4,128)S(1)}) fusion(f32[96,16,128]{2,1,0:T(8,128)} %bitcast.47), kind=kLoop, calls=%fused_computation.109 | loop fusion | bytes 786432 | tf_op jit(solution)/shard_map/slice | solution.py:31
  2.0 1.0 fusion.36
  3.7 1.3 %collective-permute-start.1 = (f32[129,4,128]{2,1,0:T(4,128)}, f32[129,4,128]{2,1,0:T(4,128)S(1)}, u32[]{:S(2)}, u32[]{:S(2)}) collective-permute-start(f32[129,4,128]{2,1,0:T(4,128)} %pad_maximum_fusion.11), channel_id=1, source_target_pairs={{32,0},{64,32},{96,64},{33,1},{65,33},{97,65},{34,2},{66,34},{98,6... | collective-permute-start | bytes 792584 | tf_op jit(solution)/shard_map/ppermute | solution.py:34
  5.8 3.8 %collective-permute-start = (f32[129,4,128]{2,1,0:T(4,128)}, f32[129,4,128]{2,1,0:T(4,128)}, u32[]{:S(2)}, u32[]{:S(2)}) collective-permute-start(f32[129,4,128]{2,1,0:T(4,128)} %pad_maximum_fusion.10), channel_id=1, source_target_pairs={{0,32},{32,64},{64,96},{1,33},{33,65},{65,97},{2,34},{34,66},{66,9... | collective-permute-start | bytes 792584 | tf_op jit(solution)/shard_map/ppermute | solution.py:33
  9.6 1.0 %pad_maximum_fusion.3 = f32[129,16,128]{2,1,0:T(8,128)S(1)} fusion(f32[1,16,128]{2,1,0:T(8,128)S(1)} %get-tuple-element.24, f32[16,16,128]{2,1,0:T(8,128)} %param.17, f32[16,16,128]{2,1,0:T(8,128)} %param.16, f32[96,16,128]{2,1,0:T(8,128)S(1)} %bitcast.48), kind=kLoop, calls=%fused_computation.43 | loop fusion | flops 792576 | bytes 2113536 | tf_op jit(solution)/shard_map/concatenate | solution.py:35
  12.6 1.3 %fusion.32 = (f32[129,16,4]{2,1,0:T(8,128)}, f32[129,16,4]{2,1,0:T(8,128)S(1)}) fusion(f32[129,16,128]{2,1,0:T(8,128)S(1)} %pad_maximum_fusion.3), kind=kLoop, calls=%fused_computation.108 | loop fusion | bytes 132096 | tf_op jit(solution)/shard_map/slice | solution.py:37
  13.9 2.0 %gather_fusion = bf16[256,24,128]{2,1,0:T(8,128)(2,1)} fusion(bf16[24,16,128]{2,0,1:T(8,128)(2,1)S(1)} %copy_bitcast_fusion, s32[1024]{0:T(1024)S(1)} %pad_clamp_fusion), kind=kCustom, calls=%fused_computation | custom fusion | bytes 3146752 | tf_op jit(solution)/shard_map/jit(_take)/gather | solution.py:93
  16.0 2.1 %broadcast_select_fusion = bf16[256,24,128]{2,1,0:T(8,128)(2,1)S(1)} fusion(bf16[256,24,128]{2,1,0:T(8,128)(2,1)} %gather_fusion, pred[256]{0:T(512)(128)(4,1)S(1)} %compare_and_fusion), kind=kLoop, calls=%fused_computation.42 | loop fusion | flops 786432 | bytes 3145984 | tf_op jit(solution)/shard_map/jit(_take)/select_n | solution.py:93
  18.0 1.4 %slice_bitcast_fusion.1 = (bf16[128,24,128]{2,1,0:T(8,128)(2,1)}, bf16[128,24,128]{2,1,0:T(8,128)(2,1)}) fusion(bf16[128,2,24,128]{3,2,1,0:T(8,128)(2,1)S(1)} %bitcast.51), kind=kLoop, calls=%fused_computation.45 | loop fusion | bytes 3145728 | tf_op jit(solution)/shard_map/squeeze | solution.py:100
  20.5 1.9 %fusion.34 = (f32[129,4,4]{2,1,0:T(4,128)S(1)}, f32[129,4,4]{2,1,0:T(4,128)}) fusion(f32[129,4,128]{2,1,0:T(4,128)} %collective-permute-done), kind=kLoop, calls=%fused_computation.110 | loop fusion | bytes 33024 | tf_op jit(solution)/shard_map/slice | solution.py:37
  22.4 0.8 fusion.35
  23.2 1.5 %pad_maximum_fusion.1 = f32[129,24,4]{2,1,0:T(8,128)S(1)} fusion(f32[129,4,4]{2,1,0:T(4,128)S(1)} %get-tuple-element.17, f32[129,16,4]{2,1,0:T(8,128)} %get-tuple-element.11, f32[129,4,4]{2,1,0:T(4,128)S(1)} %get-tuple-element.15), kind=kLoop, calls=%fused_computation.40 | loop fusion | flops 24768 | bytes 99072 | tf_op jit(solution)/shard_map/concatenate | solution.py:36
  26.0 1.6 %collective-permute-start.2 = (f32[129,96]{0,1:T(8,128)}, f32[129,96]{0,1:T(8,128)}, u32[]{:S(2)}, u32[]{:S(2)}) collective-permute-start(f32[129,96]{0,1:T(8,128)} %copy.88), channel_id=1, source_target_pairs={{0,1},{1,2},{2,3},{3,4},{4,5},{5,6},{6,7},{7,8},{8,9},{9,10},{10,1... | collective-permute-start | bytes 148616 | tf_op jit(solution)/shard_map/ppermute | solution.py:42
  27.6 1.3 %pad_maximum_fusion.2 = f32[129,24,4]{2,1,0:T(8,128)S(1)} fusion(f32[129,4,4]{2,1,0:T(4,128)} %get-tuple-element.18, f32[129,16,4]{2,1,0:T(8,128)S(1)} %get-tuple-element.12, f32[129,4,4]{2,1,0:T(4,128)} %get-tuple-element.16), kind=kLoop, calls=%fused_computation.41 | loop fusion | flops 24768 | bytes 99072 | tf_op jit(solution)/shard_map/concatenate | solution.py:39
  29.5 5.1 %collective-permute-start.3 = (f32[129,96]{0,1:T(8,128)S(1)}, f32[129,96]{0,1:T(8,128)S(1)}, u32[]{:S(2)}, u32[]{:S(2)}) collective-permute-start(f32[129,96]{0,1:T(8,128)S(1)} %copy.89), channel_id=1, source_target_pairs={{0,31},{1,0},{2,1},{3,2},{4,3},{5,4},{6,5},{7,6},{8,7},{9,8},{10,9... | collective-permute-start | bytes 148616 | tf_op jit(solution)/shard_map/ppermute | solution.py:43
  34.7 7.6 %select_select_fusion = f32[128,56,128]{2,1,0:T(8,128)} fusion(f32[128,56]{1,0:T(8,128)} %select_select_fusion.1, pred[56]{0:T(512)(128)(4,1)S(1)} %iota_compare_fusion.6, pred[128,56]{1,0:T(8,128)(4,1)S(1)} %copy.81, bf16[128,256,128]{2,1,0:T(8,128)(2,1)} %bitcast.57, bf16[128,24,128]{2,1,0:T(8,128)(2,1)} %get-tuple-element.10, ...), kind=kOutput, calls=%fused_computation.14 | convolution fusion | flops 493617152 | bytes 13667496 | tf_op jit(solution)/shard_map/trb,tbc->trc/dot_general | solution.py:106
  42.3 6.3 %all-to-all-start = ((f32[128,56,128]{2,1,0:T(8,128)}), f32[128,56,128]{2,1,0:T(8,128)}, u32[]{:S(2)}, u32[]{:S(2)}) async-start(f32[128,56,128]{2,1,0:T(8,128)} %select_select_fusion), calls=%async_computation | async-start | bytes 7340032 | tf_op jit(solution)/shard_map/all_to_all | solution.py:123
  48.6 1.0 reshape.247
  49.6 1.0 copy.78
  50.7 2.2 %copy.79 = f32[129,24,4]{2,1,0:T(8,128)} copy(f32[129,24,4]{0,2,1:T(4,128)S(1)} %reshape.249) | data formatting | bytes 99072 | tf_op jit(solution)/shard_map/reshape | solution.py:46
  52.9 6.2 %pad_maximum_fusion = f32[129,24,136]{2,1,0:T(8,128)S(1)} fusion(f32[129,24,4]{2,1,0:T(8,128)} %copy.79, f32[129,4,128]{2,1,0:T(4,128)S(1)} %copy-done.6, f32[1,16,128]{2,1,0:T(8,128)S(1)} %get-tuple-element.24, f32[16,16,128]{2,1,0:T(8,128)S(1)} %copy-done.8, f32[16,16,128]{2,1,0:T(8,128)S(1)} %copy-done.7, f32[96,16,128]{2,1,0:T(8,128)S(1)} %bitcast.49, ...), kind=kLoop, calls=%fused_computation.15 | loop fusion | flops 2947392 | bytes 3368448 | tf_op jit(solution)/shard_map/concatenate | solution.py:47
  62.2 1.0 %pad_maximum_fusion.4 = f32[16,18,129]{2,1,0:T(8,128)S(1)} fusion(f32[129,24,4]{2,1,0:T(8,128)S(1)} %copy.78, f32[129,4,128]{2,1,0:T(4,128)S(1)} %copy-done.6, f32[129,4,128]{2,1,0:T(4,128)} %collective-permute-done, f32[1,16,128]{2,1,0:T(8,128)S(1)} %get-tuple-element.24, f32[16,16,128]{2,1,0:T(8,128)S(1)} %copy-done.8, f32[16,16,128]{2,1,0:T(8,128)S(1)} %copy-done.7, ...), kind=kLoop, calls=%fused_computation.52 | loop fusion | flops 222912 | bytes 1783296 | tf_op jit(solution)/shard_map/concatenate | solution.py:47
  63.2 2.5 %slice_subtract_fusion.4 = f32[6,16,22,134]{3,2,1,0:T(8,128)S(1)} fusion(f32[6,16,23,136]{3,2,1,0:T(8,128)S(1)} %subtract_multiply_fusion.6, f32[6,16,24,135]{3,2,1,0:T(8,128)S(1)} %subtract_multiply_fusion.7, f32[6,16,24,136]{3,2,1,0:T(8,128)S(1)} %bitcast.45), kind=kLoop, calls=%fused_computation.26 | loop fusion | flops 1132032 | bytes 6792192 | tf_op jit(solution)/shard_map/sub | solution.py:63
  67.1 2.5 %slice_subtract_fusion.2 = f32[6,16,20,132]{3,2,1,0:T(8,128)S(1)} fusion(f32[6,16,21,134]{3,2,1,0:T(8,128)S(1)} %subtract_multiply_fusion.4, f32[6,16,22,133]{3,2,1,0:T(8,128)S(1)} %subtract_multiply_fusion.5, f32[6,16,22,134]{3,2,1,0:T(8,128)S(1)} %slice_subtract_fusion.4), kind=kLoop, calls=%fused_computation.22 | loop fusion | flops 1013760 | bytes 6082560 | tf_op jit(solution)/shard_map/sub | solution.py:63
  71.0 2.7 %slice_subtract_fusion = f32[6,16,18,130]{3,2,1,0:T(8,128)S(1)} fusion(f32[6,16,19,132]{3,2,1,0:T(8,128)S(1)} %subtract_multiply_fusion.2, f32[6,16,20,131]{3,2,1,0:T(8,128)S(1)} %subtract_multiply_fusion.3, f32[6,16,20,132]{3,2,1,0:T(8,128)S(1)} %slice_subtract_fusion.2), kind=kLoop, calls=%fused_computation.18 | loop fusion | flops 898560 | bytes 5391360 | tf_op jit(solution)/shard_map/sub | solution.py:63
  73.8 2.2 %subtract_multiply_fusion.1 = f32[6,16,18,129]{3,2,1,0:T(8,128)} fusion(f32[6,16,18,130]{3,2,1,0:T(8,128)S(1)} %slice_subtract_fusion, f32[16,18,129]{2,1,0:T(8,128)S(1)} %pad_maximum_fusion.4, f32[18,129]{1,0:T(8,128)S(1)} %slice_multiply_fusion.1), kind=kLoop, calls=%fused_computation.31 | loop fusion | flops 1560384 | bytes 2832840 | tf_op jit(solution)/shard_map/mul | solution.py:52
  76.0 2.1 %subtract_multiply_fusion = f32[6,16,17,130]{3,2,1,0:T(8,128)} fusion(f32[6,16,18,130]{3,2,1,0:T(8,128)S(1)} %slice_subtract_fusion, f32[16,17,130]{2,1,0:T(8,128)S(1)} %slice.474, f32[17,130]{1,0:T(8,128)S(1)} %slice_multiply_fusion), kind=kLoop, calls=%fused_computation.30 | loop fusion | flops 1485120 | bytes 2696200 | tf_op jit(solution)/shard_map/mul | solution.py:57
  78.0 16.1 %all-to-all-done = f32[128,56,128]{2,1,0:T(8,128)} async-done(((f32[128,56,128]{2,1,0:T(8,128)}), f32[128,56,128]{2,1,0:T(8,128)}, u32[]{:S(2)}, u32[]{:S(2)}) %all-to-all-start) | async-done | bytes 3670048 | tf_op jit(solution)/shard_map/all_to_all | solution.py:123
  94.2 1.3 %slice_reduce_fusion = f32[128,2]{1,0:T(8,128)S(1)} fusion(f32[128,56,128]{2,1,0:T(8,128)} %all-to-all-done), kind=kLoop, calls=%fused_computation.62 | loop fusion | bytes 2048 | tf_op jit(solution)/shard_map/slice | solution.py:124
  95.6 2.3 %slice.486 = f32[128,48,128]{2,1,0:T(8,128)S(1)} slice(f32[128,56,128]{2,1,0:T(8,128)} %all-to-all-done), slice={[0:128], [0:48], [0:128]} | slice | bytes 6291456 | tf_op jit(solution)/shard_map/slice | solution.py:125
  97.9 1.3 %fusion.12 = f32[16,24,128]{2,0,1:T(8,128)S(1)} fusion(f32[256,24,128]{2,1,0:T(8,128)S(1)} %bitcast.46, f32[256]{0:T(256)S(1)} %eq.55), kind=kOutput, calls=%fused_computation.16 | convolution fusion | flops 150999040 | bytes 3343360 | tf_op jit(solution)/shard_map/rk,kfc->rfc/dot_general | solution.py:156
  100.1 2.2 %fusion.18 = f32[6,16,16,128]{3,2,1,0:T(8,128)} fusion(f32[6,16,17,130]{3,2,1,0:T(8,128)S(1)} %copy-done.4, f32[6,16,18,129]{3,2,1,0:T(8,128)S(1)} %copy-done.3, f32[6,16,18,130]{3,2,1,0:T(8,128)S(1)} %slice_subtract_fusion, f32[6,16,16,128]{3,1,0,2:T(8,128)S(1)} %bitcast.52, f32[16,128]{1,0:T(8,128)S(1)} %get-tuple-element.23), kind=kLoop, calls=%fused_computation.47 | loop fusion | flops 1179648 | bytes 5513216 | tf_op jit(solution)/shard_map/add | solution.py:163
  (83 shorter events, 13.8 us)
Async XLA Ops:
  0.0 12.6 %copy-start = (bf16[24,2048]{1,0:T(8,128)(2,1)S(1)}, bf16[24,2048]{1,0:T(8,128)(2,1)}, u32[]{:S(2)}) copy-start(bf16[24,2048]{1,0:T(8,128)(2,1)} %param.10) | copy-start | bytes 294916
  0.0 9.6 %copy-start.2 = (f32[6,16,16,128]{3,2,1,0:T(8,128)S(1)}, f32[6,16,16,128]{3,2,1,0:T(8,128)}, u32[]{:S(2)}) copy-start(f32[6,16,16,128]{3,2,1,0:T(8,128)} %param.15) | copy-start | bytes 2359300
  0.0 10.6 %copy-start.11 = (s32[1,256]{1,0:T(1,128)S(1)}, s32[1,256]{1,0:T(1,128)}, u32[]{:S(2)}) copy-start(s32[1,256]{1,0:T(1,128)} %param.12) | copy-start | bytes 3076
  0.0 10.7 %copy-start.10 = (s32[1,128]{1,0:T(1,128)S(1)}, s32[1,128]{1,0:T(1,128)}, u32[]{:S(2)}) copy-start(s32[1,128]{1,0:T(1,128)} %param.14) | copy-start | bytes 1540
  0.0 11.5 %copy-start.12 = (s32[1,256]{1,0:T(1,128)S(1)}, s32[1,256]{1,0:T(1,128)}, u32[]{:S(2)}) copy-start(s32[1,256]{1,0:T(1,128)} %param.13) | copy-start | bytes 3076
  3.7 18.7 %collective-permute-start.1 = (f32[129,4,128]{2,1,0:T(4,128)}, f32[129,4,128]{2,1,0:T(4,128)S(1)}, u32[]{:S(2)}, u32[]{:S(2)}) collective-permute-start(f32[129,4,128]{2,1,0:T(4,128)} %pad_maximum_fusion.11), channel_id=1, source_target_pairs={{32,0},{64,32},{96,64},{33,1},{65,33},{97,65},{34,2},{66,34},{98,6... | collective-permute-start | bytes 792584 | tf_op jit(solution)/shard_map/ppermute | solution.py:34
  5.8 14.7 %collective-permute-start = (f32[129,4,128]{2,1,0:T(4,128)}, f32[129,4,128]{2,1,0:T(4,128)}, u32[]{:S(2)}, u32[]{:S(2)}) collective-permute-start(f32[129,4,128]{2,1,0:T(4,128)} %pad_maximum_fusion.10), channel_id=1, source_target_pairs={{0,32},{32,64},{64,96},{1,33},{33,65},{65,97},{2,34},{34,66},{66,9... | collective-permute-start | bytes 792584 | tf_op jit(solution)/shard_map/ppermute | solution.py:33
  22.4 0.8 copy-start.5
  26.0 22.6 %collective-permute-start.2 = (f32[129,96]{0,1:T(8,128)}, f32[129,96]{0,1:T(8,128)}, u32[]{:S(2)}, u32[]{:S(2)}) collective-permute-start(f32[129,96]{0,1:T(8,128)} %copy.88), channel_id=1, source_target_pairs={{0,1},{1,2},{2,3},{3,4},{4,5},{5,6},{6,7},{7,8},{8,9},{9,10},{10,1... | collective-permute-start | bytes 148616 | tf_op jit(solution)/shard_map/ppermute | solution.py:42
  29.5 21.1 %collective-permute-start.3 = (f32[129,96]{0,1:T(8,128)S(1)}, f32[129,96]{0,1:T(8,128)S(1)}, u32[]{:S(2)}, u32[]{:S(2)}) collective-permute-start(f32[129,96]{0,1:T(8,128)S(1)} %copy.89), channel_id=1, source_target_pairs={{0,31},{1,0},{2,1},{3,2},{4,3},{5,4},{6,5},{7,6},{8,7},{9,8},{10,9... | collective-permute-start | bytes 148616 | tf_op jit(solution)/shard_map/ppermute | solution.py:43
  42.3 51.9 %all-to-all-start = ((f32[128,56,128]{2,1,0:T(8,128)}), f32[128,56,128]{2,1,0:T(8,128)}, u32[]{:S(2)}, u32[]{:S(2)}) async-start(f32[128,56,128]{2,1,0:T(8,128)} %select_select_fusion), calls=%async_computation | async-start | bytes 7340032 | tf_op jit(solution)/shard_map/all_to_all | solution.py:123
  48.6 4.3 %copy-start.6 = (f32[129,4,128]{2,1,0:T(4,128)S(1)}, f32[129,4,128]{2,1,0:T(4,128)}, u32[]{:S(2)}) copy-start(f32[129,4,128]{2,1,0:T(4,128)} %copy-done.5) | copy-start | bytes 792580
  48.6 4.3 %copy-start.7 = (f32[16,16,128]{2,1,0:T(8,128)S(1)}, f32[16,16,128]{2,1,0:T(8,128)}, u32[]{:S(2)}) copy-start(f32[16,16,128]{2,1,0:T(8,128)} %param.16) | copy-start | bytes 393220
  48.6 4.3 %copy-start.8 = (f32[16,16,128]{2,1,0:T(8,128)S(1)}, f32[16,16,128]{2,1,0:T(8,128)}, u32[]{:S(2)}) copy-start(f32[16,16,128]{2,1,0:T(8,128)} %param.17) | copy-start | bytes 393220
  95.6 4.5 %copy-start.4 = (f32[6,16,17,130]{3,2,1,0:T(8,128)S(1)}, f32[6,16,17,130]{3,2,1,0:T(8,128)}, u32[]{:S(2)}) copy-start(f32[6,16,17,130]{3,2,1,0:T(8,128)} %subtract_multiply_fusion) | copy-start | bytes 2545924
  97.9 1.4 %copy-start.9 = (f32[96,24]{0,1:T(8,128)S(1)}, f32[96,24]{0,1:T(8,128)}, u32[]{:S(2)}) copy-start(f32[96,24]{0,1:T(8,128)} %param.19) | copy-start | bytes 27652
  97.9 2.2 %copy-start.3 = (f32[6,16,18,129]{3,2,1,0:T(8,128)S(1)}, f32[6,16,18,129]{3,2,1,0:T(8,128)}, u32[]{:S(2)}) copy-start(f32[6,16,18,129]{3,2,1,0:T(8,128)} %subtract_multiply_fusion.1) | copy-start | bytes 2674948
  100.0 2.2 %copy-start.1 = (bf16[24,2048]{1,0:T(8,128)(2,1)S(1)}, bf16[24,2048]{1,0:T(8,128)(2,1)}, u32[]{:S(2)}) copy-start(bf16[24,2048]{1,0:T(8,128)(2,1)} %param.10) | copy-start | bytes 294916

commit v14 on v13

--- a/solution.py
+++ b/solution.py
@@ -24,15 +24,10 @@
 def with_halo(block, width):
     lon_count = lax.axis_size("lon")
     lat_count = lax.axis_size("lat")
-    parts = block
-    rows, _ = parts[0].shape[-2:]
-    planes = sum(p.shape[0] for p in parts)
+    planes, rows, _ = block.shape
     tall_rows = rows + 2 * width
-    top_rows = jnp.concatenate([p[:, -width:, :] for p in parts], axis=0)
-    bottom_rows = jnp.concatenate([p[:, :width, :] for p in parts], axis=0)
-    south = lax.ppermute(top_rows, "lat", shifted_pairs(lat_count, 1, False))
-    north = lax.ppermute(bottom_rows, "lat", shifted_pairs(lat_count, -1, False))
-    block = jnp.concatenate(parts, axis=0)
+    south = lax.ppermute(block[:, -width:, :], "lat", shifted_pairs(lat_count, 1, False))
+    north = lax.ppermute(block[:, :width, :], "lat", shifted_pairs(lat_count, -1, False))
     east_edge = jnp.concatenate(
         [south[..., -width:], block[..., -width:], north[..., -width:]], axis=1
     ).reshape(planes, tall_rows * width)
@@ -126,12 +121,15 @@
 
     sea_here = land_mask.astype(jnp.float32)
     planes = tracer_count * level_count
-    stacked = [
-        tracers.reshape(planes, lat_rows, lon_cols),
-        east_velocity,
-        north_velocity,
-        sea_here[None],
-    ]
+    stacked = jnp.concatenate(
+        [
+            tracers.reshape(planes, lat_rows, lon_cols),
+            east_velocity,
+            north_velocity,
+            sea_here[None],
+        ],
+        axis=0,
+    )
     wide = with_halo(stacked, NSUB)
     tracer_now = wide[:planes].reshape(tracer_count, level_count, lat_rows + 2 * NSUB, lon_cols + 2 * NSUB)
     east_wide = wide[planes : planes + level_count]
@@ -154,11 +152,11 @@
         jnp.float32
     )
     ocean_flux = jnp.einsum(
-        "rk,kfc->rfc", chooser, arrived, precision=lax.Precision.HIGHEST,
+        "rk,kfc->rfc", chooser, arrived, precision=lax.Precision.HIGH,
         preferred_element_type=jnp.float32,
     )
     source = jnp.einsum(
-        "pf,ifj->pij", coupling, ocean_flux, precision=lax.Precision.HIGHEST
+        "pf,ifj->pij", coupling, ocean_flux, precision=lax.Precision.HIGH
     ).reshape(tracer_count, level_count, lat_rows, lon_cols)
     return tracer_now + sea_here * source
 

time: 103 us -> 101 us (0.981)
  starting transfers between devices: 18.1 us -> 24.6 us
  local copies, waits for them, and re-layouts: 21.7 us -> 16.1 us
  other arithmetic: 36.1 us -> 32.1 us
  waiting for transfers between devices: 16.1 us -> 17.8 us
    all_to_all x1, starting transfers between devices: 6.28 us -> 14.8 us  [coupled_step(): lax.all_to_all(sent, ('lat', 'lon'), split_axis=0, concat_axis=0, tiled=T...]
    concatenate x4 -> x1, other arithmetic: 3.93 us -> 1.34 us  [coupled_step(): jnp.concatenate([tracers.reshape(planes, lat_rows, lon_cols), east_veloci...]
    ppermute x2, starting transfers between devices: 5.04 us -> 2.73 us  [the longest x1 1.44 us: with_halo(): lax.ppermute(block[:, -width:, :], 'lat', shifted_pairs(lat_count, 1, Fal...]
    slice x3 -> x1, local copies, waits for them, and re-layouts: 2.15 us -> 0.09 us  [with_halo(): block[:, -width:, :]]
    ppermute x1, starting transfers between devices: 5.14 us -> 7.12 us  [with_halo(): east = lax.ppermute(west_edge, 'lon', shifted_pairs(lon_count, -1, True))]
    slice x1, local copies, waits for them, and re-layouts: 1.93 us -> 0.2 us  [with_halo(): south[..., -width:]]
    all_to_all x1, waiting for transfers between devices: 16.1 us -> 17.8 us  [coupled_step(): lax.all_to_all(sent, ('lat', 'lon'), split_axis=0, concat_axis=0, tiled=T...]
    ppermute x1, starting transfers between devices: 1.61 us -> 0.01 us  [with_halo(): west = lax.ppermute(east_edge, 'lon', shifted_pairs(lon_count, 1, True))]
  transfers between devices with their start and end apart: 5 -> 5, of which waited for: 1 -> 1; matrix products, arithmetic and copies ran while one was open for 51% -> 43% of each run, Pallas kernels for 0% -> 0%
where the time goes in v14:
time: 101 us; the launch traced here: 100 us
  other arithmetic  32.1 us (32%)
  starting transfers between devices  24.6 us (24%)
  waiting for transfers between devices  17.8 us (18%)
  local copies, waits for them, and re-layouts  16.1 us (16%)
  matrix products  9.05 us (9%)
    all_to_all x1, waiting for transfers between devices, coupled_step(): lax.all_to_all(sent, ('lat', 'lon'), split_axis=0, concat_axis=0, tiled=T...  17.8 us
    all_to_all x1, starting transfers between devices, coupled_step(): lax.all_to_all(sent, ('lat', 'lon'), split_axis=0, concat_axis=0, tiled=T...  14.8 us
    sub x3, other arithmetic, advect(): inner + east_flow[..., 1:-1, :-1] - east_flow[..., 1:-1, 1:]  7.8 us
    dot_general x1, matrix products, coupled_step(): jnp.einsum('trb,tbc->trc', lhs, stacked_weights, preferred_element_type=j...  7.6 us
    ppermute x1, starting transfers between devices, with_halo(): east = lax.ppermute(west_edge, 'lon', shifted_pairs(lon_count, -1, True))  7.12 us
    concatenate x2, other arithmetic, with_halo(): return jnp.concatenate([west, tall, east], axis=-1)  6.45 us
    mul x4, other arithmetic, advect(): mask_east * (east_speed[:, :, :-1] * (tracer_now[..., :-1] + tracer_now[....  4.22 us
    mul x4, other arithmetic, advect(): mask_north * (north_speed[:, :-1, :] * (tracer_now[..., :-1, :] + tracer_...  4.16 us
  transfers between devices with their start and end apart: 5, of which 1 were waited for; matrix products, arithmetic and copies ran while one was open for 43% of the time, Pallas kernels for 0%

profile of v14, /device:TPU:0, one launch (start us, length us, event | category | flops | bytes accessed | tf_op | source)
XLA Modules:
  0.0 100.2 jit_solution(924874522949406248)
XLA Ops:
  0.0 0.7 fusion.36
  0.7 1.3 %pad_maximum_fusion.3 = f32[129,16,128]{2,1,0:T(8,128)S(1)} fusion(f32[1,16,128]{2,1,0:T(8,128)S(1)} %get-tuple-element.20, f32[16,16,128]{2,1,0:T(8,128)} %param.17, f32[16,16,128]{2,1,0:T(8,128)} %param.16, f32[96,16,128]{2,1,0:T(8,128)} %bitcast.47), kind=kLoop, calls=%fused_computation.43 | loop fusion | flops 792576 | bytes 2113536 | tf_op jit(solution)/shard_map/concatenate | solution.py:124
  2.2 1.4 %collective-permute-start = (f32[129,4,128]{2,1,0:T(4,128)S(1)}, f32[129,4,128]{2,1,0:T(4,128)S(1)}, u32[]{:S(2)}, u32[]{:S(2)}) collective-permute-start(f32[129,4,128]{2,1,0:T(4,128)S(1)} %get-tuple-element.13), channel_id=1, source_target_pairs={{0,32},{32,64},{64,96},{1,33},{33,65},{65,97},{2,34},{34,66},{66,9... | collective-permute-start | bytes 792584 | tf_op jit(solution)/shard_map/ppermute | solution.py:29
  3.7 1.3 %collective-permute-start.1 = (f32[129,4,128]{2,1,0:T(4,128)S(1)}, f32[129,4,128]{2,1,0:T(4,128)S(1)}, u32[]{:S(2)}, u32[]{:S(2)}) collective-permute-start(f32[129,4,128]{2,1,0:T(4,128)S(1)} %get-tuple-element.14), channel_id=1, source_target_pairs={{32,0},{64,32},{96,64},{33,1},{65,33},{97,65},{34,2},{66,34},{98,6... | collective-permute-start | bytes 792584 | tf_op jit(solution)/shard_map/ppermute | solution.py:30
  5.0 1.6 %fusion.32 = (f32[129,16,4]{2,1,0:T(8,128)}, f32[129,16,4]{2,1,0:T(8,128)}) fusion(f32[129,16,128]{2,1,0:T(8,128)S(1)} %pad_maximum_fusion.3), kind=kLoop, calls=%fused_computation.106 | loop fusion | bytes 132096 | tf_op jit(solution)/shard_map/slice | solution.py:32
  8.6 1.0 gather_fusion
  9.6 0.9 broadcast_select_fusion
  10.5 1.4 %slice_bitcast_fusion.1 = (bf16[128,24,128]{2,1,0:T(8,128)(2,1)}, bf16[128,24,128]{2,1,0:T(8,128)(2,1)}) fusion(bf16[128,2,24,128]{3,2,1,0:T(8,128)(2,1)S(1)} %bitcast.50), kind=kLoop, calls=%fused_computation.45 | loop fusion | bytes 3145728 | tf_op jit(solution)/shard_map/squeeze | solution.py:95
  11.9 0.7 select_select_fusion.1
  13.7 2.2 %pad_maximum_fusion.1 = (f32[129,24,4]{2,1,0:T(8,128)S(1)}, f32[129,24,4]{2,1,0:T(8,128)S(1)}) fusion(f32[129,4,4]{2,1,0:T(4,128)S(1)} %get-tuple-element.17, f32[129,16,4]{2,1,0:T(8,128)} %get-tuple-element.11, f32[129,4,4]{2,1,0:T(4,128)S(1)} %get-tuple-element.15, f32[129,4,4]{2,1,0:T(4,128)S(1)} %get-tuple-element.18, ...), kind=kLoop, calls=%fused_computation.40 | loop fusion | flops 49536 | bytes 198144 | tf_op jit(solution)/shard_map/concatenate | solution.py:31
  17.0 0.7 copy.81
  17.7 7.1 %collective-permute-start.3 = (f32[129,96]{0,1:T(8,128)}, f32[129,96]{0,1:T(8,128)S(1)}, u32[]{:S(2)}, u32[]{:S(2)}) collective-permute-start(f32[129,96]{0,1:T(8,128)} %copy.81), channel_id=1, source_target_pairs={{0,31},{1,0},{2,1},{3,2},{4,3},{5,4},{6,5},{7,6},{8,7},{9,8},{10,9... | collective-permute-start | bytes 148616 | tf_op jit(solution)/shard_map/ppermute | solution.py:38
  24.8 7.6 %select_select_fusion = f32[128,56,128]{2,1,0:T(8,128)} fusion(f32[128,56]{1,0:T(8,128)} %select_select_fusion.1, pred[56]{0:T(512)(128)(4,1)S(1)} %iota_compare_fusion.6, pred[128,56]{1,0:T(8,128)(4,1)S(1)} %copy.73, bf16[128,256,128]{2,1,0:T(8,128)(2,1)} %bitcast.56, bf16[128,24,128]{2,1,0:T(8,128)(2,1)} %get-tuple-element.10, ...), kind=kOutput, calls=%fused_computation.14 | convolution fusion | flops 493617152 | bytes 13667496 | tf_op jit(solution)/shard_map/trb,tbc->trc/dot_general | solution.py:101
  32.4 14.8 %all-to-all-start = ((f32[128,56,128]{2,1,0:T(8,128)}), f32[128,56,128]{2,1,0:T(8,128)}, u32[]{:S(2)}, u32[]{:S(2)}) async-start(f32[128,56,128]{2,1,0:T(8,128)} %select_select_fusion), calls=%async_computation | async-start | bytes 7340032 | tf_op jit(solution)/shard_map/all_to_all | solution.py:118
  47.3 1.0 %copy.70 = f32[129,24,4]{2,1,0:T(8,128)S(1)} copy(f32[129,24,4]{0,2,1:T(4,128)S(1)} %reshape.247) | data formatting | bytes 99072 | tf_op jit(solution)/shard_map/reshape | solution.py:40
  48.4 2.2 %copy.71 = f32[129,24,4]{2,1,0:T(8,128)} copy(f32[129,24,4]{0,2,1:T(4,128)S(1)} %reshape.249) | data formatting | bytes 99072 | tf_op jit(solution)/shard_map/reshape | solution.py:41
  50.6 6.1 %pad_maximum_fusion = f32[129,24,136]{2,1,0:T(8,128)S(1)} fusion(f32[129,24,4]{2,1,0:T(8,128)} %copy.71, f32[129,4,128]{2,1,0:T(4,128)S(1)} %copy-done.6, f32[1,16,128]{2,1,0:T(8,128)S(1)} %get-tuple-element.20, f32[16,16,128]{2,1,0:T(8,128)S(1)} %copy-done.7, f32[16,16,128]{2,1,0:T(8,128)S(1)} %copy-done.8, f32[96,16,128]{2,1,0:T(8,128)S(1)} %bitcast.48, ...), kind=kLoop, calls=%fused_computation.15 | loop fusion | flops 2947392 | bytes 3368448 | tf_op jit(solution)/shard_map/concatenate | solution.py:42
  58.4 0.7 subtract_multiply_fusion.7
  59.1 0.7 subtract_multiply_fusion.6
  60.1 2.5 %slice_subtract_fusion.4 = f32[6,16,22,134]{3,2,1,0:T(8,128)S(1)} fusion(f32[6,16,23,136]{3,2,1,0:T(8,128)S(1)} %subtract_multiply_fusion.6, f32[6,16,24,135]{3,2,1,0:T(8,128)S(1)} %subtract_multiply_fusion.7, f32[6,16,24,136]{3,2,1,0:T(8,128)S(1)} %bitcast.45), kind=kLoop, calls=%fused_computation.26 | loop fusion | flops 1132032 | bytes 6792192 | tf_op jit(solution)/shard_map/sub | solution.py:58
  62.7 0.7 subtract_multiply_fusion.5
  63.4 0.7 subtract_multiply_fusion.4
  64.1 2.5 %slice_subtract_fusion.2 = f32[6,16,20,132]{3,2,1,0:T(8,128)S(1)} fusion(f32[6,16,21,134]{3,2,1,0:T(8,128)S(1)} %subtract_multiply_fusion.4, f32[6,16,22,133]{3,2,1,0:T(8,128)S(1)} %subtract_multiply_fusion.5, f32[6,16,22,134]{3,2,1,0:T(8,128)S(1)} %slice_subtract_fusion.4), kind=kLoop, calls=%fused_computation.22 | loop fusion | flops 1013760 | bytes 6082560 | tf_op jit(solution)/shard_map/sub | solution.py:58
  67.3 0.7 subtract_multiply_fusion.2
  68.0 2.7 %slice_subtract_fusion = f32[6,16,18,130]{3,2,1,0:T(8,128)S(1)} fusion(f32[6,16,19,132]{3,2,1,0:T(8,128)S(1)} %subtract_multiply_fusion.2, f32[6,16,20,131]{3,2,1,0:T(8,128)S(1)} %subtract_multiply_fusion.3, f32[6,16,20,132]{3,2,1,0:T(8,128)S(1)} %slice_subtract_fusion.2), kind=kLoop, calls=%fused_computation.18 | loop fusion | flops 898560 | bytes 5391360 | tf_op jit(solution)/shard_map/sub | solution.py:58
  70.7 2.2 %subtract_multiply_fusion.1 = f32[6,16,18,129]{3,2,1,0:T(8,128)} fusion(f32[6,16,18,130]{3,2,1,0:T(8,128)S(1)} %slice_subtract_fusion, f32[16,18,129]{2,1,0:T(8,128)S(1)} %pad_maximum_fusion.4, f32[18,129]{1,0:T(8,128)S(1)} %slice_multiply_fusion.1), kind=kLoop, calls=%fused_computation.31 | loop fusion | flops 1560384 | bytes 2832840 | tf_op jit(solution)/shard_map/mul | solution.py:47
  72.9 2.1 %subtract_multiply_fusion = f32[6,16,17,130]{3,2,1,0:T(8,128)} fusion(f32[6,16,18,130]{3,2,1,0:T(8,128)S(1)} %slice_subtract_fusion, f32[16,17,130]{2,1,0:T(8,128)S(1)} %slice.448, f32[17,130]{1,0:T(8,128)S(1)} %slice_multiply_fusion), kind=kLoop, calls=%fused_computation.30 | loop fusion | flops 1485120 | bytes 2696200 | tf_op jit(solution)/shard_map/mul | solution.py:52
  75.0 17.8 %all-to-all-done = f32[128,56,128]{2,1,0:T(8,128)} async-done(((f32[128,56,128]{2,1,0:T(8,128)}), f32[128,56,128]{2,1,0:T(8,128)}, u32[]{:S(2)}, u32[]{:S(2)}) %all-to-all-start) | async-done | bytes 3670048 | tf_op jit(solution)/shard_map/all_to_all | solution.py:118
  92.8 1.3 %slice_reduce_fusion = f32[128,2]{1,0:T(8,128)S(1)} fusion(f32[128,56,128]{2,1,0:T(8,128)} %all-to-all-done), kind=kLoop, calls=%fused_computation.60 | loop fusion | bytes 2048 | tf_op jit(solution)/shard_map/slice | solution.py:119
  94.2 2.3 %slice.460 = f32[128,48,128]{2,1,0:T(8,128)S(1)} slice(f32[128,56,128]{2,1,0:T(8,128)} %all-to-all-done), slice={[0:128], [0:48], [0:128]} | slice | bytes 6291456 | tf_op jit(solution)/shard_map/slice | solution.py:120
  96.5 0.9 fusion.12
  98.2 2.0 %fusion.18 = f32[6,16,16,128]{3,2,1,0:T(8,128)} fusion(f32[6,16,17,130]{3,2,1,0:T(8,128)S(1)} %copy-done.4, f32[6,16,18,129]{3,2,1,0:T(8,128)S(1)} %copy-done.3, f32[6,16,18,130]{3,2,1,0:T(8,128)S(1)} %slice_subtract_fusion, f32[6,16,16,128]{3,1,0,2:T(8,128)S(1)} %bitcast.51, f32[16,128]{1,0:T(8,128)S(1)} %get-tuple-element.19), kind=kLoop, calls=%fused_computation.47 | loop fusion | flops 1179648 | bytes 5513216 | tf_op jit(solution)/shard_map/add | solution.py:161
  (78 shorter events, 7.7 us)
Async XLA Ops:
  0.0 8.5 %copy-start = (bf16[24,2048]{1,0:T(8,128)(2,1)S(1)}, bf16[24,2048]{1,0:T(8,128)(2,1)}, u32[]{:S(2)}) copy-start(bf16[24,2048]{1,0:T(8,128)(2,1)} %param.10) | copy-start | bytes 294916
  2.2 4.5 %copy-start.11 = (s32[1,256]{1,0:T(1,128)S(1)}, s32[1,256]{1,0:T(1,128)}, u32[]{:S(2)}) copy-start(s32[1,256]{1,0:T(1,128)} %param.12) | copy-start | bytes 3076
  2.2 4.5 %copy-start.10 = (s32[1,128]{1,0:T(1,128)S(1)}, s32[1,128]{1,0:T(1,128)}, u32[]{:S(2)}) copy-start(s32[1,128]{1,0:T(1,128)} %param.14) | copy-start | bytes 1540
  2.2 5.3 %copy-start.12 = (s32[1,256]{1,0:T(1,128)S(1)}, s32[1,256]{1,0:T(1,128)}, u32[]{:S(2)}) copy-start(s32[1,256]{1,0:T(1,128)} %param.13) | copy-start | bytes 3076
  2.2 10.9 %collective-permute-start = (f32[129,4,128]{2,1,0:T(4,128)S(1)}, f32[129,4,128]{2,1,0:T(4,128)S(1)}, u32[]{:S(2)}, u32[]{:S(2)}) collective-permute-start(f32[129,4,128]{2,1,0:T(4,128)S(1)} %get-tuple-element.13), channel_id=1, source_target_pairs={{0,32},{32,64},{64,96},{1,33},{33,65},{65,97},{2,34},{34,66},{66,9... | collective-permute-start | bytes 792584 | tf_op jit(solution)/shard_map/ppermute | solution.py:29
  3.7 9.3 %collective-permute-start.1 = (f32[129,4,128]{2,1,0:T(4,128)S(1)}, f32[129,4,128]{2,1,0:T(4,128)S(1)}, u32[]{:S(2)}, u32[]{:S(2)}) collective-permute-start(f32[129,4,128]{2,1,0:T(4,128)S(1)} %get-tuple-element.14), channel_id=1, source_target_pairs={{32,0},{64,32},{96,64},{33,1},{65,33},{97,65},{34,2},{66,34},{98,6... | collective-permute-start | bytes 792584 | tf_op jit(solution)/shard_map/ppermute | solution.py:30
  12.9 0.7 copy-start.5
  17.7 30.6 %collective-permute-start.3 = (f32[129,96]{0,1:T(8,128)}, f32[129,96]{0,1:T(8,128)S(1)}, u32[]{:S(2)}, u32[]{:S(2)}) collective-permute-start(f32[129,96]{0,1:T(8,128)} %copy.81), channel_id=1, source_target_pairs={{0,31},{1,0},{2,1},{3,2},{4,3},{5,4},{6,5},{7,6},{8,7},{9,8},{10,9... | collective-permute-start | bytes 148616 | tf_op jit(solution)/shard_map/ppermute | solution.py:38
  24.8 22.4 %collective-permute-start.2 = (f32[129,96]{0,1:T(8,128)S(1)}, f32[129,96]{0,1:T(8,128)S(1)}, u32[]{:S(2)}, u32[]{:S(2)}) collective-permute-start(f32[129,96]{0,1:T(8,128)S(1)} %copy.80), channel_id=1, source_target_pairs={{0,1},{1,2},{2,3},{3,4},{4,5},{5,6},{6,7},{7,8},{8,9},{9,10},{10,1... | collective-permute-start | bytes 148616 | tf_op jit(solution)/shard_map/ppermute | solution.py:37
  32.4 60.4 %all-to-all-start = ((f32[128,56,128]{2,1,0:T(8,128)}), f32[128,56,128]{2,1,0:T(8,128)}, u32[]{:S(2)}, u32[]{:S(2)}) async-start(f32[128,56,128]{2,1,0:T(8,128)} %select_select_fusion), calls=%async_computation | async-start | bytes 7340032 | tf_op jit(solution)/shard_map/all_to_all | solution.py:118
  47.2 3.4 %copy-start.2 = (f32[6,16,16,128]{3,2,1,0:T(8,128)S(1)}, f32[6,16,16,128]{3,2,1,0:T(8,128)}, u32[]{:S(2)}) copy-start(f32[6,16,16,128]{3,2,1,0:T(8,128)} %param.15) | copy-start | bytes 2359300
  47.2 3.4 %copy-start.6 = (f32[129,4,128]{2,1,0:T(4,128)S(1)}, f32[129,4,128]{2,1,0:T(4,128)}, u32[]{:S(2)}) copy-start(f32[129,4,128]{2,1,0:T(4,128)} %copy-done.5) | copy-start | bytes 792580
  47.2 3.4 %copy-start.7 = (f32[16,16,128]{2,1,0:T(8,128)S(1)}, f32[16,16,128]{2,1,0:T(8,128)}, u32[]{:S(2)}) copy-start(f32[16,16,128]{2,1,0:T(8,128)} %param.17) | copy-start | bytes 393220
  47.2 3.3 %copy-start.8 = (f32[16,16,128]{2,1,0:T(8,128)S(1)}, f32[16,16,128]{2,1,0:T(8,128)}, u32[]{:S(2)}) copy-start(f32[16,16,128]{2,1,0:T(8,128)} %param.16) | copy-start | bytes 393220
  94.2 3.8 %copy-start.4 = (f32[6,16,17,130]{3,2,1,0:T(8,128)S(1)}, f32[6,16,17,130]{3,2,1,0:T(8,128)}, u32[]{:S(2)}) copy-start(f32[6,16,17,130]{3,2,1,0:T(8,128)} %subtract_multiply_fusion) | copy-start | bytes 2545924
  96.5 1.0 copy-start.9
  96.5 1.8 %copy-start.3 = (f32[6,16,18,129]{3,2,1,0:T(8,128)S(1)}, f32[6,16,18,129]{3,2,1,0:T(8,128)}, u32[]{:S(2)}) copy-start(f32[6,16,18,129]{3,2,1,0:T(8,128)} %subtract_multiply_fusion.1) | copy-start | bytes 2674948
  98.0 2.3 %copy-start.1 = (bf16[24,2048]{1,0:T(8,128)(2,1)S(1)}, bf16[24,2048]{1,0:T(8,128)(2,1)}, u32[]{:S(2)}) copy-start(bf16[24,2048]{1,0:T(8,128)(2,1)} %param.10) | copy-start | bytes 294916
